TPU v7x, 256 devices: a whole 4x4x8 slice. The times are simulated.
256 devices in a mesh: expert: 16 (over y, x_hi, core), dp: 16 (over x_lo, z).
Axes of the slice: x: 4 (x_hi: 2, x_lo: 2; x = x_hi * 2 + x_lo), y: 4, z: 8, core: 2. Of those that a mesh axis runs over, the one named last changes fastest.
Arguments:
- tokens: bfloat16 [32768, 2048], P(('expert', 'dp')), may hold values from -6 to 6
- cotangent: bfloat16 [32768, 2048], P(('expert', 'dp')), may hold values from -6 to 6
- expert_ids: int32 [32768, 8], P(('expert', 'dp')), may hold values from 0 to 127, as said below
- gate_weights: float32 [32768, 8], P(('expert', 'dp')), may hold values from 0.05 to 1
- placement: int32 [16], replicated, may hold values from 0 to 15, as said below
- w_in: bfloat16 [16, 2048, 1536], P('expert'), may hold values from -0.125 to 0.125
- w_out: bfloat16 [16, 768, 2048], P('expert'), may hold values from -0.21875 to 0.21875
Outputs:
- mixed: bfloat16 [32768, 2048], P(('expert', 'dp'))
- x_grad: bfloat16 [32768, 2048], P(('expert', 'dp'))
- gate_grad: float32 [32768, 8], P(('expert', 'dp'))
- w_in_grad: bfloat16 [16, 2048, 1536], P('expert', 'dp')
- w_out_grad: bfloat16 [16, 768, 2048], P('expert', 'dp')
Inputs may be any that keep to these rules, and one draw needn't show every extreme that they name: `expert_ids`: each row names 8 different experts, at most two of them below 16. Among the 128 tokens of one device (an aligned block of rows, one data group every 16 blocks), no expert below 16 is named by more than 16 tokens, and in every data group one such expert is named by exactly 16 tokens of every device of the group. placement[i] is i or (i + 8) % 16, and placement[placement[i]] = i; at least one pair exchanges and at least one pair stays.
All inputs are finite; a program needn't handle non-finite values.
Results may differ from a plain program's by a relative error of at most 0.018.
Values may be sent and summed in bfloat16 or wider, within the bound.
No kernel may reach another device: no remote copies, remote signals or barrier semaphores. Data moves between devices by JAX's collectives and lax.ppermute only.
A program may use at most 128 MiB of HBM per device.

v0:
```python
import jax
import jax.numpy as jnp
from jax import lax
from jax.sharding import PartitionSpec as P


def partner_2(block, axis, apart):
    count = lax.axis_size(axis)
    route = []
    for low in range(count):
        high = low | 1 << apart
        if high != low and high < count:
            route += [(low, high), (high, low)]
    return lax.ppermute(block, axis, route)


def shards(tokens, cotangent, expert_ids, gate_weights, placement, w_in, w_out):
    expert_count = lax.axis_size("expert")
    group_count = lax.axis_size("dp")
    own_index = lax.axis_index("expert")
    tok_rows = tokens.shape[0]
    model_width = tokens.shape[1]
    hidden_units = w_out.shape[1]
    pick_count = expert_ids.shape[1]
    capacity = tok_rows // 8
    slot_count = expert_count * capacity
    half_bit = expert_count.bit_length() - 2
    expert_lane = jnp.arange(expert_count, dtype=jnp.int32)
    partner = jnp.sum(jnp.where(expert_lane == own_index, placement, 0))
    is_moved = partner != own_index
    swapped = partner_2((w_in, w_out), "expert", half_bit)
    weight_in = jnp.where(is_moved, swapped[0], w_in)[0]
    weight_out = jnp.where(is_moved, swapped[1], w_out)[0]
    route_hot = (expert_ids.reshape(-1)[:, None] == expert_lane[None, :]).astype(jnp.int32)
    to_device = (placement[:, None] == expert_lane[None, :]).astype(jnp.int32)
    device_hot = jnp.dot(route_hot, to_device)
    slot_rank = jnp.cumsum(device_hot, axis=0) - device_hot
    slot_place = jnp.sum((slot_rank + expert_lane[None, :] * capacity) * device_hot, axis=1)
    is_live = jnp.sum(device_hot, axis=1) > 0
    slot_place = jnp.where(is_live, slot_place, -1).reshape(tok_rows, pick_count)
    slot_hot = slot_place[:, :, None] == jnp.arange(slot_count, dtype=jnp.int32)[None, None, :]
    select = jnp.sum(slot_hot.astype(jnp.bfloat16), axis=1)
    weigh = jnp.sum(jnp.where(slot_hot, gate_weights[:, :, None], 0.0), axis=1)
    slot_gate = jnp.sum(weigh, axis=0)
    send_x = jnp.einsum("ts,td->sd", select, tokens, preferred_element_type=jnp.float32).astype(
        jnp.bfloat16
    )
    send_dy = jnp.einsum("ts,td->sd", select, cotangent, preferred_element_type=jnp.float32)
    send_c = (send_dy * slot_gate[:, None]).astype(jnp.bfloat16)
    send_x = send_x.reshape(expert_count, capacity, model_width)
    send_c = send_c.reshape(expert_count, capacity, model_width)
    arrived_x = lax.all_to_all(send_x, "expert", split_axis=0, concat_axis=0, tiled=True)
    rows_x = arrived_x.reshape(slot_count, model_width)
    pre = jnp.dot(rows_x, weight_in, preferred_element_type=jnp.float32)
    gate_pre = pre[:, :hidden_units]
    up_pre = pre[:, hidden_units:]
    sigmoid_gate = jax.nn.sigmoid(gate_pre)
    activated = gate_pre * sigmoid_gate
    hidden = (activated * up_pre).astype(jnp.bfloat16)
    expert_out = jnp.dot(hidden, weight_out, preferred_element_type=jnp.float32).astype(
        jnp.bfloat16
    )
    returned = lax.all_to_all(
        expert_out.reshape(expert_count, capacity, model_width),
        "expert",
        split_axis=0,
        concat_axis=0,
        tiled=True,
    )
    returned = returned.reshape(slot_count, model_width)
    mixed = jnp.dot(
        weigh,
        returned.astype(jnp.float32),
        precision=lax.Precision.HIGHEST,
        preferred_element_type=jnp.float32,
    ).astype(jnp.bfloat16)
    scores = jnp.einsum("td,sd->ts", cotangent, returned, preferred_element_type=jnp.float32)
    gate_grad = jnp.sum(jnp.where(slot_hot, scores[:, None, :], 0.0), axis=2)
    arrived_c = lax.all_to_all(send_c, "expert", split_axis=0, concat_axis=0, tiled=True)
    rows_c = arrived_c.reshape(slot_count, model_width)
    hidden_grad = jnp.einsum("sd,fd->sf", rows_c, weight_out, preferred_element_type=jnp.float32)
    slope = sigmoid_gate * (1.0 + gate_pre * (1.0 - sigmoid_gate))
    gate_up_grad = jnp.concatenate(
        [hidden_grad * up_pre * slope, hidden_grad * activated], axis=1
    ).astype(jnp.bfloat16)
    pick_grad = jnp.einsum(
        "sf,df->sd", gate_up_grad, weight_in, preferred_element_type=jnp.float32
    ).astype(jnp.bfloat16)
    back = lax.all_to_all(
        pick_grad.reshape(expert_count, capacity, model_width),
        "expert",
        split_axis=0,
        concat_axis=0,
        tiled=True,
    )
    back = back.reshape(slot_count, model_width)
    x_grad = jnp.einsum("ts,sd->td", select, back, preferred_element_type=jnp.float32).astype(
        jnp.bfloat16
    )
    grad_in = (
        lax.psum_scatter(
            jnp.einsum(
                "sd,sf->df", rows_x, gate_up_grad, preferred_element_type=jnp.float32
            ).astype(jnp.bfloat16),
            "dp",
            scatter_dimension=0,
            tiled=True,
        ).astype(jnp.float32)
        / group_count
    ).astype(jnp.bfloat16)
    grad_out = (
        lax.psum_scatter(
            jnp.einsum("sf,sd->fd", hidden, rows_c, preferred_element_type=jnp.float32).astype(
                jnp.bfloat16
            ),
            "dp",
            scatter_dimension=0,
            tiled=True,
        ).astype(jnp.float32)
        / group_count
    ).astype(jnp.bfloat16)
    return (mixed, x_grad, gate_grad, grad_in[None], grad_out[None])


def solution(mesh):
    placed = (
        P(("expert", "dp"), None),
        P(("expert", "dp"), None),
        P(("expert", "dp"), None),
        P(("expert", "dp"), None),
        P(),
        P("expert", None, None),
        P("expert", None, None),
    )
    return jax.shard_map(
        shards,
        mesh=mesh,
        in_specs=placed,
        out_specs=(
            P(("expert", "dp"), None),
            P(("expert", "dp"), None),
            P(("expert", "dp"), None),
            P("expert", "dp", None),
            P("expert", "dp", None),
        ),
        check_vma=False,
    )
```

profile of v0, /device:TPU:24, one launch (start us, length us, event | category | flops | bytes accessed | tf_op | source)
XLA Modules:
  0.0 455.2 jit_solution(13869459407344235362)
XLA Ops:
  7.2 1.3 collective-permute-start
  8.5 2.3 collective-permute-start.1
  10.8 0.8 copy.21
  11.7 1.0 fusion.18
  12.7 4.5 reduce-window.6
  18.3 2.5 convolution_convert_fusion.2
  20.7 7.2 %all-to-all-start = ((bf16[16,16,2048]{2,1,0:T(8,128)(2,1)}), bf16[16,16,2048]{2,1,0:T(8,128)(2,1)S(1)}, u32[]{:S(2)}, u32[]{:S(2)}) async-start(bf16[16,16,2048]{2,1,0:T(8,128)(2,1)} %bitcast.3), calls=%async_computation | async-start | bytes 2097152 | tf_op jit(solution)/shard_map/all_to_all | solution.py:52
  27.9 0.6 fusion.27
  29.2 195.7 %all-to-all-done = bf16[16,16,2048]{2,1,0:T(8,128)(2,1)S(1)} async-done(((bf16[16,16,2048]{2,1,0:T(8,128)(2,1)}), bf16[16,16,2048]{2,1,0:T(8,128)(2,1)S(1)}, u32[]{:S(2)}, u32[]{:S(2)}) %all-to-all-start) | async-done | bytes 1048608 | tf_op jit(solution)/shard_map/all_to_all | solution.py:52
  224.9 4.7 %fusion.2 = f32[256,1536]{1,0:T(8,128)S(1)} fusion(bf16[256,2048]{1,0:T(8,128)(2,1)S(1)} %bitcast.73, bf16[1,2048,1536]{2,1,0:T(8,128)(2,1)} %collective-permute-done, bf16[1,2048,1536]{2,1,0:T(8,128)(2,1)} %param.12, pred[]{:T(512)S(6)} %ne.3), kind=kOutput, calls=%fused_computation.3 | convolution fusion | flops 1613758464 | bytes 15204353 | tf_op jit(solution)/shard_map/dot_general | solution.py:54
  229.9 4.2 fusion.12
  234.1 7.0 %all-to-all-start.1 = ((bf16[16,16,2048]{2,1,0:T(8,128)(2,1)}), bf16[16,16,2048]{2,1,0:T(8,128)(2,1)S(1)}, u32[]{:S(2)}, u32[]{:S(2)}) async-start(bf16[16,16,2048]{2,1,0:T(8,128)(2,1)} %bitcast.80), calls=%async_computation.1 | async-start | bytes 2097152 | tf_op jit(solution)/shard_map/all_to_all | solution.py:63
  241.3 15.5 %all-to-all-done.1 = bf16[16,16,2048]{2,1,0:T(8,128)(2,1)S(1)} async-done(((bf16[16,16,2048]{2,1,0:T(8,128)(2,1)}), bf16[16,16,2048]{2,1,0:T(8,128)(2,1)S(1)}, u32[]{:S(2)}, u32[]{:S(2)}) %all-to-all-start.1) | async-done | bytes 1048608 | tf_op jit(solution)/shard_map/all_to_all | solution.py:63
  257.3 0.7 select_reduce_fusion
  258.1 0.5 fusion.8
  258.6 20.6 %all_to_all.20 = bf16[16,16,2048]{2,1,0:T(8,128)(2,1)S(1)} all-to-all(bf16[16,16,2048]{2,1,0:T(8,128)(2,1)S(1)} %bitcast.76), channel_id=1, replica_groups=mesh['expert'=16,'dp'=16] {'expert'}, dimensions={0} | all-to-all | bytes 2097152 | tf_op jit(solution)/shard_map/all_to_all | solution.py:79
  279.2 1.0 copy-done.1
  280.1 2.7 convolution_convert_fusion.1
  283.1 3.9 multiply_convert_fusion.2
  287.0 0.7 copy-done.3
  287.8 4.5 convolution_convert_fusion
  292.3 1.0 copy-done.4
  293.3 5.8 %fusion.9 = bf16[256,2048]{1,0:T(8,128)(2,1)} fusion(bf16[1,2048,1536]{2,1,0:T(8,128)(2,1)} %collective-permute-done, bf16[1,2048,1536]{2,1,0:T(8,128)(2,1)} %param.12, pred[]{:T(512)S(6)} %ne.3, bf16[256,768]{1,0:T(8,128)(2,1)S(1)} %copy-done.4, bf16[256,768]{1,0:T(8,128)(2,1)S(1)} %get-tuple-element.15), kind=kOutput, calls=%fused_computation.15 | convolution fusion | flops 1615855616 | bytes 14417921 | tf_op jit(solution)/shard_map/sf,df->sd/dot_general | solution.py:86
  299.1 5.8 %all-to-all-start.3 = ((bf16[16,16,2048]{2,1,0:T(8,128)(2,1)}), bf16[16,16,2048]{2,1,0:T(8,128)(2,1)S(1)}, u32[]{:S(2)}, u32[]{:S(2)}) async-start(bf16[16,16,2048]{2,1,0:T(8,128)(2,1)} %bitcast.79), calls=%async_computation.3 | async-start | bytes 2097152 | tf_op jit(solution)/shard_map/all_to_all | solution.py:89
  304.9 0.7 copy.26
  305.5 1.4 convolution_convert_fusion.4
  306.9 27.6 %all-to-all-done.3 = bf16[16,16,2048]{2,1,0:T(8,128)(2,1)S(1)} async-done(((bf16[16,16,2048]{2,1,0:T(8,128)(2,1)}), bf16[16,16,2048]{2,1,0:T(8,128)(2,1)S(1)}, u32[]{:S(2)}, u32[]{:S(2)}) %all-to-all-start.3) | async-done | bytes 1048608 | tf_op jit(solution)/shard_map/all_to_all | solution.py:89
  334.5 1.1 convolution_convert_fusion.3
  335.6 24.9 %reduce-scatter.5.cloned.1.call-done = bf16[48,2048]{1,0:T(8,128)(2,1)} async-done(((bf16[768,2048]{1,0:T(8,128)(2,1)}), bf16[48,2048]{1,0:T(8,128)(2,1)}) %reduce-scatter.5.cloned.1.call-update) | async-done | bytes 196624 | tf_op jit(solution)/shard_map/reduce_scatter | solution.py:112
  360.5 1.6 fusion.21
  362.2 84.3 %reduce-scatter.3.cloned.1.call-done = bf16[128,1536]{1,0:T(8,128)(2,1)} async-done(((bf16[2048,1536]{1,0:T(8,128)(2,1)}), bf16[128,1536]{1,0:T(8,128)(2,1)}) %reduce-scatter.3.cloned.1.call-update) | async-done | bytes 393232 | tf_op jit(solution)/shard_map/reduce_scatter | solution.py:101
  446.5 1.8 fusion.19
  (36 shorter events, 2.3 us)
Async XLA Ops:
  7.2 249.6 %copy-start = (bf16[128,2048]{1,0:T(8,128)(2,1)S(1)}, bf16[128,2048]{1,0:T(8,128)(2,1)}, u32[]{:S(2)}) copy-start(bf16[128,2048]{1,0:T(8,128)(2,1)} %param.8) | copy-start | bytes 1572868
  7.2 20.7 %copy-start.7 = (s32[16]{0:T(128)S(1)}, s32[16]{0:T(128)}, u32[]{:S(2)}) copy-start(s32[16]{0:T(128)} %param.11) | copy-start | bytes 196
  7.2 217.7 %collective-permute-start = (bf16[1,2048,1536]{2,1,0:T(8,128)(2,1)}, bf16[1,2048,1536]{2,1,0:T(8,128)(2,1)}, u32[]{:S(2)}, u32[]{:S(2)}) collective-permute-start(bf16[1,2048,1536]{2,1,0:T(8,128)(2,1)} %param.12), channel_id=1, source_target_pairs={{0,128},{128,0},{16,144},{144,16},{32,160},{160,32},{48,176},{176,... | collective-permute-start | bytes 18874376 | tf_op jit(solution)/shard_map/ppermute | solution.py:14
  8.5 221.4 %collective-permute-start.1 = (bf16[1,768,2048]{2,1,0:T(8,128)(2,1)}, bf16[1,768,2048]{2,1,0:T(8,128)(2,1)}, u32[]{:S(2)}, u32[]{:S(2)}) collective-permute-start(bf16[1,768,2048]{2,1,0:T(8,128)(2,1)} %param.13), channel_id=1, source_target_pairs={{0,128},{128,0},{16,144},{144,16},{32,160},{160,32},{48,176},{176,... | collective-permute-start | bytes 9437192 | tf_op jit(solution)/shard_map/ppermute | solution.py:14
  20.7 204.1 %all-to-all-start = ((bf16[16,16,2048]{2,1,0:T(8,128)(2,1)}), bf16[16,16,2048]{2,1,0:T(8,128)(2,1)S(1)}, u32[]{:S(2)}, u32[]{:S(2)}) async-start(bf16[16,16,2048]{2,1,0:T(8,128)(2,1)} %bitcast.3), calls=%async_computation | async-start | bytes 2097152 | tf_op jit(solution)/shard_map/all_to_all | solution.py:52
  224.9 5.0 %copy-start.6 = (bf16[1,768,2048]{2,1,0:T(8,128)(2,1)S(1)}, bf16[1,768,2048]{2,1,0:T(8,128)(2,1)}, u32[]{:S(2)}) copy-start(bf16[1,768,2048]{2,1,0:T(8,128)(2,1)} %param.13) | copy-start | bytes 9437188
  229.6 4.5 copy-start.2
  229.9 11.3 %copy-start.5 = (f32[128,8]{0,1:T(8,128)S(1)}, f32[128,8]{0,1:T(8,128)}, u32[]{:S(2)}) copy-start(f32[128,8]{0,1:T(8,128)} %param.10) | copy-start | bytes 12292
  234.1 22.7 %all-to-all-start.1 = ((bf16[16,16,2048]{2,1,0:T(8,128)(2,1)}), bf16[16,16,2048]{2,1,0:T(8,128)(2,1)S(1)}, u32[]{:S(2)}, u32[]{:S(2)}) async-start(bf16[16,16,2048]{2,1,0:T(8,128)(2,1)} %bitcast.80), calls=%async_computation.1 | async-start | bytes 2097152 | tf_op jit(solution)/shard_map/all_to_all | solution.py:63
  241.1 119.4 %reduce-scatter.5.cloned.1.call-start = ((), (), s32[]{:S(2)}) async-start(), calls=%async_computation.7 | async-start | bytes 3342336 | tf_op jit(solution)/shard_map/reduce_scatter | solution.py:112
  279.2 1.0 copy-start.1
  282.9 163.6 %reduce-scatter.3.cloned.1.call-start = ((), (), s32[]{:S(2)}) async-start(), calls=%async_computation.6 | async-start | bytes 6684672 | tf_op jit(solution)/shard_map/reduce_scatter | solution.py:101
  287.0 0.7 copy-start.3
  292.3 1.0 copy-start.4
  299.1 35.5 %all-to-all-start.3 = ((bf16[16,16,2048]{2,1,0:T(8,128)(2,1)}), bf16[16,16,2048]{2,1,0:T(8,128)(2,1)S(1)}, u32[]{:S(2)}, u32[]{:S(2)}) async-start(bf16[16,16,2048]{2,1,0:T(8,128)(2,1)} %bitcast.79), calls=%async_computation.3 | async-start | bytes 2097152 | tf_op jit(solution)/shard_map/all_to_all | solution.py:89
Sparse Core Ops, SparseCore 0:
  283.0 77.4 reduce-scatter.4
  363.1 83.3 reduce-scatter.2
where the time goes:
time: 456 us; the launch traced here: 455 us
  waiting for transfers between devices  348 us (76%)
  matrix products  32.7 us (7%)
  starting transfers between devices  23.8 us (5%)
  blocking collectives  20.6 us (5%)
  between operations  14.9 us (3%)
  other arithmetic  10.2 us (2%)
  local copies, waits for them, and re-layouts  4.83 us (1%)
    all_to_all x1, waiting for transfers between devices, shards(): lax.all_to_all(send_x, 'expert', split_axis=0, concat_axis=0, tiled=True)  196 us
    reduce_scatter x1, waiting for transfers between devices, shards(): lax.psum_scatter(jnp.einsum('sd,sf->df', rows_x, gate_up_grad, preferred_...  84.3 us
    all_to_all x1, waiting for transfers between devices, shards(): lax.all_to_all(pick_grad.reshape(expert_count, capacity, model_width), 'e...  27.6 us
    reduce_scatter x1, waiting for transfers between devices, shards(): lax.psum_scatter(jnp.einsum('sf,sd->fd', hidden, rows_c, preferred_elemen...  24.9 us
    all_to_all x1, blocking collectives, shards(): lax.all_to_all(send_c, 'expert', split_axis=0, concat_axis=0, tiled=True)  20.6 us
    all_to_all x1, waiting for transfers between devices, shards(): lax.all_to_all(expert_out.reshape(expert_count, capacity, model_width), '...  15.5 us
  transfers between devices with their start and end apart: 7, of which 5 were waited for; matrix products, arithmetic and copies ran while one was open for 8% of the time, Pallas kernels for 0%

commit v1 on v0

--- a/solution.py
+++ b/solution.py
@@ -28,12 +28,9 @@
     expert_lane = jnp.arange(expert_count, dtype=jnp.int32)
     partner = jnp.sum(jnp.where(expert_lane == own_index, placement, 0))
     is_moved = partner != own_index
-    swapped = partner_2((w_in, w_out), "expert", half_bit)
-    weight_in = jnp.where(is_moved, swapped[0], w_in)[0]
-    weight_out = jnp.where(is_moved, swapped[1], w_out)[0]
-    route_hot = (expert_ids.reshape(-1)[:, None] == expert_lane[None, :]).astype(jnp.int32)
-    to_device = (placement[:, None] == expert_lane[None, :]).astype(jnp.int32)
-    device_hot = jnp.dot(route_hot, to_device)
+    weight_in = w_in[0]
+    weight_out = w_out[0]
+    device_hot = (expert_ids.reshape(-1)[:, None] == expert_lane[None, :]).astype(jnp.int32)
     slot_rank = jnp.cumsum(device_hot, axis=0) - device_hot
     slot_place = jnp.sum((slot_rank + expert_lane[None, :] * capacity) * device_hot, axis=1)
     is_live = jnp.sum(device_hot, axis=1) > 0
@@ -119,6 +116,9 @@
         ).astype(jnp.float32)
         / group_count
     ).astype(jnp.bfloat16)
+    swapped = partner_2((grad_in, grad_out), "expert", half_bit)
+    grad_in = jnp.where(is_moved, swapped[0], grad_in)
+    grad_out = jnp.where(is_moved, swapped[1], grad_out)
     return (mixed, x_grad, gate_grad, grad_in[None], grad_out[None])
 
 

time: 456 us -> 283 us (0.62)
  waiting for transfers between devices: 348 us -> 154 us
  blocking collectives: 20.6 us -> 43.3 us
  starting transfers between devices: 23.8 us -> 16.7 us
    all_to_all x1 -> x0, waiting for transfers between devices: 196 us -> none  [shards(): lax.all_to_all(send_x, 'expert', split_axis=0, concat_axis=0, tiled=True)]
    all_to_all x0 -> x1, blocking collectives: none -> 22.7 us  [shards(): lax.all_to_all(send_x, 'expert', split_axis=0, concat_axis=0, tiled=True)]
    all_to_all x1 -> x0, starting transfers between devices: 7.18 us -> none  [shards(): lax.all_to_all(send_x, 'expert', split_axis=0, concat_axis=0, tiled=True)]
    ppermute x2, waiting for transfers between devices: 0.01 us -> 6.3 us  [partner_2(): return lax.ppermute(block, axis, route)]
  transfers between devices with their start and end apart: 7 -> 6, of which waited for: 5 -> 5; matrix products, arithmetic and copies ran while one was open for 8% -> 8% of each run, Pallas kernels for 0% -> 0%
where the time goes in v1:
time: 283 us; the launch traced here: 282 us
  waiting for transfers between devices  154 us (54%)
  blocking collectives  43.3 us (15%)
  matrix products  33.4 us (12%)
  starting transfers between devices  16.7 us (6%)
  between operations  14.9 us (5%)
  other arithmetic  13.9 us (5%)
  local copies, waits for them, and re-layouts  6.45 us (2%)
    reduce_scatter x1, waiting for transfers between devices, shards(): lax.psum_scatter(jnp.einsum('sd,sf->df', rows_x, gate_up_grad, preferred_...  82.8 us
    all_to_all x1, waiting for transfers between devices, shards(): lax.all_to_all(pick_grad.reshape(expert_count, capacity, model_width), 'e...  25.2 us
    reduce_scatter x1, waiting for transfers between devices, shards(): lax.psum_scatter(jnp.einsum('sf,sd->fd', hidden, rows_c, preferred_elemen...  24.2 us
    all_to_all x1, blocking collectives, shards(): lax.all_to_all(send_x, 'expert', split_axis=0, concat_axis=0, tiled=True)  22.7 us
    all_to_all x1, blocking collectives, shards(): lax.all_to_all(send_c, 'expert', split_axis=0, concat_axis=0, tiled=True)  20.6 us
    all_to_all x1, waiting for transfers between devices, shards(): lax.all_to_all(expert_out.reshape(expert_count, capacity, model_width), '...  15 us
    all_to_all x1, starting transfers between devices, shards(): lax.all_to_all(pick_grad.reshape(expert_count, capacity, model_width), 'e...  6.84 us
    all_to_all x1, starting transfers between devices, shards(): lax.all_to_all(expert_out.reshape(expert_count, capacity, model_width), '...  6.52 us
  transfers between devices with their start and end apart: 6, of which 5 were waited for; matrix products, arithmetic and copies ran while one was open for 8% of the time, Pallas kernels for 0%

profile of v1, /device:TPU:24, one launch (start us, length us, event | category | flops | bytes accessed | tf_op | source)
XLA Modules:
  0.0 282.3 jit_solution(3811286307968746538)
XLA Ops:
  7.2 0.9 copy.22
  8.3 4.5 %reduce-window.6 = s32[16,8,128]{2,1,0:T(8,128)S(1)} reduce-window(s32[16,8,128]{2,1,0:T(8,128)S(1)} %fusion.21, s32[]{:T(128)} %constant.9.clone.1), window={size=1x1x128 pad=0_0x0_0x127_0}, to_apply=%region_1.2 | reduce-window | flops 2080768 | bytes 131076 | tf_op jit(solution)/shard_map/reduce-window
  13.9 1.5 convolution_convert_fusion.2
  15.4 22.7 %all_to_all.20 = bf16[16,16,2048]{2,1,0:T(8,128)(2,1)S(1)} all-to-all(bf16[16,16,2048]{2,1,0:T(8,128)(2,1)S(1)} %bitcast.59), channel_id=1, replica_groups=mesh['expert'=16,'dp'=16] {'expert'}, dimensions={0} | all-to-all | bytes 2097152 | tf_op jit(solution)/shard_map/all_to_all | solution.py:49
  38.1 4.9 %fusion.2 = f32[256,1536]{1,0:T(8,128)S(1)} fusion(bf16[256,2048]{1,0:T(8,128)(2,1)S(1)} %bitcast.56, bf16[1,2048,1536]{2,1,0:T(8,128)(2,1)} %param.12), kind=kOutput, calls=%fused_computation.3 | convolution fusion | flops 1610612736 | bytes 8912896 | tf_op jit(solution)/shard_map/dot_general | solution.py:51
  43.3 2.0 fusion.12
  45.3 6.5 %all-to-all-start.1 = ((bf16[16,16,2048]{2,1,0:T(8,128)(2,1)}), bf16[16,16,2048]{2,1,0:T(8,128)(2,1)}, u32[]{:S(2)}, u32[]{:S(2)}) async-start(bf16[16,16,2048]{2,1,0:T(8,128)(2,1)} %bitcast.63), calls=%async_computation.1 | async-start | bytes 2097152 | tf_op jit(solution)/shard_map/all_to_all | solution.py:60
  51.9 0.7 copy.26
  52.6 15.0 %all-to-all-done.1 = bf16[16,16,2048]{2,1,0:T(8,128)(2,1)} async-done(((bf16[16,16,2048]{2,1,0:T(8,128)(2,1)}), bf16[16,16,2048]{2,1,0:T(8,128)(2,1)}, u32[]{:S(2)}, u32[]{:S(2)}) %all-to-all-start.1) | async-done | bytes 1048608 | tf_op jit(solution)/shard_map/all_to_all | solution.py:60
  67.6 2.4 convolution_bitcast_fusion
  70.0 1.7 copy.27
  71.7 2.4 select_reduce_fusion
  74.1 1.5 fusion.8
  75.6 20.6 %all_to_all.21 = bf16[16,16,2048]{2,1,0:T(8,128)(2,1)S(1)} all-to-all(bf16[16,16,2048]{2,1,0:T(8,128)(2,1)S(1)} %bitcast.58), channel_id=1, replica_groups=mesh['expert'=16,'dp'=16] {'expert'}, dimensions={0} | all-to-all | bytes 2097152 | tf_op jit(solution)/shard_map/all_to_all | solution.py:76
  96.3 1.0 copy-done.3
  97.3 2.7 convolution_convert_fusion.1
  100.1 3.0 %multiply_convert_fusion.2 = (bf16[256,768]{1,0:T(8,128)(2,1)S(1)}, bf16[256,768]{1,0:T(8,128)(2,1)S(1)}) fusion(f32[256,1536]{1,0:T(8,128)} %copy-done.4, bf16[256,2048]{1,0:T(8,128)(2,1)} %bitcast.61, bf16[1,768,2048]{2,1,0:T(8,128)(2,1)S(1)} %copy-done), kind=kOutput, calls=%fused_computation.26 | convolution fusion | flops 807862272 | bytes 6553600 | tf_op jit(solution)/shard_map/sd,fd->sf/dot_general | solution.py:78
  103.9 4.5 %convolution_convert_fusion = bf16[2048,1536]{1,0:T(8,128)(2,1)} fusion(bf16[256,2048]{1,0:T(8,128)(2,1)S(1)} %bitcast.57, bf16[256,768]{1,0:T(8,128)(2,1)S(1)} %get-tuple-element.16, bf16[256,768]{1,0:T(8,128)(2,1)S(1)} %get-tuple-element.15), kind=kOutput, calls=%fused_computation | convolution fusion | flops 1615331328 | bytes 8126464 | tf_op jit(solution)/shard_map/sd,sf->df/dot_general | solution.py:99
  108.5 5.9 %fusion.9 = bf16[256,2048]{1,0:T(8,128)(2,1)} fusion(bf16[1,2048,1536]{2,1,0:T(8,128)(2,1)} %param.12, bf16[256,768]{1,0:T(8,128)(2,1)} %copy-done.10, bf16[256,768]{1,0:T(8,128)(2,1)} %copy-done.9), kind=kOutput, calls=%fused_computation.13 | convolution fusion | flops 1612709888 | bytes 8126464 | tf_op jit(solution)/shard_map/sf,df->sd/dot_general | solution.py:83
  114.4 6.8 %all-to-all-start.3 = ((bf16[16,16,2048]{2,1,0:T(8,128)(2,1)}), bf16[16,16,2048]{2,1,0:T(8,128)(2,1)}, u32[]{:S(2)}, u32[]{:S(2)}) async-start(bf16[16,16,2048]{2,1,0:T(8,128)(2,1)} %bitcast.62), calls=%async_computation.3 | async-start | bytes 2097152 | tf_op jit(solution)/shard_map/all_to_all | solution.py:86
  123.2 2.6 convolution_convert_fusion.4
  125.8 25.2 %all-to-all-done.3 = bf16[16,16,2048]{2,1,0:T(8,128)(2,1)} async-done(((bf16[16,16,2048]{2,1,0:T(8,128)(2,1)}), bf16[16,16,2048]{2,1,0:T(8,128)(2,1)}, u32[]{:S(2)}, u32[]{:S(2)}) %all-to-all-start.3) | async-done | bytes 1048608 | tf_op jit(solution)/shard_map/all_to_all | solution.py:86
  151.0 2.3 convolution_convert_fusion.3
  153.3 24.2 %reduce-scatter.5.cloned.1.call-done = bf16[48,2048]{1,0:T(8,128)(2,1)} async-done(((bf16[768,2048]{1,0:T(8,128)(2,1)}), bf16[48,2048]{1,0:T(8,128)(2,1)}) %reduce-scatter.5.cloned.1.call-update) | async-done | bytes 196624 | tf_op jit(solution)/shard_map/reduce_scatter | solution.py:109
  177.5 1.0 multiply_convert_fusion.4
  178.5 1.9 collective-permute-start.1
  180.3 82.8 %reduce-scatter.3.cloned.1.call-done = bf16[128,1536]{1,0:T(8,128)(2,1)} async-done(((bf16[2048,1536]{1,0:T(8,128)(2,1)}), bf16[128,1536]{1,0:T(8,128)(2,1)}) %reduce-scatter.3.cloned.1.call-update) | async-done | bytes 393232 | tf_op jit(solution)/shard_map/reduce_scatter | solution.py:98
  263.1 1.1 multiply_convert_fusion
  264.2 1.4 collective-permute-start
  265.6 1.7 select_bitcast_fusion.1
  267.3 6.3 %collective-permute-done = bf16[128,1536]{1,0:T(8,128)(2,1)S(1)} collective-permute-done((bf16[128,1536]{1,0:T(8,128)(2,1)S(1)}, bf16[128,1536]{1,0:T(8,128)(2,1)S(1)}, u32[]{:S(2)}, u32[]{:S(2)}) %collective-permute-start) | collective-permute-done | bytes 393248 | tf_op jit(solution)/shard_map/ppermute | solution.py:14
  273.6 1.9 select_bitcast_fusion
  (49 shorter events, 3.7 us)
Async XLA Ops:
  7.2 36.1 %copy-start = (bf16[1,768,2048]{2,1,0:T(8,128)(2,1)S(1)}, bf16[1,768,2048]{2,1,0:T(8,128)(2,1)}, u32[]{:S(2)}) copy-start(bf16[1,768,2048]{2,1,0:T(8,128)(2,1)} %param.13) | copy-start | bytes 9437188
  13.5 24.6 %copy-start.7 = (s32[128,8]{1,0:T(8,128)}, s32[128,8]{1,0:T(8,128)S(1)}, u32[]{:S(2)}) copy-start(s32[128,8]{1,0:T(8,128)S(1)} %select_n.40) | copy-start | bytes 12292
  13.9 24.2 %copy-start.5 = (bf16[128,256]{1,0:T(8,128)(2,1)}, bf16[128,256]{1,0:T(8,128)(2,1)S(1)}, u32[]{:S(2)}) copy-start(bf16[128,256]{1,0:T(8,128)(2,1)S(1)} %fusion.17) | copy-start | bytes 196612
  38.1 5.0 %copy-start.1 = (bf16[16,16,2048]{2,1,0:T(8,128)(2,1)}, bf16[16,16,2048]{2,1,0:T(8,128)(2,1)S(1)}, u32[]{:S(2)}) copy-start(bf16[16,16,2048]{2,1,0:T(8,128)(2,1)S(1)} %all_to_all.20) | copy-start | bytes 3145732
  43.0 2.3 copy-start.4
  43.3 8.6 %copy-start.12 = (f32[128,8]{0,1:T(8,128)S(1)}, f32[128,8]{0,1:T(8,128)}, u32[]{:S(2)}) copy-start(f32[128,8]{0,1:T(8,128)} %param.10) | copy-start | bytes 12292
  45.3 22.3 %all-to-all-start.1 = ((bf16[16,16,2048]{2,1,0:T(8,128)(2,1)}), bf16[16,16,2048]{2,1,0:T(8,128)(2,1)}, u32[]{:S(2)}, u32[]{:S(2)}) async-start(bf16[16,16,2048]{2,1,0:T(8,128)(2,1)} %bitcast.63), calls=%async_computation.1 | async-start | bytes 2097152 | tf_op jit(solution)/shard_map/all_to_all | solution.py:60
  51.8 125.7 %reduce-scatter.5.cloned.1.call-start = ((), (), s32[]{:S(2)}) async-start(), calls=%async_computation.7 | async-start | bytes 3342336 | tf_op jit(solution)/shard_map/reduce_scatter | solution.py:109
  96.3 1.0 copy-start.3
  100.0 163.1 %reduce-scatter.3.cloned.1.call-start = ((), (), s32[]{:S(2)}) async-start(), calls=%async_computation.6 | async-start | bytes 6684672 | tf_op jit(solution)/shard_map/reduce_scatter | solution.py:98
  100.1 3.9 %copy-start.2 = (bf16[16,16,2048]{2,1,0:T(8,128)(2,1)S(1)}, bf16[16,16,2048]{2,1,0:T(8,128)(2,1)}, u32[]{:S(2)}) copy-start(bf16[16,16,2048]{2,1,0:T(8,128)(2,1)} %copy-done.1) | copy-start | bytes 3145732
  103.1 0.7 copy-start.9
  103.1 0.9 copy-start.10
  108.5 12.8 %copy-start.13 = (s32[16]{0:T(128)S(1)}, s32[16]{0:T(128)}, u32[]{:S(2)}) copy-start(s32[16]{0:T(128)} %param.11) | copy-start | bytes 196
  108.5 14.0 %copy-start.11 = (f32[128,8]{1,0:T(8,128)S(1)}, f32[128,8]{1,0:T(8,128)}, u32[]{:S(2)}) copy-start(f32[128,8]{1,0:T(8,128)} %get-tuple-element.12) | copy-start | bytes 12292
  108.5 14.7 %copy-start.8 = (f32[128,256]{1,0:T(8,128)S(1)}, f32[128,256]{1,0:T(8,128)}, u32[]{:S(2)}) copy-start(f32[128,256]{1,0:T(8,128)} %get-tuple-element.11) | copy-start | bytes 393220
  114.4 36.6 %copy-start.6 = (bf16[128,256]{1,0:T(8,128)(2,1)S(1)}, bf16[128,256]{1,0:T(8,128)(2,1)}, u32[]{:S(2)}) copy-start(bf16[128,256]{1,0:T(8,128)(2,1)} %copy-done.5) | copy-start | bytes 196612
  114.4 36.6 %all-to-all-start.3 = ((bf16[16,16,2048]{2,1,0:T(8,128)(2,1)}), bf16[16,16,2048]{2,1,0:T(8,128)(2,1)}, u32[]{:S(2)}, u32[]{:S(2)}) async-start(bf16[16,16,2048]{2,1,0:T(8,128)(2,1)} %bitcast.62), calls=%async_computation.3 | async-start | bytes 2097152 | tf_op jit(solution)/shard_map/all_to_all | solution.py:86
  178.5 87.1 %collective-permute-start.1 = (bf16[48,2048]{1,0:T(8,128)(2,1)S(1)}, bf16[48,2048]{1,0:T(8,128)(2,1)S(1)}, u32[]{:S(2)}, u32[]{:S(2)}) collective-permute-start(bf16[48,2048]{1,0:T(8,128)(2,1)S(1)} %multiply_convert_fusion.4), channel_id=1, source_target_pairs={{0,128},{128,0},{16,144},{144,16},{32,160},{160,32},{48,176},{176,... | collective-permute-start | bytes 589832 | tf_op jit(solution)/shard_map/ppermute | solution.py:14
  264.2 9.4 %collective-permute-start = (bf16[128,1536]{1,0:T(8,128)(2,1)S(1)}, bf16[128,1536]{1,0:T(8,128)(2,1)S(1)}, u32[]{:S(2)}, u32[]{:S(2)}) collective-permute-start(bf16[128,1536]{1,0:T(8,128)(2,1)S(1)} %multiply_convert_fusion), channel_id=1, source_target_pairs={{0,128},{128,0},{16,144},{144,16},{32,160},{160,32},{48,176},{176,... | collective-permute-start | bytes 1179656 | tf_op jit(solution)/shard_map/ppermute | solution.py:14
Sparse Core Ops, SparseCore 0:
  100.1 77.3 reduce-scatter.4
  180.1 83.0 reduce-scatter.2

commit v2 on v1

v2 whole, which is shorter than its diff:
```python
import jax
import jax.numpy as jnp
from jax import lax
from jax.sharding import PartitionSpec as P


def partner_2(block, axis, apart):
    count = lax.axis_size(axis)
    route = []
    for low in range(count):
        high = low | 1 << apart
        if high != low and high < count:
            route += [(low, high), (high, low)]
    return lax.ppermute(block, axis, route)


def exchange(block, expert_count, capacity):
    shaped = block.reshape(expert_count, capacity, block.shape[-1])
    arrived = lax.all_to_all(shaped, "expert", split_axis=0, concat_axis=0, tiled=True)
    return arrived.reshape(expert_count * capacity, block.shape[-1])


def shards(tokens, cotangent, expert_ids, gate_weights, placement, w_in, w_out):
    expert_count = lax.axis_size("expert")
    group_count = lax.axis_size("dp")
    own_index = lax.axis_index("expert")
    tok_rows = tokens.shape[0]
    model_width = tokens.shape[1]
    hidden_units = w_out.shape[1]
    pick_count = expert_ids.shape[1]
    capacity = tok_rows // 8
    slot_count = expert_count * capacity
    pick_rows = tok_rows * pick_count
    half_bit = expert_count.bit_length() - 2
    expert_lane = jnp.arange(expert_count, dtype=jnp.int32)
    partner = jnp.sum(jnp.where(expert_lane == own_index, placement, 0))
    is_moved = partner != own_index
    weight_in = w_in[0]
    weight_out = w_out[0]

    device_hot = (expert_ids.reshape(-1)[:, None] == expert_lane[None, :]).astype(jnp.bfloat16)
    row_lane = jnp.arange(pick_rows, dtype=jnp.int32)
    earlier = (row_lane[None, :] < row_lane[:, None]).astype(jnp.bfloat16)
    slot_rank = jnp.dot(earlier, device_hot, preferred_element_type=jnp.float32).astype(jnp.int32)
    hot = device_hot.astype(jnp.int32)
    slot_place = jnp.sum((slot_rank + expert_lane[None, :] * capacity) * hot, axis=1)
    is_live = jnp.sum(hot, axis=1) > 0
    slot_place = jnp.where(is_live, slot_place, -1).reshape(tok_rows, pick_count)
    slot_hot = slot_place[:, :, None] == jnp.arange(slot_count, dtype=jnp.int32)[None, None, :]
    select = jnp.sum(slot_hot.astype(jnp.bfloat16), axis=1)
    weigh = jnp.sum(jnp.where(slot_hot, gate_weights[:, :, None], 0.0), axis=1)
    slot_gate = jnp.sum(weigh, axis=0)

    send_x = jnp.einsum("ts,td->sd", select, tokens, preferred_element_type=jnp.float32).astype(
        jnp.bfloat16
    )
    send_dy = jnp.einsum("ts,td->sd", select, cotangent, preferred_element_type=jnp.float32)
    send_c = (send_dy * slot_gate[:, None]).astype(jnp.bfloat16)
    arrived = exchange(jnp.concatenate([send_x, send_c], axis=1), expert_count, capacity)
    rows_x = arrived[:, :model_width]
    rows_c = arrived[:, model_width:]

    pre = jnp.dot(rows_x, weight_in, preferred_element_type=jnp.float32)
    gate_pre = pre[:, :hidden_units]
    up_pre = pre[:, hidden_units:]
    sigmoid_gate = jax.nn.sigmoid(gate_pre)
    activated = gate_pre * sigmoid_gate
    hidden = (activated * up_pre).astype(jnp.bfloat16)
    expert_out = jnp.dot(hidden, weight_out, preferred_element_type=jnp.float32).astype(
        jnp.bfloat16
    )

    hidden_grad = jnp.einsum("sd,fd->sf", rows_c, weight_out, preferred_element_type=jnp.float32)
    slope = sigmoid_gate * (1.0 + gate_pre * (1.0 - sigmoid_gate))
    gate_up_grad = jnp.concatenate(
        [hidden_grad * up_pre * slope, hidden_grad * activated], axis=1
    ).astype(jnp.bfloat16)
    part_out = jnp.einsum("sf,sd->fd", hidden, rows_c, preferred_element_type=jnp.float32).astype(
        jnp.bfloat16
    )
    grad_out = lax.psum_scatter(part_out, "dp", scatter_dimension=0, tiled=True)
    part_in = jnp.einsum("sd,sf->df", rows_x, gate_up_grad, preferred_element_type=jnp.float32).astype(
        jnp.bfloat16
    )
    grad_in = lax.psum_scatter(part_in, "dp", scatter_dimension=0, tiled=True)
    pick_grad = jnp.einsum(
        "sf,df->sd", gate_up_grad, weight_in, preferred_element_type=jnp.float32
    ).astype(jnp.bfloat16)

    back = exchange(jnp.concatenate([expert_out, pick_grad], axis=1), expert_count, capacity)
    returned = back[:, :model_width]
    back_grad = back[:, model_width:]
    mixed = jnp.dot(
        weigh,
        returned.astype(jnp.float32),
        precision=lax.Precision.HIGHEST,
        preferred_element_type=jnp.float32,
    ).astype(jnp.bfloat16)
    scores = jnp.einsum("td,sd->ts", cotangent, returned, preferred_element_type=jnp.float32)
    gate_grad = jnp.sum(jnp.where(slot_hot, scores[:, None, :], 0.0), axis=2)
    x_grad = jnp.einsum("ts,sd->td", select, back_grad, preferred_element_type=jnp.float32).astype(
        jnp.bfloat16
    )

    grad_in = (grad_in.astype(jnp.float32) / group_count).astype(jnp.bfloat16)
    grad_out = (grad_out.astype(jnp.float32) / group_count).astype(jnp.bfloat16)
    swapped = partner_2((grad_in, grad_out), "expert", half_bit)
    grad_in = jnp.where(is_moved, swapped[0], grad_in)
    grad_out = jnp.where(is_moved, swapped[1], grad_out)
    return (mixed, x_grad, gate_grad, grad_in[None], grad_out[None])


def solution(mesh):
    placed = (
        P(("expert", "dp"), None),
        P(("expert", "dp"), None),
        P(("expert", "dp"), None),
        P(("expert", "dp"), None),
        P(),
        P("expert", None, None),
        P("expert", None, None),
    )
    return jax.shard_map(
        shards,
        mesh=mesh,
        in_specs=placed,
        out_specs=(
            P(("expert", "dp"), None),
            P(("expert", "dp"), None),
            P(("expert", "dp"), None),
            P("expert", "dp", None),
            P("expert", "dp", None),
        ),
        check_vma=False,
    )
```

time: 283 us -> 238 us (0.84)
  waiting for transfers between devices: 154 us -> 135 us
  blocking collectives: 43.3 us -> 34 us
  starting transfers between devices: 16.7 us -> 9.34 us
  matrix products: 33.4 us -> 28.3 us
  other arithmetic: 13.9 us -> 10.5 us
    reduce_scatter x2, waiting for transfers between devices: 107 us -> 78.2 us  [the longest x1 78.2 us: shards(): grad_in = lax.psum_scatter(part_in, 'dp', scatter_dimension=0, tiled=True)]
    all_to_all x2 -> x1, waiting for transfers between devices: 40.2 us -> 50.7 us  [exchange(): lax.all_to_all(shaped, 'expert', split_axis=0, concat_axis=0, tiled=True)]
    all_to_all x2 -> x1, blocking collectives: 43.3 us -> 34 us  [exchange(): lax.all_to_all(shaped, 'expert', split_axis=0, concat_axis=0, tiled=True)]
    all_to_all x2 -> x1, starting transfers between devices: 13.4 us -> 6.75 us  [exchange(): lax.all_to_all(shaped, 'expert', split_axis=0, concat_axis=0, tiled=True)]
    another operation x3 -> x0, other arithmetic: 4.64 us -> none
    dot_general x1, matrix products: 4.94 us -> 1.8 us  [shards(): pre = jnp.dot(rows_x, weight_in, preferred_element_type=jnp.float32)]
  transfers between devices with their start and end apart: 6 -> 5, of which waited for: 5 -> 3; matrix products, arithmetic and copies ran while one was open for 8% -> 12% of each run, Pallas kernels for 0% -> 0%
where the time goes in v2:
time: 238 us; the launch traced here: 237 us
  waiting for transfers between devices  135 us (57%)
  blocking collectives  34 us (14%)
  matrix products  28.3 us (12%)
  between operations  15 us (6%)
  other arithmetic  10.5 us (4%)
  starting transfers between devices  9.34 us (4%)
  local copies, waits for them, and re-layouts  4.58 us (2%)
    reduce_scatter x1, waiting for transfers between devices, shards(): grad_in = lax.psum_scatter(part_in, 'dp', scatter_dimension=0, tiled=True)  78.2 us
    all_to_all x1, waiting for transfers between devices, exchange(): lax.all_to_all(shaped, 'expert', split_axis=0, concat_axis=0, tiled=True)  50.7 us
    all_to_all x1, blocking collectives, exchange(): lax.all_to_all(shaped, 'expert', split_axis=0, concat_axis=0, tiled=True)  34 us
    all_to_all x1, starting transfers between devices, exchange(): lax.all_to_all(shaped, 'expert', split_axis=0, concat_axis=0, tiled=True)  6.75 us
    ppermute x2, waiting for transfers between devices, partner_2(): return lax.ppermute(block, axis, route)  6.39 us
    dot_general x1, matrix products, shards(): jnp.einsum('sd,sf->df', rows_x, gate_up_grad, preferred_element_type=jnp....  5.92 us
  transfers between devices with their start and end apart: 5, of which 3 were waited for; matrix products, arithmetic and copies ran while one was open for 12% of the time, Pallas kernels for 0%

profile of v2, /device:TPU:24, one launch (start us, length us, event | category | flops | bytes accessed | tf_op | source)
XLA Modules:
  0.0 237.0 jit_solution(12565265884144285768)
XLA Ops:
  7.2 0.9 copy.17
  8.3 0.5 fusion.19
  8.9 0.4 fusion.29
  9.3 0.8 copy.18
  10.2 1.1 select_reduce_fusion
  11.2 1.6 convolution_convert_fusion.2
  12.9 0.5 fusion.9
  13.6 34.0 %all_to_all.10 = bf16[16,16,4096]{2,1,0:T(8,128)(2,1)S(1)} all-to-all(bf16[16,16,4096]{2,1,0:T(8,128)(2,1)S(1)} %bitcast.40), channel_id=1, replica_groups=mesh['expert'=16,'dp'=16] {'expert'}, dimensions={0} | all-to-all | bytes 4194304 | tf_op jit(solution)/shard_map/all_to_all | solution.py:19
  47.6 1.8 fusion.2
  49.4 2.3 multiply_convert_fusion.2
  51.7 2.7 %convolution_convert_fusion.1 = bf16[768,2048]{1,0:T(8,128)(2,1)} fusion(bf16[256,768]{1,0:T(8,128)(2,1)S(1)} %get-tuple-element.14, bf16[256,4096]{1,0:T(8,128)(2,1)S(1)} %bitcast.37), kind=kOutput, calls=%fused_computation.7 | convolution fusion | flops 806879232 | bytes 4587520 | tf_op jit(solution)/shard_map/sf,sd->fd/dot_general | solution.py:78
  54.5 5.9 %convolution_convert_fusion = bf16[2048,1536]{1,0:T(8,128)(2,1)} fusion(bf16[256,4096]{1,0:T(8,128)(2,1)} %bitcast.38, bf16[256,768]{1,0:T(8,128)(2,1)} %get-tuple-element.13, bf16[256,768]{1,0:T(8,128)(2,1)} %get-tuple-element.12), kind=kOutput, calls=%fused_computation | convolution fusion | flops 1615331328 | bytes 8126464 | tf_op jit(solution)/shard_map/sd,sf->df/dot_general | solution.py:82
  60.5 1.0 fusion.13
  61.6 4.6 %fusion.10 = bf16[256,2048]{1,0:T(8,128)(2,1)S(1)} fusion(bf16[1,2048,1536]{2,1,0:T(8,128)(2,1)} %param.12, bf16[256,768]{1,0:T(8,128)(2,1)S(1)} %copy-done.9, bf16[256,768]{1,0:T(8,128)(2,1)S(1)} %copy-done.8), kind=kOutput, calls=%fused_computation.15 | convolution fusion | flops 1612709888 | bytes 8126464 | tf_op jit(solution)/shard_map/sf,df->sd/dot_general | solution.py:86
  66.2 1.6 pad_maximum_fusion.1
  67.7 6.8 %all-to-all-start.1 = ((bf16[16,16,4096]{2,1,0:T(8,128)(2,1)}), bf16[16,16,4096]{2,1,0:T(8,128)(2,1)}, u32[]{:S(2)}, u32[]{:S(2)}) async-start(bf16[16,16,4096]{2,1,0:T(8,128)(2,1)} %bitcast.39), calls=%async_computation.1 | async-start | bytes 4194304 | tf_op jit(solution)/shard_map/all_to_all | solution.py:19
  74.5 0.6 fusion.32
  75.8 50.7 %all-to-all-done.1 = bf16[16,16,4096]{2,1,0:T(8,128)(2,1)} async-done(((bf16[16,16,4096]{2,1,0:T(8,128)(2,1)}), bf16[16,16,4096]{2,1,0:T(8,128)(2,1)}, u32[]{:S(2)}, u32[]{:S(2)}) %all-to-all-start.1) | async-done | bytes 2097184 | tf_op jit(solution)/shard_map/all_to_all | solution.py:19
  126.5 2.5 %convolution_bitcast_fusion = f32[128,256]{0,1:T(8,128)} fusion(bf16[128,2048]{1,0:T(8,128)(2,1)} %param.8, bf16[256,4096]{1,0:T(8,128)(2,1)} %bitcast.5), kind=kOutput, calls=%fused_computation.23 | convolution fusion | flops 134217728 | bytes 1703936 | tf_op jit(solution)/shard_map/td,sd->ts/dot_general | solution.py:99
  129.0 1.0 copy.19
  130.0 1.0 select_reduce_fusion.2
  131.0 1.5 copy.20
  132.5 2.3 convolution_convert_fusion.3
  134.9 2.6 %convolution_convert_fusion.4 = bf16[128,2048]{1,0:T(8,128)(2,1)} fusion(f32[128,256]{1,0:T(8,128)S(1)} %copy-done.7, bf16[256,4096]{1,0:T(8,128)(2,1)} %bitcast.5), kind=kOutput, calls=%fused_computation.18 | convolution fusion | flops 805568512 | bytes 1703936 | tf_op jit(solution)/shard_map/dot_general | solution.py:93
  137.5 1.0 multiply_convert_fusion.4
  138.4 1.2 collective-permute-start.1
  139.6 78.2 %reduce-scatter.3.cloned.1.call-done = bf16[128,1536]{1,0:T(8,128)(2,1)} async-done(((bf16[2048,1536]{1,0:T(8,128)(2,1)}), bf16[128,1536]{1,0:T(8,128)(2,1)}) %reduce-scatter.3.cloned.1.call-update) | async-done | bytes 393232 | tf_op jit(solution)/shard_map/reduce_scatter | solution.py:85
  217.9 1.1 multiply_convert_fusion
  218.9 1.3 collective-permute-start
  220.2 1.7 select_bitcast_fusion.1
  221.9 6.4 %collective-permute-done = bf16[128,1536]{1,0:T(8,128)(2,1)S(1)} collective-permute-done((bf16[128,1536]{1,0:T(8,128)(2,1)S(1)}, bf16[128,1536]{1,0:T(8,128)(2,1)S(1)}, u32[]{:S(2)}, u32[]{:S(2)}) %collective-permute-start) | collective-permute-done | bytes 393248 | tf_op jit(solution)/shard_map/ppermute | solution.py:14
  228.3 1.9 select_bitcast_fusion
  (39 shorter events, 0.7 us)
Async XLA Ops:
  7.2 42.3 %copy-start = (bf16[1,768,2048]{2,1,0:T(8,128)(2,1)S(1)}, bf16[1,768,2048]{2,1,0:T(8,128)(2,1)}, u32[]{:S(2)}) copy-start(bf16[1,768,2048]{2,1,0:T(8,128)(2,1)} %param.13) | copy-start | bytes 9437188
  7.2 130.3 %reduce-scatter.5.cloned.1.call-start = ((), (), s32[]{:S(2)}) async-start(), calls=%async_computation.5 | async-start | bytes 3342336 | tf_op jit(solution)/shard_map/reduce_scatter | solution.py:81
  8.9 4.7 %copy-start.4 = (s32[128,8]{1,0:T(8,128)}, s32[128,8]{1,0:T(8,128)S(1)}, u32[]{:S(2)}) copy-start(s32[128,8]{1,0:T(8,128)S(1)} %select_n.40) | copy-start | bytes 12292
  9.3 4.3 %copy-start.2 = (bf16[128,256]{1,0:T(8,128)(2,1)}, bf16[128,256]{1,0:T(8,128)(2,1)S(1)}, u32[]{:S(2)}) copy-start(bf16[128,256]{1,0:T(8,128)(2,1)S(1)} %fusion.29) | copy-start | bytes 196612
  10.1 2.7 %copy-start.6 = (bf16[128,2048]{1,0:T(8,128)(2,1)S(1)}, bf16[128,2048]{1,0:T(8,128)(2,1)}, u32[]{:S(2)}) copy-start(bf16[128,2048]{1,0:T(8,128)(2,1)} %param.8) | copy-start | bytes 1572868
  11.2 36.4 %slice-start = ((s8[6291456]{0:T(1024)(128)(4,1)}), s8[4194304]{0:T(1024)(128)(4,1)S(1)}, s32[]{:S(2)}) async-start(s8[6291456]{0:T(1024)(128)(4,1)} %bitcast.41), calls=%async_computation.6 | async-start | bytes 8388608
  13.3 34.3 %slice-start.1 = ((s8[6291456]{0:T(1024)(128)(4,1)}), s8[2097152]{0:T(1024)(128)(4,1)S(1)}, s32[]{:S(2)}) async-start(s8[6291456]{0:T(1024)(128)(4,1)} %bitcast.41), calls=%async_computation.7 | async-start | bytes 4194304
  47.6 4.1 %copy-start.1 = (bf16[16,16,4096]{2,1,0:T(8,128)(2,1)}, bf16[16,16,4096]{2,1,0:T(8,128)(2,1)S(1)}, u32[]{:S(2)}) copy-start(bf16[16,16,4096]{2,1,0:T(8,128)(2,1)S(1)} %all_to_all.10) | copy-start | bytes 6291460
  54.4 163.4 %reduce-scatter.3.cloned.1.call-start = ((), (), s32[]{:S(2)}) async-start(), calls=%async_computation.4 | async-start | bytes 6684672 | tf_op jit(solution)/shard_map/reduce_scatter | solution.py:85
  60.4 1.0 copy-start.8
  60.5 1.1 copy-start.9
  67.7 6.8 %copy-start.10 = (s32[16]{0:T(128)S(1)}, s32[16]{0:T(128)}, u32[]{:S(2)}) copy-start(s32[16]{0:T(128)} %param.11) | copy-start | bytes 196
  67.7 58.8 %all-to-all-start.1 = ((bf16[16,16,4096]{2,1,0:T(8,128)(2,1)}), bf16[16,16,4096]{2,1,0:T(8,128)(2,1)}, u32[]{:S(2)}, u32[]{:S(2)}) async-start(bf16[16,16,4096]{2,1,0:T(8,128)(2,1)} %bitcast.39), calls=%async_computation.1 | async-start | bytes 4194304 | tf_op jit(solution)/shard_map/all_to_all | solution.py:19
  74.5 55.5 %copy-start.5 = (s32[128,8]{1,0:T(8,128)S(1)}, s32[128,8]{1,0:T(8,128)}, u32[]{:S(2)}) copy-start(s32[128,8]{1,0:T(8,128)} %copy-done.4) | copy-start | bytes 12292
  74.5 58.0 %copy-start.3 = (bf16[128,256]{1,0:T(8,128)(2,1)S(1)}, bf16[128,256]{1,0:T(8,128)(2,1)}, u32[]{:S(2)}) copy-start(bf16[128,256]{1,0:T(8,128)(2,1)} %copy-done.2) | copy-start | bytes 196612
  75.1 59.7 %copy-start.7 = (f32[128,256]{1,0:T(8,128)S(1)}, f32[128,256]{1,0:T(8,128)}, u32[]{:S(2)}) copy-start(f32[128,256]{1,0:T(8,128)} %get-tuple-element.11) | copy-start | bytes 393220
  138.4 81.8 %collective-permute-start.1 = (bf16[48,2048]{1,0:T(8,128)(2,1)S(1)}, bf16[48,2048]{1,0:T(8,128)(2,1)S(1)}, u32[]{:S(2)}, u32[]{:S(2)}) collective-permute-start(bf16[48,2048]{1,0:T(8,128)(2,1)S(1)} %multiply_convert_fusion.4), channel_id=1, source_target_pairs={{0,128},{128,0},{16,144},{144,16},{32,160},{160,32},{48,176},{176,... | collective-permute-start | bytes 589832 | tf_op jit(solution)/shard_map/ppermute | solution.py:14
  218.9 9.4 %collective-permute-start = (bf16[128,1536]{1,0:T(8,128)(2,1)S(1)}, bf16[128,1536]{1,0:T(8,128)(2,1)S(1)}, u32[]{:S(2)}, u32[]{:S(2)}) collective-permute-start(bf16[128,1536]{1,0:T(8,128)(2,1)S(1)} %multiply_convert_fusion), channel_id=1, source_target_pairs={{0,128},{128,0},{16,144},{144,16},{32,160},{160,32},{48,176},{176,... | collective-permute-start | bytes 1179656 | tf_op jit(solution)/shard_map/ppermute | solution.py:14
Sparse Core Ops, SparseCore 0:
  54.6 77.4 reduce-scatter.4
  134.7 83.1 reduce-scatter.2

commit v3 on v2

--- a/solution.py
+++ b/solution.py
@@ -78,11 +78,21 @@
     part_out = jnp.einsum("sf,sd->fd", hidden, rows_c, preferred_element_type=jnp.float32).astype(
         jnp.bfloat16
     )
-    grad_out = lax.psum_scatter(part_out, "dp", scatter_dimension=0, tiled=True)
     part_in = jnp.einsum("sd,sf->df", rows_x, gate_up_grad, preferred_element_type=jnp.float32).astype(
         jnp.bfloat16
     )
-    grad_in = lax.psum_scatter(part_in, "dp", scatter_dimension=0, tiled=True)
+    in_rows = model_width // group_count
+    in_cols = part_in.shape[1]
+    out_rows = hidden_units // group_count
+    out_as = out_rows * model_width // in_cols
+    joined = jnp.concatenate(
+        [
+            part_in.reshape(group_count, in_rows, in_cols),
+            part_out.reshape(group_count, out_as, in_cols),
+        ],
+        axis=1,
+    ).reshape(group_count * (in_rows + out_as), in_cols)
+    reduced = lax.psum_scatter(joined, "dp", scatter_dimension=0, tiled=True)
     pick_grad = jnp.einsum(
         "sf,df->sd", gate_up_grad, weight_in, preferred_element_type=jnp.float32
     ).astype(jnp.bfloat16)
@@ -102,11 +112,11 @@
         jnp.bfloat16
     )
 
-    grad_in = (grad_in.astype(jnp.float32) / group_count).astype(jnp.bfloat16)
-    grad_out = (grad_out.astype(jnp.float32) / group_count).astype(jnp.bfloat16)
-    swapped = partner_2((grad_in, grad_out), "expert", half_bit)
-    grad_in = jnp.where(is_moved, swapped[0], grad_in)
-    grad_out = jnp.where(is_moved, swapped[1], grad_out)
+    reduced = (reduced.astype(jnp.float32) / group_count).astype(jnp.bfloat16)
+    swapped = partner_2(reduced, "expert", half_bit)
+    reduced = jnp.where(is_moved, swapped, reduced)
+    grad_in = reduced[:in_rows]
+    grad_out = reduced[in_rows:].reshape(out_rows, model_width)
     return (mixed, x_grad, gate_grad, grad_in[None], grad_out[None])
 
 

time: 238 us -> 238 us (level)
  local copies, waits for them, and re-layouts: 4.58 us -> 12.3 us
  waiting for transfers between devices: 135 us -> 129 us
  matrix products: 28.3 us -> 25.8 us
    reduce_scatter x2 -> x1, waiting for transfers between devices: 78.2 us -> 0.02 us  [shards(): reduced = lax.psum_scatter(joined, 'dp', scatter_dimension=0, tiled=True)]
    all_to_all x1, waiting for transfers between devices: 50.7 us -> 120 us  [exchange(): lax.all_to_all(shaped, 'expert', split_axis=0, concat_axis=0, tiled=True)]
    reshape x0 -> x1, local copies, waits for them, and re-layouts: none -> 6.02 us  [shards(): part_out.reshape(group_count, out_as, in_cols)]
    concatenate x0 -> x1, other arithmetic: none -> 3.91 us  [shards(): jnp.concatenate([part_in.reshape(group_count, in_rows, in_cols), part_out...]
    broadcast_in_dim x2 -> x0, other arithmetic: 3.52 us -> none  [shards(): return (mixed, x_grad, gate_grad, grad_in[None], grad_out[None])]
    dot_general x1, matrix products: 5.92 us -> 3.41 us  [shards(): jnp.einsum('sd,sf->df', rows_x, gate_up_grad, preferred_element_type=jnp....]
    ppermute x2 -> x1, waiting for transfers between devices: 6.39 us -> 8.14 us  [partner_2(): return lax.ppermute(block, axis, route)]
  transfers between devices with their start and end apart: 5 -> 3, of which waited for: 3 -> 2; matrix products, arithmetic and copies ran while one was open for 12% -> 8% of each run, Pallas kernels for 0% -> 0%
where the time goes in v3:
time: 238 us; the launch traced here: 236 us
  waiting for transfers between devices  129 us (54%)
  blocking collectives  34 us (14%)
  matrix products  25.8 us (11%)
  between operations  14.9 us (6%)
  local copies, waits for them, and re-layouts  12.3 us (5%)
  other arithmetic  12.1 us (5%)
  starting transfers between devices  8.25 us (3%)
    all_to_all x1, waiting for transfers between devices, exchange(): lax.all_to_all(shaped, 'expert', split_axis=0, concat_axis=0, tiled=True)  120 us
    all_to_all x1, blocking collectives, exchange(): lax.all_to_all(shaped, 'expert', split_axis=0, concat_axis=0, tiled=True)  34 us
    ppermute x1, waiting for transfers between devices, partner_2(): return lax.ppermute(block, axis, route)  8.14 us
    all_to_all x1, starting transfers between devices, exchange(): lax.all_to_all(shaped, 'expert', split_axis=0, concat_axis=0, tiled=True)  6.8 us
    reshape x1, local copies, waits for them, and re-layouts, shards(): part_out.reshape(group_count, out_as, in_cols)  6.02 us
  transfers between devices with their start and end apart: 3, of which 2 were waited for; matrix products, arithmetic and copies ran while one was open for 8% of the time, Pallas kernels for 0%

profile of v3, /device:TPU:24, one launch (start us, length us, event | category | flops | bytes accessed | tf_op | source)
XLA Modules:
  0.0 235.9 jit_solution(8062777475649416183)
XLA Ops:
  7.2 0.9 copy.18
  8.2 0.8 copy.17
  9.1 0.5 fusion.19
  9.7 0.4 fusion.29
  10.1 1.1 select_reduce_fusion
  11.2 1.6 convolution_convert_fusion.2
  12.9 0.5 fusion.9
  13.6 34.0 %all_to_all.10 = bf16[16,16,4096]{2,1,0:T(8,128)(2,1)S(1)} all-to-all(bf16[16,16,4096]{2,1,0:T(8,128)(2,1)S(1)} %bitcast.42), channel_id=1, replica_groups=mesh['expert'=16,'dp'=16] {'expert'}, dimensions={0} | all-to-all | bytes 4194304 | tf_op jit(solution)/shard_map/all_to_all | solution.py:19
  47.6 1.8 fusion.2
  49.4 2.3 multiply_convert_fusion.2
  51.7 2.7 %convolution_convert_fusion.1 = bf16[768,2048]{1,0:T(8,128)(2,1)} fusion(bf16[256,768]{1,0:T(8,128)(2,1)S(1)} %get-tuple-element.14, bf16[256,4096]{1,0:T(8,128)(2,1)S(1)} %bitcast.39), kind=kOutput, calls=%fused_computation.8 | convolution fusion | flops 806879232 | bytes 4587520 | tf_op jit(solution)/shard_map/sf,sd->fd/dot_general | solution.py:78
  54.4 6.0 %reshape.59 = bf16[16,64,1536]{2,1,0:T(8,128)(2,1)} reshape(bf16[768,2048]{1,0:T(8,128)(2,1)} %convolution_convert_fusion.1) | data formatting | bytes 6291456 | tf_op jit(solution)/shard_map/reshape | solution.py:91
  60.4 3.4 %convolution_convert_fusion = bf16[2048,1536]{1,0:T(8,128)(2,1)S(1)} fusion(bf16[256,4096]{1,0:T(8,128)(2,1)} %bitcast.40, bf16[256,768]{1,0:T(8,128)(2,1)} %get-tuple-element.13, bf16[256,768]{1,0:T(8,128)(2,1)} %get-tuple-element.12), kind=kOutput, calls=%fused_computation.1 | convolution fusion | flops 1615331328 | bytes 8126464 | tf_op jit(solution)/shard_map/sd,sf->df/dot_general | solution.py:81
  63.9 3.9 %pad_maximum_fusion = bf16[16,192,1536]{2,1,0:T(8,128)(2,1)} fusion(bf16[16,64,1536]{2,1,0:T(8,128)(2,1)S(1)} %copy-done.1, bf16[16,128,1536]{2,1,0:T(8,128)(2,1)S(1)} %bitcast.36), kind=kLoop, calls=%fused_computation | loop fusion | flops 18874368 | bytes 18874368 | tf_op jit(solution)/shard_map/concatenate | solution.py:88
  67.8 1.0 fusion.13
  68.9 4.6 %fusion.10 = bf16[256,2048]{1,0:T(8,128)(2,1)S(1)} fusion(bf16[1,2048,1536]{2,1,0:T(8,128)(2,1)} %param.12, bf16[256,768]{1,0:T(8,128)(2,1)S(1)} %copy-done.11, bf16[256,768]{1,0:T(8,128)(2,1)S(1)} %copy-done.10), kind=kOutput, calls=%fused_computation.16 | convolution fusion | flops 1612709888 | bytes 8126464 | tf_op jit(solution)/shard_map/sf,df->sd/dot_general | solution.py:96
  73.5 1.6 pad_maximum_fusion.2
  75.1 6.8 %all-to-all-start.1 = ((bf16[16,16,4096]{2,1,0:T(8,128)(2,1)}), bf16[16,16,4096]{2,1,0:T(8,128)(2,1)}, u32[]{:S(2)}, u32[]{:S(2)}) async-start(bf16[16,16,4096]{2,1,0:T(8,128)(2,1)} %bitcast.41), calls=%async_computation.1 | async-start | bytes 4194304 | tf_op jit(solution)/shard_map/all_to_all | solution.py:19
  81.9 0.6 fusion.32
  83.2 120.4 %all-to-all-done.1 = bf16[16,16,4096]{2,1,0:T(8,128)(2,1)} async-done(((bf16[16,16,4096]{2,1,0:T(8,128)(2,1)}), bf16[16,16,4096]{2,1,0:T(8,128)(2,1)}, u32[]{:S(2)}, u32[]{:S(2)}) %all-to-all-start.1) | async-done | bytes 2097184 | tf_op jit(solution)/shard_map/all_to_all | solution.py:19
  203.6 2.4 %convolution_bitcast_fusion = f32[128,256]{0,1:T(8,128)} fusion(bf16[128,2048]{1,0:T(8,128)(2,1)} %param.8, bf16[256,4096]{1,0:T(8,128)(2,1)} %bitcast.5), kind=kOutput, calls=%fused_computation.25 | convolution fusion | flops 134217728 | bytes 1703936 | tf_op jit(solution)/shard_map/td,sd->ts/dot_general | solution.py:109
  206.0 1.0 copy.19
  207.1 2.0 multiply_convert_fusion
  209.1 1.4 collective-permute-start
  210.5 1.0 select_reduce_fusion.2
  211.5 1.5 copy.20
  213.0 2.4 %convolution_convert_fusion.3 = bf16[128,2048]{1,0:T(8,128)(2,1)} fusion(bf16[128,256]{1,0:T(8,128)(2,1)S(1)} %copy-done.5, bf16[256,4096]{1,0:T(8,128)(2,1)} %bitcast.5), kind=kOutput, calls=%fused_computation.18 | convolution fusion | flops 134479872 | bytes 1638400 | tf_op jit(solution)/shard_map/ts,sd->td/dot_general | solution.py:111
  215.4 2.6 %convolution_convert_fusion.4 = bf16[128,2048]{1,0:T(8,128)(2,1)} fusion(f32[128,256]{1,0:T(8,128)S(1)} %copy-done.9, bf16[256,4096]{1,0:T(8,128)(2,1)} %bitcast.5), kind=kOutput, calls=%fused_computation.19 | convolution fusion | flops 805568512 | bytes 1703936 | tf_op jit(solution)/shard_map/dot_general | solution.py:103
  218.0 8.1 %collective-permute-done = bf16[192,1536]{1,0:T(8,128)(2,1)} collective-permute-done((bf16[192,1536]{1,0:T(8,128)(2,1)}, bf16[192,1536]{1,0:T(8,128)(2,1)}, u32[]{:S(2)}, u32[]{:S(2)}) %collective-permute-start) | collective-permute-done | bytes 589856 | tf_op jit(solution)/shard_map/ppermute | solution.py:14
  226.2 1.2 broadcast_select_fusion
  227.4 0.8 slice_bitcast_fusion
  228.2 0.9 broadcast_in_dim_reshape.2
  (41 shorter events, 0.7 us)
Async XLA Ops:
  7.2 42.3 %copy-start = (bf16[1,768,2048]{2,1,0:T(8,128)(2,1)S(1)}, bf16[1,768,2048]{2,1,0:T(8,128)(2,1)}, u32[]{:S(2)}) copy-start(bf16[1,768,2048]{2,1,0:T(8,128)(2,1)} %param.13) | copy-start | bytes 9437188
  7.2 199.9 %reduce-scatter.2.cloned.1.call-start = ((), (), s32[]{:S(2)}) async-start(), calls=%async_computation.3 | async-start | bytes 10027008 | tf_op jit(solution)/shard_map/reduce_scatter | solution.py:95
  9.7 3.9 %copy-start.6 = (s32[128,8]{1,0:T(8,128)}, s32[128,8]{1,0:T(8,128)S(1)}, u32[]{:S(2)}) copy-start(s32[128,8]{1,0:T(8,128)S(1)} %select_n.32) | copy-start | bytes 12292
  9.7 3.2 %copy-start.8 = (bf16[128,2048]{1,0:T(8,128)(2,1)S(1)}, bf16[128,2048]{1,0:T(8,128)(2,1)}, u32[]{:S(2)}) copy-start(bf16[128,2048]{1,0:T(8,128)(2,1)} %param.8) | copy-start | bytes 1572868
  10.1 2.7 %copy-start.4 = (bf16[128,256]{1,0:T(8,128)(2,1)}, bf16[128,256]{1,0:T(8,128)(2,1)S(1)}, u32[]{:S(2)}) copy-start(bf16[128,256]{1,0:T(8,128)(2,1)S(1)} %fusion.29) | copy-start | bytes 196612
  11.2 36.4 %slice-start = ((s8[6291456]{0:T(1024)(128)(4,1)}), s8[4194304]{0:T(1024)(128)(4,1)S(1)}, s32[]{:S(2)}) async-start(s8[6291456]{0:T(1024)(128)(4,1)} %bitcast.43), calls=%async_computation.4 | async-start | bytes 8388608
  13.3 34.3 %slice-start.1 = ((s8[6291456]{0:T(1024)(128)(4,1)}), s8[2097152]{0:T(1024)(128)(4,1)S(1)}, s32[]{:S(2)}) async-start(s8[6291456]{0:T(1024)(128)(4,1)} %bitcast.43), calls=%async_computation.5 | async-start | bytes 4194304
  47.6 4.1 %copy-start.2 = (bf16[16,16,4096]{2,1,0:T(8,128)(2,1)}, bf16[16,16,4096]{2,1,0:T(8,128)(2,1)S(1)}, u32[]{:S(2)}) copy-start(bf16[16,16,4096]{2,1,0:T(8,128)(2,1)S(1)} %all_to_all.10) | copy-start | bytes 6291460
  60.4 3.4 %copy-start.1 = (bf16[16,64,1536]{2,1,0:T(8,128)(2,1)S(1)}, bf16[16,64,1536]{2,1,0:T(8,128)(2,1)}, u32[]{:S(2)}) copy-start(bf16[16,64,1536]{2,1,0:T(8,128)(2,1)} %reshape.59) | copy-start | bytes 9437188
  67.8 1.0 copy-start.10
  67.8 1.1 copy-start.11
  75.1 6.8 %copy-start.12 = (s32[16]{0:T(128)S(1)}, s32[16]{0:T(128)}, u32[]{:S(2)}) copy-start(s32[16]{0:T(128)} %param.11) | copy-start | bytes 196
  75.1 128.5 %all-to-all-start.1 = ((bf16[16,16,4096]{2,1,0:T(8,128)(2,1)}), bf16[16,16,4096]{2,1,0:T(8,128)(2,1)}, u32[]{:S(2)}, u32[]{:S(2)}) async-start(bf16[16,16,4096]{2,1,0:T(8,128)(2,1)} %bitcast.41), calls=%async_computation.1 | async-start | bytes 4194304 | tf_op jit(solution)/shard_map/all_to_all | solution.py:19
  81.9 128.7 %copy-start.7 = (s32[128,8]{1,0:T(8,128)S(1)}, s32[128,8]{1,0:T(8,128)}, u32[]{:S(2)}) copy-start(s32[128,8]{1,0:T(8,128)} %copy-done.6) | copy-start | bytes 12292
  81.9 131.2 %copy-start.5 = (bf16[128,256]{1,0:T(8,128)(2,1)S(1)}, bf16[128,256]{1,0:T(8,128)(2,1)}, u32[]{:S(2)}) copy-start(bf16[128,256]{1,0:T(8,128)(2,1)} %copy-done.4) | copy-start | bytes 196612
  206.0 9.4 %copy-start.9 = (f32[128,256]{1,0:T(8,128)S(1)}, f32[128,256]{1,0:T(8,128)}, u32[]{:S(2)}) copy-start(f32[128,256]{1,0:T(8,128)} %get-tuple-element.11) | copy-start | bytes 393220
  209.1 17.1 %collective-permute-start = (bf16[192,1536]{1,0:T(8,128)(2,1)}, bf16[192,1536]{1,0:T(8,128)(2,1)}, u32[]{:S(2)}, u32[]{:S(2)}) collective-permute-start(bf16[192,1536]{1,0:T(8,128)(2,1)} %multiply_convert_fusion), channel_id=1, source_target_pairs={{0,128},{128,0},{16,144},{144,16},{32,160},{160,32},{48,176},{176,... | collective-permute-start | bytes 1769480 | tf_op jit(solution)/shard_map/ppermute | solution.py:14
  213.0 13.1 %copy-start.3 = (bf16[192,1536]{1,0:T(8,128)(2,1)S(1)}, bf16[192,1536]{1,0:T(8,128)(2,1)}, u32[]{:S(2)}) copy-start(bf16[192,1536]{1,0:T(8,128)(2,1)} %reduce-scatter.2.cloned.1.call-done) | copy-start | bytes 1769476
Sparse Core Ops, SparseCore 0:
  67.9 111.9 reduce-scatter.1

commit v4 on v3

--- a/solution.py
+++ b/solution.py
@@ -69,37 +69,42 @@
     expert_out = jnp.dot(hidden, weight_out, preferred_element_type=jnp.float32).astype(
         jnp.bfloat16
     )
+    returned = exchange(expert_out, expert_count, capacity)
 
     hidden_grad = jnp.einsum("sd,fd->sf", rows_c, weight_out, preferred_element_type=jnp.float32)
     slope = sigmoid_gate * (1.0 + gate_pre * (1.0 - sigmoid_gate))
     gate_up_grad = jnp.concatenate(
         [hidden_grad * up_pre * slope, hidden_grad * activated], axis=1
     ).astype(jnp.bfloat16)
-    part_out = jnp.einsum("sf,sd->fd", hidden, rows_c, preferred_element_type=jnp.float32).astype(
-        jnp.bfloat16
-    )
+    pick_grad = jnp.einsum(
+        "sf,df->sd", gate_up_grad, weight_in, preferred_element_type=jnp.float32
+    ).astype(jnp.bfloat16)
+    back_grad = exchange(pick_grad, expert_count, capacity)
+    in_cols = gate_up_grad.shape[1]
+    rest = model_width - in_cols
+    part_out = jnp.einsum(
+        "sf,sd->fd", hidden, rows_c[:, :in_cols], preferred_element_type=jnp.float32
+    ).astype(jnp.bfloat16)
+    part_rest = jnp.einsum(
+        "sf,sd->fd", hidden, rows_c[:, in_cols:], preferred_element_type=jnp.float32
+    ).astype(jnp.bfloat16)
     part_in = jnp.einsum("sd,sf->df", rows_x, gate_up_grad, preferred_element_type=jnp.float32).astype(
         jnp.bfloat16
     )
     in_rows = model_width // group_count
-    in_cols = part_in.shape[1]
     out_rows = hidden_units // group_count
-    out_as = out_rows * model_width // in_cols
+    rest_as = out_rows * rest // in_cols
     joined = jnp.concatenate(
         [
             part_in.reshape(group_count, in_rows, in_cols),
-            part_out.reshape(group_count, out_as, in_cols),
+            part_out.reshape(group_count, out_rows, in_cols),
+            part_rest.reshape(group_count, rest_as, in_cols),
         ],
         axis=1,
-    ).reshape(group_count * (in_rows + out_as), in_cols)
+    ).reshape(group_count * (in_rows + out_rows + rest_as), in_cols)
+    returned, back_grad, joined = lax.optimization_barrier((returned, back_grad, joined))
     reduced = lax.psum_scatter(joined, "dp", scatter_dimension=0, tiled=True)
-    pick_grad = jnp.einsum(
-        "sf,df->sd", gate_up_grad, weight_in, preferred_element_type=jnp.float32
-    ).astype(jnp.bfloat16)
 
-    back = exchange(jnp.concatenate([expert_out, pick_grad], axis=1), expert_count, capacity)
-    returned = back[:, :model_width]
-    back_grad = back[:, model_width:]
     mixed = jnp.dot(
         weigh,
         returned.astype(jnp.float32),
@@ -116,7 +121,10 @@
     swapped = partner_2(reduced, "expert", half_bit)
     reduced = jnp.where(is_moved, swapped, reduced)
     grad_in = reduced[:in_rows]
-    grad_out = reduced[in_rows:].reshape(out_rows, model_width)
+    grad_out = jnp.concatenate(
+        [reduced[in_rows : in_rows + out_rows], reduced[in_rows + out_rows :].reshape(out_rows, rest)],
+        axis=1,
+    )
     return (mixed, x_grad, gate_grad, grad_in[None], grad_out[None])
 
 

time: 238 us -> 241 us (1.013)
  starting transfers between devices: 8.25 us -> 14.6 us
  waiting for transfers between devices: 129 us -> 123 us
  local copies, waits for them, and re-layouts: 12.3 us -> 8.12 us
  matrix products: 25.8 us -> 29.1 us
  other arithmetic: 12.1 us -> 15 us
    all_to_all x1 -> x2, waiting for transfers between devices: 120 us -> 8.45 us  [exchange(): lax.all_to_all(shaped, 'expert', split_axis=0, concat_axis=0, tiled=True)]
    reduce_scatter x1, waiting for transfers between devices: 0.02 us -> 107 us  [shards(): reduced = lax.psum_scatter(joined, 'dp', scatter_dimension=0, tiled=True)]
    all_to_all x1 -> x2, starting transfers between devices: 6.8 us -> 13.1 us  [exchange(): lax.all_to_all(shaped, 'expert', split_axis=0, concat_axis=0, tiled=True)]
    concatenate x1, other arithmetic: 3.91 us -> 8.8 us  [shards(): jnp.concatenate([part_in.reshape(group_count, in_rows, in_cols), part_out...]
    reshape x1 -> x2, local copies, waits for them, and re-layouts: 6.02 us -> 2.23 us  [the longest x1 2.2 us: shards(): part_rest.reshape(group_count, rest_as, in_cols)]
    dot_general x1 -> x2, matrix products: 2.71 us -> 5.57 us  [the longest x1 3.33 us: shards(): jnp.einsum('sf,sd->fd', hidden, rows_c[:, :in_cols], preferred_element_ty...]
  transfers between devices with their start and end apart: 3 -> 4, of which waited for: 2 -> 4; matrix products, arithmetic and copies ran while one was open for 8% -> 15% of each run, Pallas kernels for 0% -> 0%
where the time goes in v4:
time: 241 us; the launch traced here: 239 us
  waiting for transfers between devices  123 us (51%)
  blocking collectives  34 us (14%)
  matrix products  29.1 us (12%)
  other arithmetic  15 us (6%)
  between operations  14.9 us (6%)
  starting transfers between devices  14.6 us (6%)
  local copies, waits for them, and re-layouts  8.12 us (3%)
    reduce_scatter x1, waiting for transfers between devices, shards(): reduced = lax.psum_scatter(joined, 'dp', scatter_dimension=0, tiled=True)  107 us
    all_to_all x1, blocking collectives, exchange(): lax.all_to_all(shaped, 'expert', split_axis=0, concat_axis=0, tiled=True)  34 us
    all_to_all x2, starting transfers between devices, exchange(): lax.all_to_all(shaped, 'expert', split_axis=0, concat_axis=0, tiled=True)  13.1 us
    concatenate x1, other arithmetic, shards(): jnp.concatenate([part_in.reshape(group_count, in_rows, in_cols), part_out...  8.8 us
    all_to_all x2, waiting for transfers between devices, exchange(): lax.all_to_all(shaped, 'expert', split_axis=0, concat_axis=0, tiled=True)  8.45 us
    ppermute x1, waiting for transfers between devices, partner_2(): return lax.ppermute(block, axis, route)  8.01 us
  transfers between devices with their start and end apart: 4, of which 4 were waited for; matrix products, arithmetic and copies ran while one was open for 15% of the time, Pallas kernels for 0%

profile of v4, /device:TPU:24, one launch (start us, length us, event | category | flops | bytes accessed | tf_op | source)
XLA Modules:
  0.0 239.0 jit_solution(1245935728335264217)
XLA Ops:
  7.2 0.9 copy.17
  9.3 0.8 copy.18
  10.1 1.1 select_reduce_fusion
  11.2 1.6 convolution_convert_fusion.2
  12.8 1.5 fusion.9
  14.6 34.0 %all_to_all.15 = bf16[16,16,4096]{2,1,0:T(8,128)(2,1)S(1)} all-to-all(bf16[16,16,4096]{2,1,0:T(8,128)(2,1)S(1)} %bitcast.52), channel_id=1, replica_groups=mesh['expert'=16,'dp'=16] {'expert'}, dimensions={0} | all-to-all | bytes 4194304 | tf_op jit(solution)/shard_map/all_to_all | solution.py:19
  48.6 1.8 fusion.2
  50.4 1.4 multiply_convert_fusion.2
  51.8 2.8 %fusion.10 = bf16[256,2048]{1,0:T(8,128)(2,1)} fusion(bf16[1,2048,1536]{2,1,0:T(8,128)(2,1)S(1)} %bitcast.56, bf16[256,768]{1,0:T(8,128)(2,1)S(1)} %get-tuple-element.19, bf16[256,768]{1,0:T(8,128)(2,1)S(1)} %get-tuple-element.18), kind=kOutput, calls=%fused_computation.16 | convolution fusion | flops 1612709888 | bytes 8126464 | tf_op jit(solution)/shard_map/sf,df->sd/dot_general | solution.py:79
  54.6 6.5 %all-to-all-start.2 = ((bf16[16,16,2048]{2,1,0:T(8,128)(2,1)}), bf16[16,16,2048]{2,1,0:T(8,128)(2,1)}, u32[]{:S(2)}, u32[]{:S(2)}) async-start(bf16[16,16,2048]{2,1,0:T(8,128)(2,1)} %bitcast.54), calls=%async_computation.2 | async-start | bytes 2097152 | tf_op jit(solution)/shard_map/all_to_all | solution.py:19
  61.2 3.3 %convolution_convert_fusion.1 = bf16[768,1536]{1,0:T(8,128)(2,1)} fusion(bf16[256,768]{1,0:T(8,128)(2,1)S(1)} %get-tuple-element.20, bf16[256,4096]{1,0:T(8,128)(2,1)} %bitcast.48), kind=kOutput, calls=%fused_computation.8 | convolution fusion | flops 605159424 | bytes 3538944 | tf_op jit(solution)/shard_map/sf,sd->fd/dot_general | solution.py:85
  64.5 2.0 fusion.13
  66.5 4.5 %convolution_convert_fusion = bf16[2048,1536]{1,0:T(8,128)(2,1)} fusion(bf16[256,4096]{1,0:T(8,128)(2,1)S(1)} %bitcast.50, bf16[256,768]{1,0:T(8,128)(2,1)S(1)} %copy-done.12, bf16[256,768]{1,0:T(8,128)(2,1)S(1)} %copy-done.10), kind=kOutput, calls=%fused_computation.1 | convolution fusion | flops 1615331328 | bytes 8126464 | tf_op jit(solution)/shard_map/sd,sf->df/dot_general | solution.py:91
  71.0 5.9 %all-to-all-done.2 = bf16[16,16,2048]{2,1,0:T(8,128)(2,1)} async-done(((bf16[16,16,2048]{2,1,0:T(8,128)(2,1)}), bf16[16,16,2048]{2,1,0:T(8,128)(2,1)}, u32[]{:S(2)}, u32[]{:S(2)}) %all-to-all-start.2) | async-done | bytes 1048608 | tf_op jit(solution)/shard_map/all_to_all | solution.py:19
  77.0 6.6 %all-to-all-start.1 = ((bf16[16,16,2048]{2,1,0:T(8,128)(2,1)}), bf16[16,16,2048]{2,1,0:T(8,128)(2,1)}, u32[]{:S(2)}, u32[]{:S(2)}) async-start(bf16[16,16,2048]{2,1,0:T(8,128)(2,1)} %bitcast.53), calls=%async_computation.1 | async-start | bytes 2097152 | tf_op jit(solution)/shard_map/all_to_all | solution.py:19
  83.6 2.2 convolution_convert_fusion.5
  85.9 2.2 reshape.74
  88.0 8.8 %pad_maximum_fusion = bf16[16,192,1536]{2,1,0:T(8,128)(2,1)} fusion(bf16[16,16,1536]{2,1,0:T(8,128)(2,1)} %reshape.74, bf16[16,48,1536]{2,1,0:T(8,128)(2,1)} %bitcast.51, bf16[16,128,1536]{2,1,0:T(8,128)(2,1)} %bitcast.45), kind=kLoop, calls=%fused_computation | loop fusion | flops 28311552 | bytes 18874368 | tf_op jit(solution)/shard_map/concatenate | solution.py:97
  96.9 2.5 %all-to-all-done.1 = bf16[16,16,2048]{2,1,0:T(8,128)(2,1)} async-done(((bf16[16,16,2048]{2,1,0:T(8,128)(2,1)}), bf16[16,16,2048]{2,1,0:T(8,128)(2,1)}, u32[]{:S(2)}, u32[]{:S(2)}) %all-to-all-start.1) | async-done | bytes 1048608 | tf_op jit(solution)/shard_map/all_to_all | solution.py:19
  100.0 0.6 fusion.30
  101.3 2.5 %convolution_bitcast_fusion = f32[128,256]{0,1:T(8,128)} fusion(bf16[256,2048]{1,0:T(8,128)(2,1)} %bitcast.5, bf16[128,2048]{1,0:T(8,128)(2,1)} %param.8), kind=kOutput, calls=%fused_computation.25 | convolution fusion | flops 134217728 | bytes 1703936 | tf_op jit(solution)/shard_map/td,sd->ts/dot_general | solution.py:114
  103.8 1.0 copy.19
  104.8 106.7 %reduce-scatter.2.cloned.1.call-done = bf16[192,1536]{1,0:T(8,128)(2,1)} async-done(((bf16[3072,1536]{1,0:T(8,128)(2,1)}), bf16[192,1536]{1,0:T(8,128)(2,1)}) %reduce-scatter.2.cloned.1.call-update) | async-done | bytes 589840 | tf_op jit(solution)/shard_map/reduce_scatter | solution.py:106
  211.5 2.0 multiply_convert_fusion
  213.5 1.4 collective-permute-start
  214.9 1.0 select_reduce_fusion.2
  215.9 1.5 copy.20
  217.4 2.4 convolution_convert_fusion.3
  219.8 2.6 %convolution_convert_fusion.4 = bf16[128,2048]{1,0:T(8,128)(2,1)} fusion(f32[128,256]{1,0:T(8,128)S(1)} %copy-done.8, bf16[256,2048]{1,0:T(8,128)(2,1)} %bitcast.5), kind=kOutput, calls=%fused_computation.19 | convolution fusion | flops 805568512 | bytes 1703936 | tf_op jit(solution)/shard_map/dot_general | solution.py:108
  222.4 8.0 %collective-permute-done = bf16[192,1536]{1,0:T(8,128)(2,1)} collective-permute-done((bf16[192,1536]{1,0:T(8,128)(2,1)}, bf16[192,1536]{1,0:T(8,128)(2,1)}, u32[]{:S(2)}, u32[]{:S(2)}) %collective-permute-start) | collective-permute-done | bytes 589856 | tf_op jit(solution)/shard_map/ppermute | solution.py:14
  230.6 0.8 slice_bitcast_fusion
  231.5 0.7 maximum_bitcast_fusion
  (47 shorter events, 2.3 us)
Async XLA Ops:
  7.2 43.3 %copy-start = (bf16[1,768,2048]{2,1,0:T(8,128)(2,1)S(1)}, bf16[1,768,2048]{2,1,0:T(8,128)(2,1)}, u32[]{:S(2)}) copy-start(bf16[1,768,2048]{2,1,0:T(8,128)(2,1)} %param.13) | copy-start | bytes 9437188
  8.9 5.7 %copy-start.6 = (s32[128,8]{1,0:T(8,128)}, s32[128,8]{1,0:T(8,128)S(1)}, u32[]{:S(2)}) copy-start(s32[128,8]{1,0:T(8,128)S(1)} %select_n.32) | copy-start | bytes 12292
  9.3 5.3 %copy-start.4 = (bf16[128,256]{1,0:T(8,128)(2,1)}, bf16[128,256]{1,0:T(8,128)(2,1)S(1)}, u32[]{:S(2)}) copy-start(bf16[128,256]{1,0:T(8,128)(2,1)S(1)} %fusion.26) | copy-start | bytes 196612
  11.2 37.4 %slice-start = ((s8[6291456]{0:T(1024)(128)(4,1)}), s8[4194304]{0:T(1024)(128)(4,1)S(1)}, s32[]{:S(2)}) async-start(s8[6291456]{0:T(1024)(128)(4,1)} %bitcast.55), calls=%async_computation.5 | async-start | bytes 8388608
  14.3 34.3 %slice-start.1 = ((s8[6291456]{0:T(1024)(128)(4,1)}), s8[2097152]{0:T(1024)(128)(4,1)S(1)}, s32[]{:S(2)}) async-start(s8[6291456]{0:T(1024)(128)(4,1)} %bitcast.55), calls=%async_computation.6 | async-start | bytes 4194304
  48.6 1.8 copy-start.1
  51.8 2.8 %copy-start.9 = (bf16[256,768]{1,0:T(8,128)(2,1)}, bf16[256,768]{1,0:T(8,128)(2,1)S(1)}, u32[]{:S(2)}) copy-start(bf16[256,768]{1,0:T(8,128)(2,1)S(1)} %get-tuple-element.18) | copy-start | bytes 1179652
  51.8 2.8 %copy-start.11 = (bf16[256,768]{1,0:T(8,128)(2,1)}, bf16[256,768]{1,0:T(8,128)(2,1)S(1)}, u32[]{:S(2)}) copy-start(bf16[256,768]{1,0:T(8,128)(2,1)S(1)} %get-tuple-element.19) | copy-start | bytes 1179652
  54.6 22.3 %all-to-all-start.2 = ((bf16[16,16,2048]{2,1,0:T(8,128)(2,1)}), bf16[16,16,2048]{2,1,0:T(8,128)(2,1)}, u32[]{:S(2)}, u32[]{:S(2)}) async-start(bf16[16,16,2048]{2,1,0:T(8,128)(2,1)} %bitcast.54), calls=%async_computation.2 | async-start | bytes 2097152 | tf_op jit(solution)/shard_map/all_to_all | solution.py:19
  64.5 2.0 copy-start.2
  64.5 2.0 copy-start.10
  64.5 2.0 copy-start.12
  77.0 22.4 %all-to-all-start.1 = ((bf16[16,16,2048]{2,1,0:T(8,128)(2,1)}), bf16[16,16,2048]{2,1,0:T(8,128)(2,1)}, u32[]{:S(2)}, u32[]{:S(2)}) async-start(bf16[16,16,2048]{2,1,0:T(8,128)(2,1)} %bitcast.53), calls=%async_computation.1 | async-start | bytes 2097152 | tf_op jit(solution)/shard_map/all_to_all | solution.py:19
  83.6 127.9 %reduce-scatter.2.cloned.1.call-start = ((), (), s32[]{:S(2)}) async-start(), calls=%async_computation.4 | async-start | bytes 10027008 | tf_op jit(solution)/shard_map/reduce_scatter | solution.py:106
  99.4 0.7 copy-start.13
  99.4 115.5 %copy-start.7 = (s32[128,8]{1,0:T(8,128)S(1)}, s32[128,8]{1,0:T(8,128)}, u32[]{:S(2)}) copy-start(s32[128,8]{1,0:T(8,128)} %copy-done.6) | copy-start | bytes 12292
  99.4 118.0 %copy-start.5 = (bf16[128,256]{1,0:T(8,128)(2,1)S(1)}, bf16[128,256]{1,0:T(8,128)(2,1)}, u32[]{:S(2)}) copy-start(bf16[128,256]{1,0:T(8,128)(2,1)} %copy-done.4) | copy-start | bytes 196612
  101.3 118.5 %copy-start.8 = (f32[128,256]{1,0:T(8,128)S(1)}, f32[128,256]{1,0:T(8,128)}, u32[]{:S(2)}) copy-start(f32[128,256]{1,0:T(8,128)} %get-tuple-element.17) | copy-start | bytes 393220
  213.5 16.9 %collective-permute-start = (bf16[192,1536]{1,0:T(8,128)(2,1)}, bf16[192,1536]{1,0:T(8,128)(2,1)}, u32[]{:S(2)}, u32[]{:S(2)}) collective-permute-start(bf16[192,1536]{1,0:T(8,128)(2,1)} %multiply_convert_fusion), channel_id=1, source_target_pairs={{0,128},{128,0},{16,144},{144,16},{32,160},{160,32},{48,176},{176,... | collective-permute-start | bytes 1769480 | tf_op jit(solution)/shard_map/ppermute | solution.py:14
  217.4 13.0 %copy-start.3 = (bf16[192,1536]{1,0:T(8,128)(2,1)S(1)}, bf16[192,1536]{1,0:T(8,128)(2,1)}, u32[]{:S(2)}) copy-start(bf16[192,1536]{1,0:T(8,128)(2,1)} %reduce-scatter.2.cloned.1.call-done) | copy-start | bytes 1769476
Sparse Core Ops, SparseCore 0:
  99.5 111.9 reduce-scatter.1

commit v5 on v4

--- a/solution.py
+++ b/solution.py
@@ -79,31 +79,27 @@
     pick_grad = jnp.einsum(
         "sf,df->sd", gate_up_grad, weight_in, preferred_element_type=jnp.float32
     ).astype(jnp.bfloat16)
-    back_grad = exchange(pick_grad, expert_count, capacity)
     in_cols = gate_up_grad.shape[1]
     rest = model_width - in_cols
-    part_out = jnp.einsum(
-        "sf,sd->fd", hidden, rows_c[:, :in_cols], preferred_element_type=jnp.float32
-    ).astype(jnp.bfloat16)
-    part_rest = jnp.einsum(
-        "sf,sd->fd", hidden, rows_c[:, in_cols:], preferred_element_type=jnp.float32
-    ).astype(jnp.bfloat16)
-    part_in = jnp.einsum("sd,sf->df", rows_x, gate_up_grad, preferred_element_type=jnp.float32).astype(
-        jnp.bfloat16
-    )
     in_rows = model_width // group_count
     out_rows = hidden_units // group_count
-    rest_as = out_rows * rest // in_cols
+    rest_rows = out_rows // (in_cols // rest)
+    scale = 1.0 / group_count
+    part_out = (
+        jnp.einsum("sf,sd->fd", hidden, rows_c, preferred_element_type=jnp.float32) * scale
+    ).astype(jnp.bfloat16).reshape(group_count, out_rows, model_width)
+    part_in = (
+        jnp.einsum("sd,sf->df", rows_x, gate_up_grad, preferred_element_type=jnp.float32) * scale
+    ).astype(jnp.bfloat16).reshape(group_count, in_rows, in_cols)
+    tail = part_out[:, :, in_cols:]
+    bands = [tail[:, k * rest_rows : (k + 1) * rest_rows] for k in range(in_cols // rest)]
     joined = jnp.concatenate(
-        [
-            part_in.reshape(group_count, in_rows, in_cols),
-            part_out.reshape(group_count, out_rows, in_cols),
-            part_rest.reshape(group_count, rest_as, in_cols),
-        ],
-        axis=1,
-    ).reshape(group_count * (in_rows + out_rows + rest_as), in_cols)
-    returned, back_grad, joined = lax.optimization_barrier((returned, back_grad, joined))
+        [part_in, part_out[:, :, :in_cols], jnp.concatenate(bands, axis=2)], axis=1
+    ).reshape(group_count * (in_rows + out_rows + rest_rows), in_cols)
+    returned, joined = lax.optimization_barrier((returned, joined))
     reduced = lax.psum_scatter(joined, "dp", scatter_dimension=0, tiled=True)
+    reduced, pick_grad = lax.optimization_barrier((reduced, pick_grad))
+    back_grad = exchange(pick_grad, expert_count, capacity)
 
     mixed = jnp.dot(
         weigh,
@@ -117,12 +113,13 @@
         jnp.bfloat16
     )
 
-    reduced = (reduced.astype(jnp.float32) / group_count).astype(jnp.bfloat16)
     swapped = partner_2(reduced, "expert", half_bit)
     reduced = jnp.where(is_moved, swapped, reduced)
     grad_in = reduced[:in_rows]
+    tail = reduced[in_rows + out_rows :]
     grad_out = jnp.concatenate(
-        [reduced[in_rows : in_rows + out_rows], reduced[in_rows + out_rows :].reshape(out_rows, rest)],
+        [reduced[in_rows : in_rows + out_rows],
+         jnp.concatenate([tail[:, k * rest : (k + 1) * rest] for k in range(in_cols // rest)], axis=0)],
         axis=1,
     )
     return (mixed, x_grad, gate_grad, grad_in[None], grad_out[None])

time: 241 us -> 238 us (0.988)
  waiting for transfers between devices: 123 us -> 120 us
    ppermute x1, waiting for transfers between devices: 8.01 us -> 0.31 us  [partner_2(): return lax.ppermute(block, axis, route)]
    all_to_all x2, waiting for transfers between devices: 8.45 us -> 15.6 us  [exchange(): lax.all_to_all(shaped, 'expert', split_axis=0, concat_axis=0, tiled=True)]
    dot_general x2 -> x1, matrix products: 5.57 us -> 1.01 us  [shards(): jnp.einsum('sf,sd->fd', hidden, rows_c, preferred_element_type=jnp.float32)]
    dot_general x1, matrix products: 2.8 us -> 5.88 us  [shards(): jnp.einsum('sf,df->sd', gate_up_grad, weight_in, preferred_element_type=j...]
    slice x1 -> x3, local copies, waits for them, and re-layouts: 0.01 us -> 2.5 us  [the longest x1 1.63 us: shards(): part_out[:, :, :in_cols]]
  transfers between devices with their start and end apart: 4 -> 4, of which waited for: 4 -> 4; matrix products, arithmetic and copies ran while one was open for 15% -> 13% of each run, Pallas kernels for 0% -> 0%
where the time goes in v5:
time: 238 us; the launch traced here: 234 us
  waiting for transfers between devices  120 us (50%)
  blocking collectives  34 us (14%)
  matrix products  27.3 us (11%)
  between operations  14.9 us (6%)
  other arithmetic  14.7 us (6%)
  starting transfers between devices  14.6 us (6%)
  local copies, waits for them, and re-layouts  8.35 us (4%)
    reduce_scatter x1, waiting for transfers between devices, shards(): reduced = lax.psum_scatter(joined, 'dp', scatter_dimension=0, tiled=True)  104 us
    all_to_all x1, blocking collectives, exchange(): lax.all_to_all(shaped, 'expert', split_axis=0, concat_axis=0, tiled=True)  34 us
    all_to_all x2, waiting for transfers between devices, exchange(): lax.all_to_all(shaped, 'expert', split_axis=0, concat_axis=0, tiled=True)  15.6 us
    all_to_all x2, starting transfers between devices, exchange(): lax.all_to_all(shaped, 'expert', split_axis=0, concat_axis=0, tiled=True)  13.2 us
    concatenate x1, other arithmetic, shards(): jnp.concatenate([part_in, part_out[:, :, :in_cols], jnp.concatenate(bands...  9.54 us
    dot_general x1, matrix products, shards(): jnp.einsum('sf,df->sd', gate_up_grad, weight_in, preferred_element_type=j...  5.88 us
  transfers between devices with their start and end apart: 4, of which 4 were waited for; matrix products, arithmetic and copies ran while one was open for 13% of the time, Pallas kernels for 0%

profile of v5, /device:TPU:24, one launch (start us, length us, event | category | flops | bytes accessed | tf_op | source)
XLA Modules:
  0.0 234.2 jit_solution(1077427665186658694)
XLA Ops:
  7.2 0.9 copy.17
  9.3 0.8 copy.18
  10.1 1.1 select_reduce_fusion
  11.1 1.6 convolution_convert_fusion
  12.8 1.5 fusion.9
  14.5 34.0 %all_to_all.15 = bf16[16,16,4096]{2,1,0:T(8,128)(2,1)S(1)} all-to-all(bf16[16,16,4096]{2,1,0:T(8,128)(2,1)S(1)} %bitcast.44), channel_id=1, replica_groups=mesh['expert'=16,'dp'=16] {'expert'}, dimensions={0} | all-to-all | bytes 4194304 | tf_op jit(solution)/shard_map/all_to_all | solution.py:19
  48.5 1.8 fusion.2
  50.4 2.3 multiply_convert_fusion.3
  52.6 1.0 multiply_convert_fusion.1
  53.6 0.9 fusion.32
  54.5 1.6 slice.64
  56.1 2.0 fusion.13
  58.1 6.5 %all-to-all-start.1 = ((bf16[16,16,2048]{2,1,0:T(8,128)(2,1)}), bf16[16,16,2048]{2,1,0:T(8,128)(2,1)}, u32[]{:S(2)}, u32[]{:S(2)}) async-start(bf16[16,16,2048]{2,1,0:T(8,128)(2,1)} %bitcast.53), calls=%async_computation.1 | async-start | bytes 2097152 | tf_op jit(solution)/shard_map/all_to_all | solution.py:19
  64.7 3.4 %multiply_convert_fusion = bf16[2048,1536]{1,0:T(8,128)(2,1)S(1)} fusion(bf16[256,4096]{1,0:T(8,128)(2,1)} %bitcast.51, bf16[256,768]{1,0:T(8,128)(2,1)} %get-tuple-element.24, bf16[256,768]{1,0:T(8,128)(2,1)} %get-tuple-element.23), kind=kOutput, calls=%fused_computation | convolution fusion | flops 1618477056 | bytes 8126464 | tf_op jit(solution)/shard_map/sd,sf->df/dot_general | solution.py:92
  68.2 9.5 %maximum_maximum_fusion = bf16[16,192,1536]{2,1,0:T(8,128)(2,1)} fusion(bf16[16,16,512]{2,1,0:T(8,128)(2,1)S(1)} %copy-done.3, bf16[16,16,512]{2,1,0:T(8,128)(2,1)S(1)} %copy-done.4, bf16[16,16,512]{2,1,0:T(8,128)(2,1)S(1)} %get-tuple-element.20, bf16[16,48,1536]{2,1,0:T(8,128)(2,1)S(1)} %copy-done.1, bf16[16,128,1536]{2,1,0:T(8,128)(2,1)S(1)} %bitcast.45), kind=kLoop, calls=%fused_computation.1 | loop fusion | flops 47185920 | bytes 18874368 | tf_op jit(solution)/shard_map/concatenate | solution.py:96
  77.7 2.7 %all-to-all-done.1 = bf16[16,16,2048]{2,1,0:T(8,128)(2,1)} async-done(((bf16[16,16,2048]{2,1,0:T(8,128)(2,1)}), bf16[16,16,2048]{2,1,0:T(8,128)(2,1)}, u32[]{:S(2)}, u32[]{:S(2)}) %all-to-all-start.1) | async-done | bytes 1048608 | tf_op jit(solution)/shard_map/all_to_all | solution.py:19
  80.4 0.6 copy-done.6
  81.1 0.6 fusion.29
  82.4 5.9 %fusion.10 = bf16[256,2048]{1,0:T(8,128)(2,1)} fusion(bf16[1,2048,1536]{2,1,0:T(8,128)(2,1)} %param.12, bf16[256,768]{1,0:T(8,128)(2,1)} %get-tuple-element.24, bf16[256,768]{1,0:T(8,128)(2,1)} %get-tuple-element.23), kind=kOutput, calls=%fused_computation.16 | convolution fusion | flops 1612709888 | bytes 8126464 | tf_op jit(solution)/shard_map/sf,df->sd/dot_general | solution.py:79
  88.2 104.3 %reduce-scatter.2.cloned.1.call-done = bf16[192,1536]{1,0:T(8,128)(2,1)} async-done(((bf16[3072,1536]{1,0:T(8,128)(2,1)}), bf16[192,1536]{1,0:T(8,128)(2,1)}) %reduce-scatter.2.cloned.1.call-update) | async-done | bytes 589840 | tf_op jit(solution)/shard_map/reduce_scatter | solution.py:100
  192.6 1.4 collective-permute-start
  194.0 2.4 %convolution_bitcast_fusion = f32[128,256]{0,1:T(8,128)} fusion(bf16[256,2048]{1,0:T(8,128)(2,1)} %bitcast.5, bf16[128,2048]{1,0:T(8,128)(2,1)} %param.8), kind=kOutput, calls=%fused_computation.23 | convolution fusion | flops 134217728 | bytes 1703936 | tf_op jit(solution)/shard_map/td,sd->ts/dot_general | solution.py:110
  196.4 1.0 copy.19
  197.4 1.0 select_reduce_fusion.2
  198.4 1.5 copy.20
  199.9 2.6 %convolution_convert_fusion.2 = bf16[128,2048]{1,0:T(8,128)(2,1)} fusion(f32[128,256]{1,0:T(8,128)S(1)} %copy-done.5, bf16[256,2048]{1,0:T(8,128)(2,1)} %bitcast.5), kind=kOutput, calls=%fused_computation.19 | convolution fusion | flops 805568512 | bytes 1703936 | tf_op jit(solution)/shard_map/dot_general | solution.py:104
  202.5 6.6 %all-to-all-start.2 = ((bf16[16,16,2048]{2,1,0:T(8,128)(2,1)}), bf16[16,16,2048]{2,1,0:T(8,128)(2,1)}, u32[]{:S(2)}, u32[]{:S(2)}) async-start(bf16[16,16,2048]{2,1,0:T(8,128)(2,1)} %bitcast.52), calls=%async_computation.3 | async-start | bytes 2097152 | tf_op jit(solution)/shard_map/all_to_all | solution.py:19
  209.5 1.1 broadcast_select_fusion
  210.7 0.7 maximum_bitcast_fusion
  211.4 0.8 slice_bitcast_fusion
  212.1 12.9 %all-to-all-done.2 = bf16[16,16,2048]{2,1,0:T(8,128)(2,1)} async-done(((bf16[16,16,2048]{2,1,0:T(8,128)(2,1)}), bf16[16,16,2048]{2,1,0:T(8,128)(2,1)}, u32[]{:S(2)}, u32[]{:S(2)}) %all-to-all-start.2) | async-done | bytes 1048608 | tf_op jit(solution)/shard_map/all_to_all | solution.py:19
  225.0 2.3 convolution_convert_fusion.1
  (31 shorter events, 1.8 us)
Async XLA Ops:
  7.2 43.2 %copy-start = (bf16[1,768,2048]{2,1,0:T(8,128)(2,1)S(1)}, bf16[1,768,2048]{2,1,0:T(8,128)(2,1)}, u32[]{:S(2)}) copy-start(bf16[1,768,2048]{2,1,0:T(8,128)(2,1)} %param.13) | copy-start | bytes 9437188
  11.1 37.4 %slice-start = ((s8[6291456]{0:T(1024)(128)(4,1)}), s8[4194304]{0:T(1024)(128)(4,1)S(1)}, s32[]{:S(2)}) async-start(s8[6291456]{0:T(1024)(128)(4,1)} %bitcast.54), calls=%async_computation.5 | async-start | bytes 8388608
  14.3 34.3 %slice-start.1 = ((s8[6291456]{0:T(1024)(128)(4,1)}), s8[2097152]{0:T(1024)(128)(4,1)S(1)}, s32[]{:S(2)}) async-start(s8[6291456]{0:T(1024)(128)(4,1)} %bitcast.54), calls=%async_computation.6 | async-start | bytes 4194304
  48.5 4.1 %copy-start.2 = (bf16[16,16,4096]{2,1,0:T(8,128)(2,1)}, bf16[16,16,4096]{2,1,0:T(8,128)(2,1)S(1)}, u32[]{:S(2)}) copy-start(bf16[16,16,4096]{2,1,0:T(8,128)(2,1)S(1)} %all_to_all.15) | copy-start | bytes 6291460
  58.1 22.3 %all-to-all-start.1 = ((bf16[16,16,2048]{2,1,0:T(8,128)(2,1)}), bf16[16,16,2048]{2,1,0:T(8,128)(2,1)}, u32[]{:S(2)}, u32[]{:S(2)}) async-start(bf16[16,16,2048]{2,1,0:T(8,128)(2,1)} %bitcast.53), calls=%async_computation.1 | async-start | bytes 2097152 | tf_op jit(solution)/shard_map/all_to_all | solution.py:19
  64.6 127.9 %reduce-scatter.2.cloned.1.call-start = ((), (), s32[]{:S(2)}) async-start(), calls=%async_computation.4 | async-start | bytes 10027008 | tf_op jit(solution)/shard_map/reduce_scatter | solution.py:100
  64.7 3.5 %copy-start.1 = (bf16[16,48,1536]{2,1,0:T(8,128)(2,1)S(1)}, bf16[16,48,1536]{2,1,0:T(8,128)(2,1)}, u32[]{:S(2)}) copy-start(bf16[16,48,1536]{2,1,0:T(8,128)(2,1)} %slice.64) | copy-start | bytes 7077892
  64.7 3.5 %copy-start.3 = (bf16[16,16,512]{2,1,0:T(8,128)(2,1)S(1)}, bf16[16,16,512]{2,1,0:T(8,128)(2,1)}, u32[]{:S(2)}) copy-start(bf16[16,16,512]{2,1,0:T(8,128)(2,1)} %get-tuple-element.21) | copy-start | bytes 786436
  64.7 3.5 %copy-start.4 = (bf16[16,16,512]{2,1,0:T(8,128)(2,1)S(1)}, bf16[16,16,512]{2,1,0:T(8,128)(2,1)}, u32[]{:S(2)}) copy-start(bf16[16,16,512]{2,1,0:T(8,128)(2,1)} %get-tuple-element.22) | copy-start | bytes 786436
  80.4 0.7 copy-start.6
  82.4 117.6 %copy-start.5 = (f32[128,256]{1,0:T(8,128)S(1)}, f32[128,256]{1,0:T(8,128)}, u32[]{:S(2)}) copy-start(f32[128,256]{1,0:T(8,128)} %get-tuple-element.19) | copy-start | bytes 393220
  192.6 16.9 %collective-permute-start = (bf16[192,1536]{1,0:T(8,128)(2,1)}, bf16[192,1536]{1,0:T(8,128)(2,1)}, u32[]{:S(2)}, u32[]{:S(2)}) collective-permute-start(bf16[192,1536]{1,0:T(8,128)(2,1)} %reduce-scatter.2.cloned.1.call-done), channel_id=1, source_target_pairs={{0,128},{128,0},{16,144},{144,16},{32,160},{160,32},{48,176},{176,... | collective-permute-start | bytes 1769480 | tf_op jit(solution)/shard_map/ppermute | solution.py:14
  202.5 22.4 %all-to-all-start.2 = ((bf16[16,16,2048]{2,1,0:T(8,128)(2,1)}), bf16[16,16,2048]{2,1,0:T(8,128)(2,1)}, u32[]{:S(2)}, u32[]{:S(2)}) async-start(bf16[16,16,2048]{2,1,0:T(8,128)(2,1)} %bitcast.52), calls=%async_computation.3 | async-start | bytes 2097152 | tf_op jit(solution)/shard_map/all_to_all | solution.py:19
Sparse Core Ops, SparseCore 0:
  80.6 111.9 reduce-scatter.1

commit v6 on v5

--- a/solution.py
+++ b/solution.py
@@ -14,9 +14,30 @@
     return lax.ppermute(block, axis, route)
 
 
+def pair_groups(expert_count, group_count):
+    half = group_count // 2
+    groups = []
+    for flip in range(2):
+        for z in range(half):
+            members = []
+            for e in range(expert_count):
+                x_lo = flip ^ ((e >> 1) & 1)
+                members.append(e * group_count + x_lo * half + z)
+            groups.append(members)
+    return groups
+
+
 def exchange(block, expert_count, capacity):
+    group_count = lax.axis_size("dp")
     shaped = block.reshape(expert_count, capacity, block.shape[-1])
-    arrived = lax.all_to_all(shaped, "expert", split_axis=0, concat_axis=0, tiled=True)
+    arrived = lax.all_to_all(
+        shaped,
+        ("expert", "dp"),
+        split_axis=0,
+        concat_axis=0,
+        tiled=True,
+        axis_index_groups=pair_groups(expert_count, group_count),
+    )
     return arrived.reshape(expert_count * capacity, block.shape[-1])
 
 

time: 238 us -> 236 us (level)
  no operation moved by 1% of the time
where the time goes in v6:
time: 236 us; the launch traced here: 233 us
  waiting for transfers between devices  120 us (51%)
  blocking collectives  33.5 us (14%)
  matrix products  27.4 us (12%)
  between operations  14.9 us (6%)
  other arithmetic  14.7 us (6%)
  starting transfers between devices  14.2 us (6%)
  local copies, waits for them, and re-layouts  8.35 us (4%)
    reduce_scatter x1, waiting for transfers between devices, shards(): reduced = lax.psum_scatter(joined, 'dp', scatter_dimension=0, tiled=True)  104 us
    all_to_all x1, blocking collectives, exchange(): lax.all_to_all(shaped, ('expert', 'dp'), split_axis=0, concat_axis=0, til...  33.5 us
    all_to_all x2, waiting for transfers between devices, exchange(): lax.all_to_all(shaped, ('expert', 'dp'), split_axis=0, concat_axis=0, til...  14.6 us
    all_to_all x2, starting transfers between devices, exchange(): lax.all_to_all(shaped, ('expert', 'dp'), split_axis=0, concat_axis=0, til...  12.8 us
    concatenate x1, other arithmetic, shards(): jnp.concatenate([part_in, part_out[:, :, :in_cols], jnp.concatenate(bands...  9.54 us
    dot_general x1, matrix products, shards(): jnp.einsum('sf,df->sd', gate_up_grad, weight_in, preferred_element_type=j...  5.88 us
  transfers between devices with their start and end apart: 4, of which 4 were waited for; matrix products, arithmetic and copies ran while one was open for 13% of the time, Pallas kernels for 0%

profile of v6, /device:TPU:24, one launch (start us, length us, event | category | flops | bytes accessed | tf_op | source)
XLA Modules:
  0.0 232.6 jit_solution(484006447716463895)
XLA Ops:
  7.2 0.9 copy.17
  9.3 0.8 copy.18
  10.1 1.1 select_reduce_fusion
  11.1 1.6 convolution_convert_fusion
  12.8 1.5 fusion.9
  14.5 33.5 %all_to_all.15 = bf16[16,16,4096]{2,1,0:T(8,128)(2,1)S(1)} all-to-all(bf16[16,16,4096]{2,1,0:T(8,128)(2,1)S(1)} %bitcast.44), channel_id=1, replica_groups={{0,16,40,56,64,80,104,120,128,144,168,184,192,208,232,248},{1,17,41,57,..., dimensions={0} | all-to-all | bytes 4194304 | tf_op jit(solution)/shard_map/all_to_all | solution.py:33
  48.0 1.8 fusion.2
  49.8 2.3 multiply_convert_fusion.3
  52.1 1.0 multiply_convert_fusion.1
  53.1 0.9 fusion.32
  53.9 1.6 slice.64
  55.6 2.0 fusion.13
  57.6 6.5 %all-to-all-start.1 = ((bf16[16,16,2048]{2,1,0:T(8,128)(2,1)}), bf16[16,16,2048]{2,1,0:T(8,128)(2,1)}, u32[]{:S(2)}, u32[]{:S(2)}) async-start(bf16[16,16,2048]{2,1,0:T(8,128)(2,1)} %bitcast.53), calls=%async_computation.1 | async-start | bytes 2097152 | tf_op jit(solution)/shard_map/all_to_all | solution.py:33
  64.1 3.4 %multiply_convert_fusion = bf16[2048,1536]{1,0:T(8,128)(2,1)S(1)} fusion(bf16[256,4096]{1,0:T(8,128)(2,1)} %bitcast.51, bf16[256,768]{1,0:T(8,128)(2,1)} %get-tuple-element.24, bf16[256,768]{1,0:T(8,128)(2,1)} %get-tuple-element.23), kind=kOutput, calls=%fused_computation | convolution fusion | flops 1618477056 | bytes 8126464 | tf_op jit(solution)/shard_map/sd,sf->df/dot_general | solution.py:113
  67.6 9.5 %maximum_maximum_fusion = bf16[16,192,1536]{2,1,0:T(8,128)(2,1)} fusion(bf16[16,16,512]{2,1,0:T(8,128)(2,1)S(1)} %copy-done.3, bf16[16,16,512]{2,1,0:T(8,128)(2,1)S(1)} %copy-done.4, bf16[16,16,512]{2,1,0:T(8,128)(2,1)S(1)} %get-tuple-element.20, bf16[16,48,1536]{2,1,0:T(8,128)(2,1)S(1)} %copy-done.1, bf16[16,128,1536]{2,1,0:T(8,128)(2,1)S(1)} %bitcast.45), kind=kLoop, calls=%fused_computation.1 | loop fusion | flops 47185920 | bytes 18874368 | tf_op jit(solution)/shard_map/concatenate | solution.py:117
  77.1 2.4 %all-to-all-done.1 = bf16[16,16,2048]{2,1,0:T(8,128)(2,1)} async-done(((bf16[16,16,2048]{2,1,0:T(8,128)(2,1)}), bf16[16,16,2048]{2,1,0:T(8,128)(2,1)}, u32[]{:S(2)}, u32[]{:S(2)}) %all-to-all-start.1) | async-done | bytes 1048608 | tf_op jit(solution)/shard_map/all_to_all | solution.py:33
  80.2 0.6 fusion.29
  81.5 5.9 %fusion.10 = bf16[256,2048]{1,0:T(8,128)(2,1)} fusion(bf16[1,2048,1536]{2,1,0:T(8,128)(2,1)} %param.12, bf16[256,768]{1,0:T(8,128)(2,1)} %get-tuple-element.24, bf16[256,768]{1,0:T(8,128)(2,1)} %get-tuple-element.23), kind=kOutput, calls=%fused_computation.16 | convolution fusion | flops 1612709888 | bytes 8126464 | tf_op jit(solution)/shard_map/sf,df->sd/dot_general | solution.py:100
  87.4 104.3 %reduce-scatter.2.cloned.1.call-done = bf16[192,1536]{1,0:T(8,128)(2,1)} async-done(((bf16[3072,1536]{1,0:T(8,128)(2,1)}), bf16[192,1536]{1,0:T(8,128)(2,1)}) %reduce-scatter.2.cloned.1.call-update) | async-done | bytes 589840 | tf_op jit(solution)/shard_map/reduce_scatter | solution.py:121
  191.7 1.4 collective-permute-start
  193.1 2.4 %convolution_bitcast_fusion = f32[128,256]{0,1:T(8,128)} fusion(bf16[256,2048]{1,0:T(8,128)(2,1)} %bitcast.5, bf16[128,2048]{1,0:T(8,128)(2,1)} %param.8), kind=kOutput, calls=%fused_computation.23 | convolution fusion | flops 134217728 | bytes 1703936 | tf_op jit(solution)/shard_map/td,sd->ts/dot_general | solution.py:131
  195.6 1.0 copy.19
  196.6 1.0 select_reduce_fusion.2
  197.6 1.5 copy.20
  199.1 2.6 %convolution_convert_fusion.2 = bf16[128,2048]{1,0:T(8,128)(2,1)} fusion(f32[128,256]{1,0:T(8,128)S(1)} %copy-done.5, bf16[256,2048]{1,0:T(8,128)(2,1)} %bitcast.5), kind=kOutput, calls=%fused_computation.19 | convolution fusion | flops 805568512 | bytes 1703936 | tf_op jit(solution)/shard_map/dot_general | solution.py:125
  201.7 6.2 %all-to-all-start.2 = ((bf16[16,16,2048]{2,1,0:T(8,128)(2,1)}), bf16[16,16,2048]{2,1,0:T(8,128)(2,1)}, u32[]{:S(2)}, u32[]{:S(2)}) async-start(bf16[16,16,2048]{2,1,0:T(8,128)(2,1)} %bitcast.52), calls=%async_computation.3 | async-start | bytes 2097152 | tf_op jit(solution)/shard_map/all_to_all | solution.py:33
  207.9 0.7 collective-permute-done
  208.7 1.1 broadcast_select_fusion
  209.8 0.7 maximum_bitcast_fusion
  210.5 0.8 slice_bitcast_fusion
  211.3 12.1 %all-to-all-done.2 = bf16[16,16,2048]{2,1,0:T(8,128)(2,1)} async-done(((bf16[16,16,2048]{2,1,0:T(8,128)(2,1)}), bf16[16,16,2048]{2,1,0:T(8,128)(2,1)}, u32[]{:S(2)}, u32[]{:S(2)}) %all-to-all-start.2) | async-done | bytes 1048608 | tf_op jit(solution)/shard_map/all_to_all | solution.py:33
  223.4 2.3 %convolution_convert_fusion.1 = bf16[128,2048]{1,0:T(8,128)(2,1)} fusion(bf16[128,256]{1,0:T(8,128)(2,1)S(1)} %fusion.26, bf16[256,2048]{1,0:T(8,128)(2,1)} %bitcast.10), kind=kOutput, calls=%fused_computation.18 | convolution fusion | flops 134479872 | bytes 1638400 | tf_op jit(solution)/shard_map/ts,sd->td/dot_general | solution.py:133
  (31 shorter events, 2.1 us)
Async XLA Ops:
  7.2 42.6 %copy-start = (bf16[1,768,2048]{2,1,0:T(8,128)(2,1)S(1)}, bf16[1,768,2048]{2,1,0:T(8,128)(2,1)}, u32[]{:S(2)}) copy-start(bf16[1,768,2048]{2,1,0:T(8,128)(2,1)} %param.13) | copy-start | bytes 9437188
  11.1 36.8 %slice-start = ((s8[6291456]{0:T(1024)(128)(4,1)}), s8[4194304]{0:T(1024)(128)(4,1)S(1)}, s32[]{:S(2)}) async-start(s8[6291456]{0:T(1024)(128)(4,1)} %bitcast.54), calls=%async_computation.5 | async-start | bytes 8388608
  14.3 33.7 %slice-start.1 = ((s8[6291456]{0:T(1024)(128)(4,1)}), s8[2097152]{0:T(1024)(128)(4,1)S(1)}, s32[]{:S(2)}) async-start(s8[6291456]{0:T(1024)(128)(4,1)} %bitcast.54), calls=%async_computation.6 | async-start | bytes 4194304
  48.0 4.1 %copy-start.2 = (bf16[16,16,4096]{2,1,0:T(8,128)(2,1)}, bf16[16,16,4096]{2,1,0:T(8,128)(2,1)S(1)}, u32[]{:S(2)}) copy-start(bf16[16,16,4096]{2,1,0:T(8,128)(2,1)S(1)} %all_to_all.15) | copy-start | bytes 6291460
  57.6 22.0 %all-to-all-start.1 = ((bf16[16,16,2048]{2,1,0:T(8,128)(2,1)}), bf16[16,16,2048]{2,1,0:T(8,128)(2,1)}, u32[]{:S(2)}, u32[]{:S(2)}) async-start(bf16[16,16,2048]{2,1,0:T(8,128)(2,1)} %bitcast.53), calls=%async_computation.1 | async-start | bytes 2097152 | tf_op jit(solution)/shard_map/all_to_all | solution.py:33
  64.1 127.7 %reduce-scatter.2.cloned.1.call-start = ((), (), s32[]{:S(2)}) async-start(), calls=%async_computation.4 | async-start | bytes 10027008 | tf_op jit(solution)/shard_map/reduce_scatter | solution.py:121
  64.1 3.5 %copy-start.1 = (bf16[16,48,1536]{2,1,0:T(8,128)(2,1)S(1)}, bf16[16,48,1536]{2,1,0:T(8,128)(2,1)}, u32[]{:S(2)}) copy-start(bf16[16,48,1536]{2,1,0:T(8,128)(2,1)} %slice.64) | copy-start | bytes 7077892
  64.1 3.5 %copy-start.3 = (bf16[16,16,512]{2,1,0:T(8,128)(2,1)S(1)}, bf16[16,16,512]{2,1,0:T(8,128)(2,1)}, u32[]{:S(2)}) copy-start(bf16[16,16,512]{2,1,0:T(8,128)(2,1)} %get-tuple-element.21) | copy-start | bytes 786436
  64.1 3.5 %copy-start.4 = (bf16[16,16,512]{2,1,0:T(8,128)(2,1)S(1)}, bf16[16,16,512]{2,1,0:T(8,128)(2,1)}, u32[]{:S(2)}) copy-start(bf16[16,16,512]{2,1,0:T(8,128)(2,1)} %get-tuple-element.22) | copy-start | bytes 786436
  79.6 0.7 copy-start.6
  81.5 117.6 %copy-start.5 = (f32[128,256]{1,0:T(8,128)S(1)}, f32[128,256]{1,0:T(8,128)}, u32[]{:S(2)}) copy-start(f32[128,256]{1,0:T(8,128)} %get-tuple-element.19) | copy-start | bytes 393220
  191.7 16.9 %collective-permute-start = (bf16[192,1536]{1,0:T(8,128)(2,1)}, bf16[192,1536]{1,0:T(8,128)(2,1)}, u32[]{:S(2)}, u32[]{:S(2)}) collective-permute-start(bf16[192,1536]{1,0:T(8,128)(2,1)} %reduce-scatter.2.cloned.1.call-done), channel_id=1, source_target_pairs={{0,128},{128,0},{16,144},{144,16},{32,160},{160,32},{48,176},{176,... | collective-permute-start | bytes 1769480 | tf_op jit(solution)/shard_map/ppermute | solution.py:14
  201.7 21.7 %all-to-all-start.2 = ((bf16[16,16,2048]{2,1,0:T(8,128)(2,1)}), bf16[16,16,2048]{2,1,0:T(8,128)(2,1)}, u32[]{:S(2)}, u32[]{:S(2)}) async-start(bf16[16,16,2048]{2,1,0:T(8,128)(2,1)} %bitcast.52), calls=%async_computation.3 | async-start | bytes 2097152 | tf_op jit(solution)/shard_map/all_to_all | solution.py:33
Sparse Core Ops, SparseCore 0:
  79.7 111.9 reduce-scatter.1

commit v7 on v6

--- a/solution.py
+++ b/solution.py
@@ -117,9 +117,7 @@
     joined = jnp.concatenate(
         [part_in, part_out[:, :, :in_cols], jnp.concatenate(bands, axis=2)], axis=1
     ).reshape(group_count * (in_rows + out_rows + rest_rows), in_cols)
-    returned, joined = lax.optimization_barrier((returned, joined))
     reduced = lax.psum_scatter(joined, "dp", scatter_dimension=0, tiled=True)
-    reduced, pick_grad = lax.optimization_barrier((reduced, pick_grad))
     back_grad = exchange(pick_grad, expert_count, capacity)
 
     mixed = jnp.dot(

time: 236 us -> 202 us (0.86); the launches traced: 233 us -> 202 us
  waiting for transfers between devices: 120 us -> 92.8 us
  local copies, waits for them, and re-layouts: 8.35 us -> 5.52 us
    reduce_scatter x1, waiting for transfers between devices: 104 us -> 75.5 us  [shards(): reduced = lax.psum_scatter(joined, 'dp', scatter_dimension=0, tiled=True)]
    ppermute x1, waiting for transfers between devices: 0.73 us -> 8.02 us  [partner_2(): return lax.ppermute(block, axis, route)]
    all_to_all x2, waiting for transfers between devices: 14.6 us -> 9.21 us  [exchange(): lax.all_to_all(shaped, ('expert', 'dp'), split_axis=0, concat_axis=0, til...]
  transfers between devices with their start and end apart: 4 -> 4, of which waited for: 4 -> 3; matrix products, arithmetic and copies ran while one was open for 13% -> 10% of each run, Pallas kernels for 0% -> 0%
where the time goes in v7:
time: 202 us
  waiting for transfers between devices  92.8 us (46%)
  blocking collectives  33.5 us (17%)
  matrix products  26.2 us (13%)
  between operations  14.9 us (7%)
  starting transfers between devices  14.7 us (7%)
  other arithmetic  14.1 us (7%)
  local copies, waits for them, and re-layouts  5.52 us (3%)
    reduce_scatter x1, waiting for transfers between devices, shards(): reduced = lax.psum_scatter(joined, 'dp', scatter_dimension=0, tiled=True)  75.5 us
    all_to_all x1, blocking collectives, exchange(): lax.all_to_all(shaped, ('expert', 'dp'), split_axis=0, concat_axis=0, til...  33.5 us
    all_to_all x2, starting transfers between devices, exchange(): lax.all_to_all(shaped, ('expert', 'dp'), split_axis=0, concat_axis=0, til...  13.3 us
    concatenate x1, other arithmetic, shards(): jnp.concatenate([part_in, part_out[:, :, :in_cols], jnp.concatenate(bands...  9.54 us
    all_to_all x2, waiting for transfers between devices, exchange(): lax.all_to_all(shaped, ('expert', 'dp'), split_axis=0, concat_axis=0, til...  9.21 us
    ppermute x1, waiting for transfers between devices, partner_2(): return lax.ppermute(block, axis, route)  8.02 us
    dot_general x1, matrix products, shards(): jnp.einsum('sf,df->sd', gate_up_grad, weight_in, preferred_element_type=j...  6.27 us
  transfers between devices with their start and end apart: 4, of which 3 were waited for; matrix products, arithmetic and copies ran while one was open for 10% of the time, Pallas kernels for 0%

profile of v7, /device:TPU:24, one launch (start us, length us, event | category | flops | bytes accessed | tf_op | source)
XLA Modules:
  0.0 201.7 jit_solution(5111124049376237518)
XLA Ops:
  7.2 0.9 copy.18
  8.2 0.8 copy.17
  9.1 0.5 fusion.19
  9.7 0.4 fusion.26
  10.1 0.4 select_reduce_fusion
  10.5 1.6 convolution_convert_fusion
  12.2 1.5 fusion.9
  13.7 0.2 pad_maximum_fusion
  13.9 33.5 %all_to_all.15 = bf16[16,16,4096]{2,1,0:T(8,128)(2,1)S(1)} all-to-all(bf16[16,16,4096]{2,1,0:T(8,128)(2,1)S(1)} %bitcast.44), channel_id=1, replica_groups={{0,16,40,56,64,80,104,120,128,144,168,184,192,208,232,248},{1,17,41,57,..., dimensions={0} | all-to-all | bytes 4194304 | tf_op jit(solution)/shard_map/all_to_all | solution.py:33
  47.4 1.8 fusion.2
  49.2 1.3 multiply_convert_fusion.3
  50.5 1.0 multiply_convert_fusion.1
  51.9 1.8 multiply_convert_fusion
  53.7 9.5 %maximum_maximum_fusion = bf16[16,192,1536]{2,1,0:T(8,128)(2,1)} fusion(bf16[16,16,512]{2,1,0:T(8,128)(2,1)S(1)} %get-tuple-element.13, bf16[16,16,512]{2,1,0:T(8,128)(2,1)S(1)} %get-tuple-element.14, bf16[16,16,512]{2,1,0:T(8,128)(2,1)S(1)} %get-tuple-element.12, bf16[16,48,1536]{2,1,0:T(8,128)(2,1)S(1)} %slice.64, bf16[16,128,1536]{2,1,0:T(8,128)(2,1)S(1)} %bitcast.45), kind=kLoop, calls=%fused_computation.1 | loop fusion | flops 47185920 | bytes 18874368 | tf_op jit(solution)/shard_map/concatenate | solution.py:117
  63.3 3.0 %fusion.13 = bf16[256,2048]{1,0:T(8,128)(2,1)} fusion(bf16[256,768]{1,0:T(8,128)(2,1)} %copy-done.3, bf16[1,768,2048]{2,1,0:T(8,128)(2,1)S(1)} %copy-done), kind=kOutput, calls=%fused_computation.17 | convolution fusion | flops 805830656 | bytes 4587520 | tf_op jit(solution)/shard_map/dot_general | solution.py:90
  66.2 6.5 %all-to-all-start.1 = ((bf16[16,16,2048]{2,1,0:T(8,128)(2,1)}), bf16[16,16,2048]{2,1,0:T(8,128)(2,1)}, u32[]{:S(2)}, u32[]{:S(2)}) async-start(bf16[16,16,2048]{2,1,0:T(8,128)(2,1)} %bitcast.53), calls=%async_computation.1 | async-start | bytes 2097152 | tf_op jit(solution)/shard_map/all_to_all | solution.py:33
  72.8 6.3 %fusion.10 = bf16[256,2048]{1,0:T(8,128)(2,1)} fusion(bf16[1,2048,1536]{2,1,0:T(8,128)(2,1)} %param.12, bf16[256,768]{1,0:T(8,128)(2,1)} %copy-done.5, bf16[256,768]{1,0:T(8,128)(2,1)} %copy-done.4), kind=kOutput, calls=%fused_computation.16 | convolution fusion | flops 1612709888 | bytes 8126464 | tf_op jit(solution)/shard_map/sf,df->sd/dot_general | solution.py:100
  79.0 9.2 %all-to-all-done.1 = bf16[16,16,2048]{2,1,0:T(8,128)(2,1)} async-done(((bf16[16,16,2048]{2,1,0:T(8,128)(2,1)}), bf16[16,16,2048]{2,1,0:T(8,128)(2,1)}, u32[]{:S(2)}, u32[]{:S(2)}) %all-to-all-start.1) | async-done | bytes 1048608 | tf_op jit(solution)/shard_map/all_to_all | solution.py:33
  88.2 6.8 %all-to-all-start.2 = ((bf16[16,16,2048]{2,1,0:T(8,128)(2,1)}), bf16[16,16,2048]{2,1,0:T(8,128)(2,1)}, u32[]{:S(2)}, u32[]{:S(2)}) async-start(bf16[16,16,2048]{2,1,0:T(8,128)(2,1)} %bitcast.52), calls=%async_computation.2 | async-start | bytes 2097152 | tf_op jit(solution)/shard_map/all_to_all | solution.py:33
  95.0 0.6 fusion.29
  96.3 2.5 %convolution_bitcast_fusion = f32[128,256]{0,1:T(8,128)} fusion(bf16[256,2048]{1,0:T(8,128)(2,1)} %bitcast.5, bf16[128,2048]{1,0:T(8,128)(2,1)} %param.8), kind=kOutput, calls=%fused_computation.23 | convolution fusion | flops 134217728 | bytes 1703936 | tf_op jit(solution)/shard_map/td,sd->ts/dot_general | solution.py:129
  98.8 1.0 copy.19
  99.8 75.5 %reduce-scatter.2.cloned.1.call-done = bf16[192,1536]{1,0:T(8,128)(2,1)} async-done(((bf16[3072,1536]{1,0:T(8,128)(2,1)}), bf16[192,1536]{1,0:T(8,128)(2,1)}) %reduce-scatter.2.cloned.1.call-update) | async-done | bytes 589840 | tf_op jit(solution)/shard_map/reduce_scatter | solution.py:120
  175.3 1.4 collective-permute-start
  176.7 1.0 select_reduce_fusion.2
  177.7 1.5 copy.20
  179.2 2.4 %convolution_convert_fusion.1 = bf16[128,2048]{1,0:T(8,128)(2,1)} fusion(bf16[128,256]{1,0:T(8,128)(2,1)S(1)} %fusion.26, bf16[256,2048]{1,0:T(8,128)(2,1)} %bitcast.7), kind=kOutput, calls=%fused_computation.18 | convolution fusion | flops 134479872 | bytes 1638400 | tf_op jit(solution)/shard_map/ts,sd->td/dot_general | solution.py:131
  181.6 2.6 %convolution_convert_fusion.2 = bf16[128,2048]{1,0:T(8,128)(2,1)} fusion(f32[128,256]{1,0:T(8,128)S(1)} %get-tuple-element.11, bf16[256,2048]{1,0:T(8,128)(2,1)} %bitcast.5), kind=kOutput, calls=%fused_computation.19 | convolution fusion | flops 805568512 | bytes 1703936 | tf_op jit(solution)/shard_map/dot_general | solution.py:123
  184.2 8.0 %collective-permute-done = bf16[192,1536]{1,0:T(8,128)(2,1)} collective-permute-done((bf16[192,1536]{1,0:T(8,128)(2,1)}, bf16[192,1536]{1,0:T(8,128)(2,1)}, u32[]{:S(2)}, u32[]{:S(2)}) %collective-permute-start) | collective-permute-done | bytes 589856 | tf_op jit(solution)/shard_map/ppermute | solution.py:14
  192.3 1.1 broadcast_select_fusion
  193.4 0.8 slice_bitcast_fusion
  194.2 0.7 maximum_bitcast_fusion
  (29 shorter events, 0.6 us)
Async XLA Ops:
  7.2 42.0 %copy-start = (bf16[1,768,2048]{2,1,0:T(8,128)(2,1)S(1)}, bf16[1,768,2048]{2,1,0:T(8,128)(2,1)}, u32[]{:S(2)}) copy-start(bf16[1,768,2048]{2,1,0:T(8,128)(2,1)} %param.13) | copy-start | bytes 9437188
  7.2 168.1 %reduce-scatter.2.cloned.1.call-start = ((), (), s32[]{:S(2)}) async-start(), calls=%async_computation.4 | async-start | bytes 10027008 | tf_op jit(solution)/shard_map/reduce_scatter | solution.py:120
  10.5 36.9 %slice-start = ((s8[6291456]{0:T(1024)(128)(4,1)}), s8[4194304]{0:T(1024)(128)(4,1)S(1)}, s32[]{:S(2)}) async-start(s8[6291456]{0:T(1024)(128)(4,1)} %bitcast.54), calls=%async_computation.5 | async-start | bytes 8388608
  13.7 33.7 %slice-start.1 = ((s8[6291456]{0:T(1024)(128)(4,1)}), s8[2097152]{0:T(1024)(128)(4,1)S(1)}, s32[]{:S(2)}) async-start(s8[6291456]{0:T(1024)(128)(4,1)} %bitcast.54), calls=%async_computation.6 | async-start | bytes 4194304
  50.5 1.1 copy-start.3
  50.5 1.4 copy-start.4
  50.5 1.4 copy-start.5
  66.2 22.0 %all-to-all-start.1 = ((bf16[16,16,2048]{2,1,0:T(8,128)(2,1)}), bf16[16,16,2048]{2,1,0:T(8,128)(2,1)}, u32[]{:S(2)}, u32[]{:S(2)}) async-start(bf16[16,16,2048]{2,1,0:T(8,128)(2,1)} %bitcast.53), calls=%async_computation.1 | async-start | bytes 2097152 | tf_op jit(solution)/shard_map/all_to_all | solution.py:33
  72.7 22.3 %copy-start.2 = (s32[16]{0:T(128)S(1)}, s32[16]{0:T(128)}, u32[]{:S(2)}) copy-start(s32[16]{0:T(128)} %param.11) | copy-start | bytes 196
  88.2 91.0 %all-to-all-start.2 = ((bf16[16,16,2048]{2,1,0:T(8,128)(2,1)}), bf16[16,16,2048]{2,1,0:T(8,128)(2,1)}, u32[]{:S(2)}, u32[]{:S(2)}) async-start(bf16[16,16,2048]{2,1,0:T(8,128)(2,1)} %bitcast.52), calls=%async_computation.2 | async-start | bytes 2097152 | tf_op jit(solution)/shard_map/all_to_all | solution.py:33
  175.3 16.9 %collective-permute-start = (bf16[192,1536]{1,0:T(8,128)(2,1)}, bf16[192,1536]{1,0:T(8,128)(2,1)}, u32[]{:S(2)}, u32[]{:S(2)}) collective-permute-start(bf16[192,1536]{1,0:T(8,128)(2,1)} %reduce-scatter.2.cloned.1.call-done), channel_id=1, source_target_pairs={{0,128},{128,0},{16,144},{144,16},{32,160},{160,32},{48,176},{176,... | collective-permute-start | bytes 1769480 | tf_op jit(solution)/shard_map/ppermute | solution.py:14
  179.2 13.0 %copy-start.1 = (bf16[192,1536]{1,0:T(8,128)(2,1)S(1)}, bf16[192,1536]{1,0:T(8,128)(2,1)}, u32[]{:S(2)}) copy-start(bf16[192,1536]{1,0:T(8,128)(2,1)} %reduce-scatter.2.cloned.1.call-done) | copy-start | bytes 1769476
Sparse Core Ops, SparseCore 0:
  63.4 111.8 reduce-scatter.1

commit v8 on v7

--- a/solution.py
+++ b/solution.py
@@ -132,6 +132,7 @@
         jnp.bfloat16
     )
 
+    mixed, x_grad, gate_grad, reduced = lax.optimization_barrier((mixed, x_grad, gate_grad, reduced))
     swapped = partner_2(reduced, "expert", half_bit)
     reduced = jnp.where(is_moved, swapped, reduced)
     grad_in = reduced[:in_rows]

time: 202 us -> 203 us (level)
    reduce_scatter x1, waiting for transfers between devices: 75.5 us -> 59.8 us  [shards(): reduced = lax.psum_scatter(joined, 'dp', scatter_dimension=0, tiled=True)]
    all_to_all x2, waiting for transfers between devices: 9.21 us -> 20.2 us  [exchange(): lax.all_to_all(shaped, ('expert', 'dp'), split_axis=0, concat_axis=0, til...]
    ppermute x1, waiting for transfers between devices: 8.02 us -> 13.6 us  [partner_2(): return lax.ppermute(block, axis, route)]
  transfers between devices with their start and end apart: 4 -> 4, of which waited for: 3 -> 4; matrix products, arithmetic and copies ran while one was open for 10% -> 10% of each run, Pallas kernels for 0% -> 0%
where the time goes in v8:
time: 203 us; the launch traced here: 202 us
  waiting for transfers between devices  93.7 us (46%)
  blocking collectives  33.5 us (17%)
  matrix products  26.2 us (13%)
  between operations  14.9 us (7%)
  starting transfers between devices  14.7 us (7%)
  other arithmetic  14.1 us (7%)
  local copies, waits for them, and re-layouts  4.69 us (2%)
    reduce_scatter x1, waiting for transfers between devices, shards(): reduced = lax.psum_scatter(joined, 'dp', scatter_dimension=0, tiled=True)  59.8 us
    all_to_all x1, blocking collectives, exchange(): lax.all_to_all(shaped, ('expert', 'dp'), split_axis=0, concat_axis=0, til...  33.5 us
    all_to_all x2, waiting for transfers between devices, exchange(): lax.all_to_all(shaped, ('expert', 'dp'), split_axis=0, concat_axis=0, til...  20.2 us
    ppermute x1, waiting for transfers between devices, partner_2(): return lax.ppermute(block, axis, route)  13.6 us
    all_to_all x2, starting transfers between devices, exchange(): lax.all_to_all(shaped, ('expert', 'dp'), split_axis=0, concat_axis=0, til...  13.3 us
    concatenate x1, other arithmetic, shards(): jnp.concatenate([part_in, part_out[:, :, :in_cols], jnp.concatenate(bands...  9.54 us
    dot_general x1, matrix products, shards(): jnp.einsum('sf,df->sd', gate_up_grad, weight_in, preferred_element_type=j...  6.26 us
  transfers between devices with their start and end apart: 4, of which 4 were waited for; matrix products, arithmetic and copies ran while one was open for 10% of the time, Pallas kernels for 0%

profile of v8, /device:TPU:24, one launch (start us, length us, event | category | flops | bytes accessed | tf_op | source)
XLA Modules:
  0.0 201.7 jit_solution(6927965918207252668)
XLA Ops:
  7.2 0.9 copy.18
  8.2 0.8 copy.17
  9.1 0.5 fusion.19
  9.7 0.4 fusion.26
  10.1 0.4 select_reduce_fusion
  10.5 1.6 convolution_convert_fusion
  12.2 1.5 fusion.9
  13.9 33.5 %all_to_all.15 = bf16[16,16,4096]{2,1,0:T(8,128)(2,1)S(1)} all-to-all(bf16[16,16,4096]{2,1,0:T(8,128)(2,1)S(1)} %bitcast.44), channel_id=1, replica_groups={{0,16,40,56,64,80,104,120,128,144,168,184,192,208,232,248},{1,17,41,57,..., dimensions={0} | all-to-all | bytes 4194304 | tf_op jit(solution)/shard_map/all_to_all | solution.py:33
  47.4 1.8 fusion.2
  49.2 1.3 multiply_convert_fusion.3
  50.5 1.0 multiply_convert_fusion.1
  51.9 1.8 multiply_convert_fusion
  53.7 9.5 %maximum_maximum_fusion = bf16[16,192,1536]{2,1,0:T(8,128)(2,1)} fusion(bf16[16,16,512]{2,1,0:T(8,128)(2,1)S(1)} %get-tuple-element.21, bf16[16,16,512]{2,1,0:T(8,128)(2,1)S(1)} %get-tuple-element.22, bf16[16,16,512]{2,1,0:T(8,128)(2,1)S(1)} %get-tuple-element.20, bf16[16,48,1536]{2,1,0:T(8,128)(2,1)S(1)} %slice.64, bf16[16,128,1536]{2,1,0:T(8,128)(2,1)S(1)} %bitcast.45), kind=kLoop, calls=%fused_computation.1 | loop fusion | flops 47185920 | bytes 18874368 | tf_op jit(solution)/shard_map/concatenate | solution.py:117
  63.3 3.0 %fusion.13 = bf16[256,2048]{1,0:T(8,128)(2,1)} fusion(bf16[256,768]{1,0:T(8,128)(2,1)} %copy-done.3, bf16[1,768,2048]{2,1,0:T(8,128)(2,1)S(1)} %copy-done), kind=kOutput, calls=%fused_computation.17 | convolution fusion | flops 805830656 | bytes 4587520 | tf_op jit(solution)/shard_map/dot_general | solution.py:90
  66.2 6.5 %all-to-all-start.1 = ((bf16[16,16,2048]{2,1,0:T(8,128)(2,1)}), bf16[16,16,2048]{2,1,0:T(8,128)(2,1)}, u32[]{:S(2)}, u32[]{:S(2)}) async-start(bf16[16,16,2048]{2,1,0:T(8,128)(2,1)} %bitcast.53), calls=%async_computation.1 | async-start | bytes 2097152 | tf_op jit(solution)/shard_map/all_to_all | solution.py:33
  72.8 6.3 %fusion.10 = bf16[256,2048]{1,0:T(8,128)(2,1)} fusion(bf16[1,2048,1536]{2,1,0:T(8,128)(2,1)} %param.12, bf16[256,768]{1,0:T(8,128)(2,1)} %copy-done.5, bf16[256,768]{1,0:T(8,128)(2,1)} %copy-done.4), kind=kOutput, calls=%fused_computation.16 | convolution fusion | flops 1612709888 | bytes 8126464 | tf_op jit(solution)/shard_map/sf,df->sd/dot_general | solution.py:100
  79.0 9.2 %all-to-all-done.1 = bf16[16,16,2048]{2,1,0:T(8,128)(2,1)} async-done(((bf16[16,16,2048]{2,1,0:T(8,128)(2,1)}), bf16[16,16,2048]{2,1,0:T(8,128)(2,1)}, u32[]{:S(2)}, u32[]{:S(2)}) %all-to-all-start.1) | async-done | bytes 1048608 | tf_op jit(solution)/shard_map/all_to_all | solution.py:33
  88.2 6.8 %all-to-all-start.2 = ((bf16[16,16,2048]{2,1,0:T(8,128)(2,1)}), bf16[16,16,2048]{2,1,0:T(8,128)(2,1)}, u32[]{:S(2)}, u32[]{:S(2)}) async-start(bf16[16,16,2048]{2,1,0:T(8,128)(2,1)} %bitcast.52), calls=%async_computation.2 | async-start | bytes 2097152 | tf_op jit(solution)/shard_map/all_to_all | solution.py:33
  95.0 2.5 %convolution_bitcast_fusion = f32[128,256]{0,1:T(8,128)} fusion(bf16[256,2048]{1,0:T(8,128)(2,1)} %bitcast.5, bf16[128,2048]{1,0:T(8,128)(2,1)} %param.8), kind=kOutput, calls=%fused_computation.23 | convolution fusion | flops 134217728 | bytes 1703936 | tf_op jit(solution)/shard_map/td,sd->ts/dot_general | solution.py:129
  97.5 1.0 copy.19
  98.5 1.0 select_reduce_fusion.2
  99.5 11.0 %all-to-all-done.2 = bf16[16,16,2048]{2,1,0:T(8,128)(2,1)} async-done(((bf16[16,16,2048]{2,1,0:T(8,128)(2,1)}), bf16[16,16,2048]{2,1,0:T(8,128)(2,1)}, u32[]{:S(2)}, u32[]{:S(2)}) %all-to-all-start.2) | async-done | bytes 1048608 | tf_op jit(solution)/shard_map/all_to_all | solution.py:33
  110.5 2.3 %convolution_convert_fusion.1 = bf16[128,2048]{1,0:T(8,128)(2,1)} fusion(bf16[128,256]{1,0:T(8,128)(2,1)S(1)} %fusion.26, bf16[256,2048]{1,0:T(8,128)(2,1)} %bitcast.7), kind=kOutput, calls=%fused_computation.18 | convolution fusion | flops 134479872 | bytes 1638400 | tf_op jit(solution)/shard_map/ts,sd->td/dot_general | solution.py:131
  112.9 2.6 %convolution_convert_fusion.2 = bf16[128,2048]{1,0:T(8,128)(2,1)} fusion(f32[128,256]{1,0:T(8,128)S(1)} %get-tuple-element.19, bf16[256,2048]{1,0:T(8,128)(2,1)} %bitcast.5), kind=kOutput, calls=%fused_computation.19 | convolution fusion | flops 805568512 | bytes 1703936 | tf_op jit(solution)/shard_map/dot_general | solution.py:123
  115.5 59.8 %reduce-scatter.2.cloned.1.call-done = bf16[192,1536]{1,0:T(8,128)(2,1)} async-done(((bf16[3072,1536]{1,0:T(8,128)(2,1)}), bf16[192,1536]{1,0:T(8,128)(2,1)}) %reduce-scatter.2.cloned.1.call-update) | async-done | bytes 589840 | tf_op jit(solution)/shard_map/reduce_scatter | solution.py:120
  175.3 1.4 collective-permute-start
  176.7 0.6 fusion.29
  178.0 0.7 copy.20
  178.7 13.6 %collective-permute-done = bf16[192,1536]{1,0:T(8,128)(2,1)} collective-permute-done((bf16[192,1536]{1,0:T(8,128)(2,1)}, bf16[192,1536]{1,0:T(8,128)(2,1)}, u32[]{:S(2)}, u32[]{:S(2)}) %collective-permute-start) | collective-permute-done | bytes 589856 | tf_op jit(solution)/shard_map/ppermute | solution.py:14
  192.2 1.1 broadcast_select_fusion
  193.4 0.8 slice_bitcast_fusion
  194.2 0.7 maximum_bitcast_fusion
  (29 shorter events, 0.8 us)
Async XLA Ops:
  7.2 42.0 %copy-start = (bf16[1,768,2048]{2,1,0:T(8,128)(2,1)S(1)}, bf16[1,768,2048]{2,1,0:T(8,128)(2,1)}, u32[]{:S(2)}) copy-start(bf16[1,768,2048]{2,1,0:T(8,128)(2,1)} %param.13) | copy-start | bytes 9437188
  7.2 168.1 %reduce-scatter.2.cloned.1.call-start = ((), (), s32[]{:S(2)}) async-start(), calls=%async_computation.4 | async-start | bytes 10027008 | tf_op jit(solution)/shard_map/reduce_scatter | solution.py:120
  10.5 36.9 %slice-start = ((s8[6291456]{0:T(1024)(128)(4,1)}), s8[4194304]{0:T(1024)(128)(4,1)S(1)}, s32[]{:S(2)}) async-start(s8[6291456]{0:T(1024)(128)(4,1)} %bitcast.54), calls=%async_computation.5 | async-start | bytes 8388608
  13.7 33.7 %slice-start.1 = ((s8[6291456]{0:T(1024)(128)(4,1)}), s8[2097152]{0:T(1024)(128)(4,1)S(1)}, s32[]{:S(2)}) async-start(s8[6291456]{0:T(1024)(128)(4,1)} %bitcast.54), calls=%async_computation.6 | async-start | bytes 4194304
  50.5 1.1 copy-start.3
  50.5 1.4 copy-start.4
  50.5 1.4 copy-start.5
  66.2 22.0 %all-to-all-start.1 = ((bf16[16,16,2048]{2,1,0:T(8,128)(2,1)}), bf16[16,16,2048]{2,1,0:T(8,128)(2,1)}, u32[]{:S(2)}, u32[]{:S(2)}) async-start(bf16[16,16,2048]{2,1,0:T(8,128)(2,1)} %bitcast.53), calls=%async_computation.1 | async-start | bytes 2097152 | tf_op jit(solution)/shard_map/all_to_all | solution.py:33
  88.2 22.3 %all-to-all-start.2 = ((bf16[16,16,2048]{2,1,0:T(8,128)(2,1)}), bf16[16,16,2048]{2,1,0:T(8,128)(2,1)}, u32[]{:S(2)}, u32[]{:S(2)}) async-start(bf16[16,16,2048]{2,1,0:T(8,128)(2,1)} %bitcast.52), calls=%async_computation.2 | async-start | bytes 2097152 | tf_op jit(solution)/shard_map/all_to_all | solution.py:33
  95.0 81.7 %copy-start.2 = (s32[16]{0:T(128)S(1)}, s32[16]{0:T(128)}, u32[]{:S(2)}) copy-start(s32[16]{0:T(128)} %param.11) | copy-start | bytes 196
  99.5 78.5 %copy-start.1 = (f32[128,8]{1,0:T(8,128)S(1)}, f32[128,8]{1,0:T(8,128)}, u32[]{:S(2)}) copy-start(f32[128,8]{1,0:T(8,128)} %select_reduce_fusion.2) | copy-start | bytes 12292
  175.3 16.9 %collective-permute-start = (bf16[192,1536]{1,0:T(8,128)(2,1)}, bf16[192,1536]{1,0:T(8,128)(2,1)}, u32[]{:S(2)}, u32[]{:S(2)}) collective-permute-start(bf16[192,1536]{1,0:T(8,128)(2,1)} %reduce-scatter.2.cloned.1.call-done), channel_id=1, source_target_pairs={{0,128},{128,0},{16,144},{144,16},{32,160},{160,32},{48,176},{176,... | collective-permute-start | bytes 1769480 | tf_op jit(solution)/shard_map/ppermute | solution.py:14
Sparse Core Ops, SparseCore 0:
  63.4 111.8 reduce-scatter.1

commit v9 on v8

--- a/solution.py
+++ b/solution.py
@@ -1,6 +1,7 @@
 import jax
 import jax.numpy as jnp
 from jax import lax
+from jax.experimental import pallas as pl
 from jax.sharding import PartitionSpec as P
 
 
@@ -12,6 +13,48 @@
         if high != low and high < count:
             route += [(low, high), (high, low)]
     return lax.ppermute(block, axis, route)
+
+
+def joined_grads(x_t, gate_up_grad, hidden_t, rows_c, groups, scale):
+    model_width, slots = x_t.shape
+    in_cols = gate_up_grad.shape[1]
+    hidden_units = hidden_t.shape[0]
+    in_rows = model_width // groups
+    out_rows = hidden_units // groups
+    rest = model_width - in_cols
+    bands = in_cols // rest
+    rest_rows = out_rows // bands
+    total = in_rows + out_rows + rest_rows
+
+    def body(x_ref, gu_ref, h_ref, c_ref, o_ref):
+        part_in = jnp.dot(x_ref[...], gu_ref[...], preferred_element_type=jnp.float32) * scale
+        o_ref[0, 0:in_rows, :] = part_in.astype(o_ref.dtype)
+        h = h_ref[...]
+        part_out = jnp.dot(h, c_ref[:, 0:in_cols], preferred_element_type=jnp.float32) * scale
+        o_ref[0, in_rows : in_rows + out_rows, :] = part_out.astype(o_ref.dtype)
+        tail = jnp.dot(h, c_ref[:, in_cols:], preferred_element_type=jnp.float32) * scale
+        for k in range(bands):
+            o_ref[0, in_rows + out_rows :, k * rest : (k + 1) * rest] = tail[
+                k * rest_rows : (k + 1) * rest_rows
+            ].astype(o_ref.dtype)
+
+    flops = 2 * slots * (model_width * in_cols + hidden_units * model_width)
+    return pl.pallas_call(
+        body,
+        out_shape=jax.ShapeDtypeStruct((groups, total, in_cols), jnp.bfloat16),
+        grid=(groups,),
+        in_specs=[
+            pl.BlockSpec((in_rows, slots), lambda g: (g, 0)),
+            pl.BlockSpec((slots, in_cols), lambda g: (0, 0)),
+            pl.BlockSpec((out_rows, slots), lambda g: (g, 0)),
+            pl.BlockSpec((slots, model_width), lambda g: (0, 0)),
+        ],
+        out_specs=pl.BlockSpec((1, total, in_cols), lambda g: (g, 0, 0)),
+        cost_estimate=pl.CostEstimate(
+            flops=flops, transcendentals=0,
+            bytes_accessed=2 * (slots * (2 * model_width + in_cols + hidden_units) + groups * total * in_cols),
+        ),
+    )(x_t, gate_up_grad, hidden_t, rows_c)
 
 
 def pair_groups(expert_count, group_count):
@@ -106,17 +149,8 @@
     out_rows = hidden_units // group_count
     rest_rows = out_rows // (in_cols // rest)
     scale = 1.0 / group_count
-    part_out = (
-        jnp.einsum("sf,sd->fd", hidden, rows_c, preferred_element_type=jnp.float32) * scale
-    ).astype(jnp.bfloat16).reshape(group_count, out_rows, model_width)
-    part_in = (
-        jnp.einsum("sd,sf->df", rows_x, gate_up_grad, preferred_element_type=jnp.float32) * scale
-    ).astype(jnp.bfloat16).reshape(group_count, in_rows, in_cols)
-    tail = part_out[:, :, in_cols:]
-    bands = [tail[:, k * rest_rows : (k + 1) * rest_rows] for k in range(in_cols // rest)]
-    joined = jnp.concatenate(
-        [part_in, part_out[:, :, :in_cols], jnp.concatenate(bands, axis=2)], axis=1
-    ).reshape(group_count * (in_rows + out_rows + rest_rows), in_cols)
+    joined = joined_grads(rows_x.T, gate_up_grad, hidden.T, rows_c, group_count, scale)
+    joined = joined.reshape(group_count * joined.shape[1], in_cols)
     reduced = lax.psum_scatter(joined, "dp", scatter_dimension=0, tiled=True)
     back_grad = exchange(pick_grad, expert_count, capacity)
 

time: 203 us -> 213 us (1.049)
  Pallas kernels: 0 us -> 13.5 us
  other arithmetic: 14.1 us -> 5.46 us
  local copies, waits for them, and re-layouts: 4.69 us -> 11.3 us
  matrix products: 26.2 us -> 23.8 us
    pallas_call x0 -> x1, Pallas kernels: none -> 13.5 us  [joined_grads(): pl.pallas_call(body, out_shape=jax.ShapeDtypeStruct((groups, total, in_co...]
    concatenate x1, other arithmetic: 9.54 us -> 0.93 us  [shards(): jnp.concatenate([hidden_grad * up_pre * slope, hidden_grad * activated],...]
    dot_general x2 -> x0, matrix products: 2.86 us -> none  [the longest x1 1.84 us: shards(): jnp.einsum('sd,sf->df', rows_x, gate_up_grad, preferred_element_type=jnp....]
    concatenate x0 -> x1, local copies, waits for them, and re-layouts: none -> 2.29 us  [shards(): jnp.concatenate([hidden_grad * up_pre * slope, hidden_grad * activated],...]
    transpose x0 -> x1, local copies, waits for them, and re-layouts: none -> 2.28 us  [shards(): joined = joined_grads(rows_x.T, gate_up_grad, hidden.T, rows_c, group_cou...]
  transfers between devices with their start and end apart: 4 -> 4, of which waited for: 4 -> 4; matrix products, arithmetic and copies ran while one was open for 10% -> 9% of each run, Pallas kernels for 0% -> 0%
where the time goes in v9:
time: 213 us; the launch traced here: 211 us
  waiting for transfers between devices  93.8 us (44%)
  blocking collectives  33.6 us (16%)
  matrix products  23.8 us (11%)
  between operations  14.8 us (7%)
  starting transfers between devices  14.6 us (7%)
  Pallas kernels  13.5 us (6%)
  local copies, waits for them, and re-layouts  11.3 us (5%)
  other arithmetic  5.46 us (3%)
    reduce_scatter x1, waiting for transfers between devices, shards(): reduced = lax.psum_scatter(joined, 'dp', scatter_dimension=0, tiled=True)  60 us
    all_to_all x1, blocking collectives, exchange(): lax.all_to_all(shaped, ('expert', 'dp'), split_axis=0, concat_axis=0, til...  33.6 us
    all_to_all x2, waiting for transfers between devices, exchange(): lax.all_to_all(shaped, ('expert', 'dp'), split_axis=0, concat_axis=0, til...  20.2 us
    ppermute x1, waiting for transfers between devices, partner_2(): return lax.ppermute(block, axis, route)  13.6 us
    pallas_call x1, Pallas kernels, joined_grads(): pl.pallas_call(body, out_shape=jax.ShapeDtypeStruct((groups, total, in_co...  13.5 us
    all_to_all x2, starting transfers between devices, exchange(): lax.all_to_all(shaped, ('expert', 'dp'), split_axis=0, concat_axis=0, til...  13.1 us
    dot_general x1, matrix products, shards(): jnp.einsum('sf,df->sd', gate_up_grad, weight_in, preferred_element_type=j...  6.29 us
  transfers between devices with their start and end apart: 4, of which 4 were waited for; matrix products, arithmetic and copies ran while one was open for 9% of the time, Pallas kernels for 0%

profile of v9, /device:TPU:24, one launch (start us, length us, event | category | flops | bytes accessed | tf_op | source)
XLA Modules:
  0.0 210.9 jit_solution(16490831838225253846)
XLA Ops:
  7.2 0.9 copy.29
  8.3 0.5 fusion.19
  9.3 0.8 copy.30
  10.5 1.5 convolution_convert_fusion
  12.7 33.6 %all_to_all.15 = bf16[16,16,4096]{2,1,0:T(8,128)(2,1)S(1)} all-to-all(bf16[16,16,4096]{2,1,0:T(8,128)(2,1)S(1)} %bitcast.47), channel_id=1, replica_groups={{0,16,40,56,64,80,104,120,128,144,168,184,192,208,232,248},{1,17,41,57,..., dimensions={0} | all-to-all | bytes 4194304 | tf_op jit(solution)/shard_map/all_to_all | solution.py:76
  46.3 1.5 fusion.28
  47.8 2.7 %fusion.2 = f32[256,1536]{0,1:T(8,128)S(1)} fusion(bf16[1,2048,1536]{2,1,0:T(8,128)(2,1)S(1)} %bitcast.52, bf16[256,4096]{1,0:T(8,128)(2,1)S(1)} %bitcast.45), kind=kOutput, calls=%fused_computation.2 | convolution fusion | flops 1610612736 | bytes 8912896 | tf_op jit(solution)/shard_map/dot_general | solution.py:127
  50.5 2.0 multiply_convert_fusion.1
  52.5 0.7 copy-done.2
  53.4 0.9 pad_maximum_fusion.1
  54.4 2.3 %copy.37.gu_ref = bf16[256,1536]{1,0:T(8,128)(2,1)} copy(bf16[256,1536]{0,1:T(8,128)(2,1)} %pad_maximum_fusion.1) | data formatting | bytes 1572864 | tf_op jit(solution)/shard_map/concatenate | solution.py:140
  56.6 2.3 %copy.36.x_ref = bf16[2048,256]{1,0:T(8,128)(2,1)} copy(bf16[2048,256]{0,1:T(8,128)(2,1)} %get-tuple-element.23) | data formatting | bytes 2097152 | tf_op jit(solution)/shard_map/transpose | solution.py:152
  58.9 13.5 %shard_map.110 = bf16[16,192,1536]{2,1,0:T(8,128)(2,1)} custom-call(bf16[2048,256]{1,0:T(8,128)(2,1)} %copy.36.x_ref, bf16[256,1536]{1,0:T(8,128)(2,1)} %copy.37.gu_ref, bf16[768,256]{1,0:T(8,128)(2,1)} %bitcast.50, bf16[256,2048]{1,0:T(8,128)(2,1)} %get-tuple-element.22.c_ref), custom_call_target="tpu_custom_call" | custom-call | flops 2415919104 | bytes 12713984 | tf_op jit(solution)/shard_map/pallas_call | solution.py:42
  72.4 3.0 %fusion.13 = bf16[256,2048]{1,0:T(8,128)(2,1)} fusion(bf16[256,768]{0,1:T(8,128)(2,1)} %get-tuple-element.24, bf16[1,768,2048]{2,1,0:T(8,128)(2,1)S(1)} %copy-done), kind=kOutput, calls=%fused_computation.14 | convolution fusion | flops 805830656 | bytes 4587520 | tf_op jit(solution)/shard_map/dot_general | solution.py:133
  75.4 6.5 %all-to-all-start.1 = ((bf16[16,16,2048]{2,1,0:T(8,128)(2,1)}), bf16[16,16,2048]{2,1,0:T(8,128)(2,1)}, u32[]{:S(2)}, u32[]{:S(2)}) async-start(bf16[16,16,2048]{2,1,0:T(8,128)(2,1)} %bitcast.49), calls=%async_computation.1 | async-start | bytes 2097152 | tf_op jit(solution)/shard_map/all_to_all | solution.py:76
  81.9 6.3 %fusion.10 = bf16[256,2048]{1,0:T(8,128)(2,1)} fusion(bf16[1,2048,1536]{2,1,0:T(8,128)(2,1)} %param.12, bf16[256,768]{0,1:T(8,128)(2,1)} %copy-done.3, bf16[256,768]{0,1:T(8,128)(2,1)} %copy-done.2), kind=kOutput, calls=%fused_computation.13 | convolution fusion | flops 1612709888 | bytes 8126464 | tf_op jit(solution)/shard_map/sf,df->sd/dot_general | solution.py:143
  88.2 9.2 %all-to-all-done.1 = bf16[16,16,2048]{2,1,0:T(8,128)(2,1)} async-done(((bf16[16,16,2048]{2,1,0:T(8,128)(2,1)}), bf16[16,16,2048]{2,1,0:T(8,128)(2,1)}, u32[]{:S(2)}, u32[]{:S(2)}) %all-to-all-start.1) | async-done | bytes 1048608 | tf_op jit(solution)/shard_map/all_to_all | solution.py:76
  97.4 6.6 %all-to-all-start.2 = ((bf16[16,16,2048]{2,1,0:T(8,128)(2,1)}), bf16[16,16,2048]{2,1,0:T(8,128)(2,1)}, u32[]{:S(2)}, u32[]{:S(2)}) async-start(bf16[16,16,2048]{2,1,0:T(8,128)(2,1)} %bitcast.48), calls=%async_computation.2 | async-start | bytes 2097152 | tf_op jit(solution)/shard_map/all_to_all | solution.py:76
  104.0 2.5 %convolution_bitcast_fusion = f32[128,256]{0,1:T(8,128)} fusion(bf16[256,2048]{1,0:T(8,128)(2,1)} %bitcast.5, bf16[128,2048]{1,0:T(8,128)(2,1)} %param.8), kind=kOutput, calls=%fused_computation.20 | convolution fusion | flops 134217728 | bytes 1703936 | tf_op jit(solution)/shard_map/td,sd->ts/dot_general | solution.py:163
  106.5 1.0 copy.35
  107.5 1.0 select_reduce_fusion.2
  108.5 11.0 %all-to-all-done.2 = bf16[16,16,2048]{2,1,0:T(8,128)(2,1)} async-done(((bf16[16,16,2048]{2,1,0:T(8,128)(2,1)}), bf16[16,16,2048]{2,1,0:T(8,128)(2,1)}, u32[]{:S(2)}, u32[]{:S(2)}) %all-to-all-start.2) | async-done | bytes 1048608 | tf_op jit(solution)/shard_map/all_to_all | solution.py:76
  119.5 2.4 %convolution_convert_fusion.1 = bf16[128,2048]{1,0:T(8,128)(2,1)} fusion(bf16[128,256]{1,0:T(8,128)(2,1)S(1)} %fusion.23, bf16[256,2048]{1,0:T(8,128)(2,1)} %bitcast.7), kind=kOutput, calls=%fused_computation.15 | convolution fusion | flops 134479872 | bytes 1638400 | tf_op jit(solution)/shard_map/ts,sd->td/dot_general | solution.py:165
  121.9 2.6 %convolution_convert_fusion.2 = bf16[128,2048]{1,0:T(8,128)(2,1)} fusion(f32[128,256]{1,0:T(8,128)S(1)} %get-tuple-element.19, bf16[256,2048]{1,0:T(8,128)(2,1)} %bitcast.5), kind=kOutput, calls=%fused_computation.16 | convolution fusion | flops 805568512 | bytes 1703936 | tf_op jit(solution)/shard_map/dot_general | solution.py:157
  124.5 60.0 %reduce-scatter.2.cloned.1.call-done = bf16[192,1536]{1,0:T(8,128)(2,1)} async-done(((bf16[3072,1536]{1,0:T(8,128)(2,1)}), bf16[192,1536]{1,0:T(8,128)(2,1)}) %reduce-scatter.2.cloned.1.call-update) | async-done | bytes 589840 | tf_op jit(solution)/shard_map/reduce_scatter | solution.py:154
  184.5 1.4 collective-permute-start
  185.9 0.6 fusion.26
  187.2 0.7 copy.38
  187.8 13.6 %collective-permute-done = bf16[192,1536]{1,0:T(8,128)(2,1)} collective-permute-done((bf16[192,1536]{1,0:T(8,128)(2,1)}, bf16[192,1536]{1,0:T(8,128)(2,1)}, u32[]{:S(2)}, u32[]{:S(2)}) %collective-permute-start) | collective-permute-done | bytes 589856 | tf_op jit(solution)/shard_map/ppermute | solution.py:15
  201.4 1.1 broadcast_select_fusion
  202.6 0.8 slice_bitcast_fusion.1
  203.3 0.7 maximum_bitcast_fusion
  (29 shorter events, 1.9 us)
Async XLA Ops:
  7.2 43.4 %copy-start = (bf16[1,768,2048]{2,1,0:T(8,128)(2,1)S(1)}, bf16[1,768,2048]{2,1,0:T(8,128)(2,1)}, u32[]{:S(2)}) copy-start(bf16[1,768,2048]{2,1,0:T(8,128)(2,1)} %param.13) | copy-start | bytes 9437188
  7.2 177.3 %reduce-scatter.2.cloned.1.call-start = ((), (), s32[]{:S(2)}) async-start(), calls=%async_computation.4 | async-start | bytes 10027008 | tf_op jit(solution)/shard_map/reduce_scatter | solution.py:154
  10.1 1.9 copy-start.1
  12.5 35.3 %slice-start = ((s8[6291456]{0:T(1024)(128)(4,1)}), s8[4194304]{0:T(1024)(128)(4,1)S(1)}, s32[]{:S(2)}) async-start(s8[6291456]{0:T(1024)(128)(4,1)} %bitcast.51), calls=%async_computation.5 | async-start | bytes 8388608
  12.7 35.1 %slice-start.1 = ((s8[6291456]{0:T(1024)(128)(4,1)}), s8[2097152]{0:T(1024)(128)(4,1)S(1)}, s32[]{:S(2)}) async-start(s8[6291456]{0:T(1024)(128)(4,1)} %bitcast.51), calls=%async_computation.6 | async-start | bytes 4194304
  52.5 0.7 copy-start.2
  52.5 0.9 copy-start.3
  75.4 22.0 %all-to-all-start.1 = ((bf16[16,16,2048]{2,1,0:T(8,128)(2,1)}), bf16[16,16,2048]{2,1,0:T(8,128)(2,1)}, u32[]{:S(2)}, u32[]{:S(2)}) async-start(bf16[16,16,2048]{2,1,0:T(8,128)(2,1)} %bitcast.49), calls=%async_computation.1 | async-start | bytes 2097152 | tf_op jit(solution)/shard_map/all_to_all | solution.py:76
  97.4 22.1 %all-to-all-start.2 = ((bf16[16,16,2048]{2,1,0:T(8,128)(2,1)}), bf16[16,16,2048]{2,1,0:T(8,128)(2,1)}, u32[]{:S(2)}, u32[]{:S(2)}) async-start(bf16[16,16,2048]{2,1,0:T(8,128)(2,1)} %bitcast.48), calls=%async_computation.2 | async-start | bytes 2097152 | tf_op jit(solution)/shard_map/all_to_all | solution.py:76
  106.5 79.4 %copy-start.5 = (s32[16]{0:T(128)S(1)}, s32[16]{0:T(128)}, u32[]{:S(2)}) copy-start(s32[16]{0:T(128)} %param.11) | copy-start | bytes 196
  108.5 78.6 %copy-start.4 = (f32[128,8]{1,0:T(8,128)S(1)}, f32[128,8]{1,0:T(8,128)}, u32[]{:S(2)}) copy-start(f32[128,8]{1,0:T(8,128)} %select_reduce_fusion.2) | copy-start | bytes 12292
  184.5 17.0 %collective-permute-start = (bf16[192,1536]{1,0:T(8,128)(2,1)}, bf16[192,1536]{1,0:T(8,128)(2,1)}, u32[]{:S(2)}, u32[]{:S(2)}) collective-permute-start(bf16[192,1536]{1,0:T(8,128)(2,1)} %reduce-scatter.2.cloned.1.call-done), channel_id=1, source_target_pairs={{0,128},{128,0},{16,144},{144,16},{32,160},{160,32},{48,176},{176,... | collective-permute-start | bytes 1769480 | tf_op jit(solution)/shard_map/ppermute | solution.py:15
Sparse Core Ops, SparseCore 0:
  72.6 111.8 reduce-scatter.1

commit v10 on v8

--- a/solution.py
+++ b/solution.py
@@ -133,8 +133,13 @@
     )
 
     mixed, x_grad, gate_grad, reduced = lax.optimization_barrier((mixed, x_grad, gate_grad, reduced))
-    swapped = partner_2(reduced, "expert", half_bit)
-    reduced = jnp.where(is_moved, swapped, reduced)
+    expert_count = lax.axis_size("expert")
+    step = expert_count // 4
+    back_route = [(i, (i - step) % expert_count) for i in range(expert_count)]
+    split = reduced.shape[0] // 2
+    direct = partner_2(reduced[:split], "expert", half_bit)
+    relayed = lax.ppermute(lax.ppermute(reduced[split:], "expert", back_route), "expert", back_route)
+    reduced = jnp.where(is_moved, jnp.concatenate([direct, relayed], axis=0), reduced)
     grad_in = reduced[:in_rows]
     tail = reduced[in_rows + out_rows :]
     grad_out = jnp.concatenate(

time: 203 us -> 212 us (1.044)
  waiting for transfers between devices: 93.7 us -> 100 us
  local copies, waits for them, and re-layouts: 4.69 us -> 7.32 us
    ppermute x0 -> x2, waiting for transfers between devices: none -> 20.2 us  [the longest x1 14.5 us: shards(): lax.ppermute(reduced[split:], 'expert', back_route)]
    ppermute x1, waiting for transfers between devices: 13.6 us -> 0.01 us  [partner_2(): return lax.ppermute(block, axis, route)]
  transfers between devices with their start and end apart: 4 -> 6, of which waited for: 4 -> 5; matrix products, arithmetic and copies ran while one was open for 10% -> 10% of each run, Pallas kernels for 0% -> 0%
where the time goes in v10:
time: 212 us
  waiting for transfers between devices  100 us (47%)
  blocking collectives  33.5 us (16%)
  matrix products  26.2 us (12%)
  starting transfers between devices  15.3 us (7%)
  between operations  14.9 us (7%)
  other arithmetic  14.1 us (7%)
  local copies, waits for them, and re-layouts  7.32 us (3%)
    reduce_scatter x1, waiting for transfers between devices, shards(): reduced = lax.psum_scatter(joined, 'dp', scatter_dimension=0, tiled=True)  59.8 us
    all_to_all x1, blocking collectives, exchange(): lax.all_to_all(shaped, ('expert', 'dp'), split_axis=0, concat_axis=0, til...  33.5 us
    all_to_all x2, waiting for transfers between devices, exchange(): lax.all_to_all(shaped, ('expert', 'dp'), split_axis=0, concat_axis=0, til...  20.2 us
    ppermute x1, waiting for transfers between devices, shards(): lax.ppermute(reduced[split:], 'expert', back_route)  14.5 us
    all_to_all x2, starting transfers between devices, exchange(): lax.all_to_all(shaped, ('expert', 'dp'), split_axis=0, concat_axis=0, til...  13.3 us
    concatenate x1, other arithmetic, shards(): jnp.concatenate([part_in, part_out[:, :, :in_cols], jnp.concatenate(bands...  9.55 us
    dot_general x1, matrix products, shards(): jnp.einsum('sf,df->sd', gate_up_grad, weight_in, preferred_element_type=j...  6.27 us
    ppermute x1, waiting for transfers between devices, shards(): lax.ppermute(lax.ppermute(reduced[split:], 'expert', back_route), 'expert...  5.73 us
  transfers between devices with their start and end apart: 6, of which 5 were waited for; matrix products, arithmetic and copies ran while one was open for 10% of the time, Pallas kernels for 0%

profile of v10, /device:TPU:24, one launch (start us, length us, event | category | flops | bytes accessed | tf_op | source)
XLA Modules:
  0.0 211.5 jit_solution(10849527553099383870)
XLA Ops:
  7.2 0.9 copy.18
  8.2 0.8 copy.17
  10.5 1.6 convolution_convert_fusion
  12.2 1.5 fusion.9
  13.9 33.5 %all_to_all.15 = bf16[16,16,4096]{2,1,0:T(8,128)(2,1)S(1)} all-to-all(bf16[16,16,4096]{2,1,0:T(8,128)(2,1)S(1)} %bitcast.44), channel_id=1, replica_groups={{0,16,40,56,64,80,104,120,128,144,168,184,192,208,232,248},{1,17,41,57,..., dimensions={0} | all-to-all | bytes 4194304 | tf_op jit(solution)/shard_map/all_to_all | solution.py:33
  47.4 1.8 fusion.2
  49.2 1.3 multiply_convert_fusion.3
  50.5 1.0 multiply_convert_fusion.1
  51.9 1.8 multiply_convert_fusion
  53.7 9.6 %maximum_maximum_fusion = bf16[16,192,1536]{2,1,0:T(8,128)(2,1)} fusion(bf16[16,16,512]{2,1,0:T(8,128)(2,1)S(1)} %get-tuple-element.21, bf16[16,16,512]{2,1,0:T(8,128)(2,1)S(1)} %get-tuple-element.22, bf16[16,16,512]{2,1,0:T(8,128)(2,1)S(1)} %get-tuple-element.20, bf16[16,48,1536]{2,1,0:T(8,128)(2,1)S(1)} %slice.72, bf16[16,128,1536]{2,1,0:T(8,128)(2,1)S(1)} %bitcast.45), kind=kLoop, calls=%fused_computation.1 | loop fusion | flops 47185920 | bytes 18874368 | tf_op jit(solution)/shard_map/concatenate | solution.py:117
  63.3 3.0 %fusion.13 = bf16[256,2048]{1,0:T(8,128)(2,1)} fusion(bf16[256,768]{1,0:T(8,128)(2,1)} %copy-done.2, bf16[1,768,2048]{2,1,0:T(8,128)(2,1)S(1)} %copy-done), kind=kOutput, calls=%fused_computation.17 | convolution fusion | flops 805830656 | bytes 4587520 | tf_op jit(solution)/shard_map/dot_general | solution.py:90
  66.2 6.5 %all-to-all-start.1 = ((bf16[16,16,2048]{2,1,0:T(8,128)(2,1)}), bf16[16,16,2048]{2,1,0:T(8,128)(2,1)}, u32[]{:S(2)}, u32[]{:S(2)}) async-start(bf16[16,16,2048]{2,1,0:T(8,128)(2,1)} %bitcast.53), calls=%async_computation.1 | async-start | bytes 2097152 | tf_op jit(solution)/shard_map/all_to_all | solution.py:33
  72.8 6.3 %fusion.10 = bf16[256,2048]{1,0:T(8,128)(2,1)} fusion(bf16[1,2048,1536]{2,1,0:T(8,128)(2,1)} %param.12, bf16[256,768]{1,0:T(8,128)(2,1)} %copy-done.4, bf16[256,768]{1,0:T(8,128)(2,1)} %copy-done.3), kind=kOutput, calls=%fused_computation.16 | convolution fusion | flops 1612709888 | bytes 8126464 | tf_op jit(solution)/shard_map/sf,df->sd/dot_general | solution.py:100
  79.0 9.2 %all-to-all-done.1 = bf16[16,16,2048]{2,1,0:T(8,128)(2,1)} async-done(((bf16[16,16,2048]{2,1,0:T(8,128)(2,1)}), bf16[16,16,2048]{2,1,0:T(8,128)(2,1)}, u32[]{:S(2)}, u32[]{:S(2)}) %all-to-all-start.1) | async-done | bytes 1048608 | tf_op jit(solution)/shard_map/all_to_all | solution.py:33
  88.3 6.8 %all-to-all-start.2 = ((bf16[16,16,2048]{2,1,0:T(8,128)(2,1)}), bf16[16,16,2048]{2,1,0:T(8,128)(2,1)}, u32[]{:S(2)}, u32[]{:S(2)}) async-start(bf16[16,16,2048]{2,1,0:T(8,128)(2,1)} %bitcast.52), calls=%async_computation.2 | async-start | bytes 2097152 | tf_op jit(solution)/shard_map/all_to_all | solution.py:33
  95.0 2.5 %convolution_bitcast_fusion = f32[128,256]{0,1:T(8,128)} fusion(bf16[256,2048]{1,0:T(8,128)(2,1)} %bitcast.5, bf16[128,2048]{1,0:T(8,128)(2,1)} %param.8), kind=kOutput, calls=%fused_computation.23 | convolution fusion | flops 134217728 | bytes 1703936 | tf_op jit(solution)/shard_map/td,sd->ts/dot_general | solution.py:129
  97.5 1.0 copy.19
  98.5 1.0 select_reduce_fusion.2
  99.5 11.0 %all-to-all-done.2 = bf16[16,16,2048]{2,1,0:T(8,128)(2,1)} async-done(((bf16[16,16,2048]{2,1,0:T(8,128)(2,1)}), bf16[16,16,2048]{2,1,0:T(8,128)(2,1)}, u32[]{:S(2)}, u32[]{:S(2)}) %all-to-all-start.2) | async-done | bytes 1048608 | tf_op jit(solution)/shard_map/all_to_all | solution.py:33
  110.5 2.3 %convolution_convert_fusion.1 = bf16[128,2048]{1,0:T(8,128)(2,1)} fusion(bf16[128,256]{1,0:T(8,128)(2,1)S(1)} %fusion.26, bf16[256,2048]{1,0:T(8,128)(2,1)} %bitcast.7), kind=kOutput, calls=%fused_computation.18 | convolution fusion | flops 134479872 | bytes 1638400 | tf_op jit(solution)/shard_map/ts,sd->td/dot_general | solution.py:131
  112.9 2.6 %convolution_convert_fusion.2 = bf16[128,2048]{1,0:T(8,128)(2,1)} fusion(f32[128,256]{1,0:T(8,128)S(1)} %get-tuple-element.19, bf16[256,2048]{1,0:T(8,128)(2,1)} %bitcast.5), kind=kOutput, calls=%fused_computation.19 | convolution fusion | flops 805568512 | bytes 1703936 | tf_op jit(solution)/shard_map/dot_general | solution.py:123
  115.5 59.8 %reduce-scatter.2.cloned.1.call-done = bf16[192,1536]{1,0:T(8,128)(2,1)} async-done(((bf16[3072,1536]{1,0:T(8,128)(2,1)}), bf16[192,1536]{1,0:T(8,128)(2,1)}) %reduce-scatter.2.cloned.1.call-update) | async-done | bytes 589840 | tf_op jit(solution)/shard_map/reduce_scatter | solution.py:120
  175.3 1.8 fusion.34
  177.1 0.8 collective-permute-start.1
  177.9 1.1 collective-permute-start
  179.1 14.5 %collective-permute-done.1 = bf16[96,1536]{1,0:T(8,128)(2,1)} collective-permute-done((bf16[96,1536]{1,0:T(8,128)(2,1)S(1)}, bf16[96,1536]{1,0:T(8,128)(2,1)}, u32[]{:S(2)}, u32[]{:S(2)}) %collective-permute-start.1) | collective-permute-done | bytes 294944 | tf_op jit(solution)/shard_map/ppermute | solution.py:141
  193.6 0.6 fusion.29
  194.9 1.5 copy.20
  196.4 5.7 %collective-permute-done.2 = bf16[96,1536]{1,0:T(8,128)(2,1)} collective-permute-done((bf16[96,1536]{1,0:T(8,128)(2,1)}, bf16[96,1536]{1,0:T(8,128)(2,1)}, u32[]{:S(2)}, u32[]{:S(2)}) %collective-permute-start.2) | collective-permute-done | bytes 294944 | tf_op jit(solution)/shard_map/ppermute | solution.py:141
  202.1 1.1 maximum_select_fusion
  203.2 0.8 slice_bitcast_fusion
  204.0 0.7 maximum_bitcast_fusion
  (32 shorter events, 2.1 us)
Async XLA Ops:
  7.2 42.0 %copy-start = (bf16[1,768,2048]{2,1,0:T(8,128)(2,1)S(1)}, bf16[1,768,2048]{2,1,0:T(8,128)(2,1)}, u32[]{:S(2)}) copy-start(bf16[1,768,2048]{2,1,0:T(8,128)(2,1)} %param.13) | copy-start | bytes 9437188
  7.2 168.1 %reduce-scatter.2.cloned.1.call-start = ((), (), s32[]{:S(2)}) async-start(), calls=%async_computation.4 | async-start | bytes 10027008 | tf_op jit(solution)/shard_map/reduce_scatter | solution.py:120
  10.5 36.9 %slice-start = ((s8[6291456]{0:T(1024)(128)(4,1)}), s8[4194304]{0:T(1024)(128)(4,1)S(1)}, s32[]{:S(2)}) async-start(s8[6291456]{0:T(1024)(128)(4,1)} %bitcast.54), calls=%async_computation.5 | async-start | bytes 8388608
  13.7 33.7 %slice-start.1 = ((s8[6291456]{0:T(1024)(128)(4,1)}), s8[2097152]{0:T(1024)(128)(4,1)S(1)}, s32[]{:S(2)}) async-start(s8[6291456]{0:T(1024)(128)(4,1)} %bitcast.54), calls=%async_computation.6 | async-start | bytes 4194304
  50.5 1.1 copy-start.2
  50.5 1.4 copy-start.3
  50.5 1.4 copy-start.4
  66.2 22.0 %all-to-all-start.1 = ((bf16[16,16,2048]{2,1,0:T(8,128)(2,1)}), bf16[16,16,2048]{2,1,0:T(8,128)(2,1)}, u32[]{:S(2)}, u32[]{:S(2)}) async-start(bf16[16,16,2048]{2,1,0:T(8,128)(2,1)} %bitcast.53), calls=%async_computation.1 | async-start | bytes 2097152 | tf_op jit(solution)/shard_map/all_to_all | solution.py:33
  88.3 22.3 %all-to-all-start.2 = ((bf16[16,16,2048]{2,1,0:T(8,128)(2,1)}), bf16[16,16,2048]{2,1,0:T(8,128)(2,1)}, u32[]{:S(2)}, u32[]{:S(2)}) async-start(bf16[16,16,2048]{2,1,0:T(8,128)(2,1)} %bitcast.52), calls=%async_computation.2 | async-start | bytes 2097152 | tf_op jit(solution)/shard_map/all_to_all | solution.py:33
  95.0 98.5 %copy-start.1 = (s32[16]{0:T(128)S(1)}, s32[16]{0:T(128)}, u32[]{:S(2)}) copy-start(s32[16]{0:T(128)} %param.11) | copy-start | bytes 196
  177.1 16.4 %collective-permute-start.1 = (bf16[96,1536]{1,0:T(8,128)(2,1)S(1)}, bf16[96,1536]{1,0:T(8,128)(2,1)}, u32[]{:S(2)}, u32[]{:S(2)}) collective-permute-start(bf16[96,1536]{1,0:T(8,128)(2,1)S(1)} %get-tuple-element.30), channel_id=1, source_target_pairs={{0,192},{16,208},{32,224},{48,240},{64,0},{80,16},{96,32},{112,48}... | collective-permute-start | bytes 884744 | tf_op jit(solution)/shard_map/ppermute | solution.py:141
  177.9 18.4 %collective-permute-start = (bf16[96,1536]{1,0:T(8,128)(2,1)}, bf16[96,1536]{1,0:T(8,128)(2,1)S(1)}, u32[]{:S(2)}, u32[]{:S(2)}) collective-permute-start(bf16[96,1536]{1,0:T(8,128)(2,1)} %get-tuple-element.29), channel_id=1, source_target_pairs={{0,128},{128,0},{16,144},{144,16},{32,160},{160,32},{48,176},{176,... | collective-permute-start | bytes 884744 | tf_op jit(solution)/shard_map/ppermute | solution.py:14
  193.6 8.5 %collective-permute-start.2 = (bf16[96,1536]{1,0:T(8,128)(2,1)}, bf16[96,1536]{1,0:T(8,128)(2,1)}, u32[]{:S(2)}, u32[]{:S(2)}) collective-permute-start(bf16[96,1536]{1,0:T(8,128)(2,1)} %collective-permute-done.1), channel_id=1, source_target_pairs={{0,192},{16,208},{32,224},{48,240},{64,0},{80,16},{96,32},{112,48}... | collective-permute-start | bytes 884744 | tf_op jit(solution)/shard_map/ppermute | solution.py:141
Sparse Core Ops, SparseCore 0:
  63.4 111.8 reduce-scatter.1

commit v11 on v8

--- a/solution.py
+++ b/solution.py
@@ -107,16 +107,20 @@
     rest_rows = out_rows // (in_cols // rest)
     scale = 1.0 / group_count
     part_out = (
-        jnp.einsum("sf,sd->fd", hidden, rows_c, preferred_element_type=jnp.float32) * scale
-    ).astype(jnp.bfloat16).reshape(group_count, out_rows, model_width)
+        jnp.einsum("sf,sd->fd", hidden, rows_c[:, :in_cols], preferred_element_type=jnp.float32) * scale
+    ).astype(jnp.bfloat16).reshape(group_count, out_rows, in_cols)
     part_in = (
         jnp.einsum("sd,sf->df", rows_x, gate_up_grad, preferred_element_type=jnp.float32) * scale
     ).astype(jnp.bfloat16).reshape(group_count, in_rows, in_cols)
-    tail = part_out[:, :, in_cols:]
-    bands = [tail[:, k * rest_rows : (k + 1) * rest_rows] for k in range(in_cols // rest)]
-    joined = jnp.concatenate(
-        [part_in, part_out[:, :, :in_cols], jnp.concatenate(bands, axis=2)], axis=1
-    ).reshape(group_count * (in_rows + out_rows + rest_rows), in_cols)
+    band_count = in_cols // rest
+    hidden_bands = hidden.reshape(hidden.shape[0], group_count, band_count, rest_rows)
+    bands = (
+        jnp.einsum("sgkr,sd->grkd", hidden_bands, rows_c[:, in_cols:], preferred_element_type=jnp.float32)
+        * scale
+    ).astype(jnp.bfloat16).reshape(group_count, rest_rows, in_cols)
+    joined = jnp.concatenate([part_in, part_out, bands], axis=1).reshape(
+        group_count * (in_rows + out_rows + rest_rows), in_cols
+    )
     reduced = lax.psum_scatter(joined, "dp", scatter_dimension=0, tiled=True)
     back_grad = exchange(pick_grad, expert_count, capacity)
 

time: 203 us -> 197 us (0.970)
  other arithmetic: 14.1 us -> 8.7 us
    concatenate x1, other arithmetic: 9.54 us -> 3.96 us  [shards(): jnp.concatenate([part_in, part_out, bands], axis=1)]
where the time goes in v11:
time: 197 us; the launch traced here: 196 us
  waiting for transfers between devices  93.8 us (48%)
  blocking collectives  33.5 us (17%)
  matrix products  26.4 us (13%)
  between operations  14.9 us (8%)
  starting transfers between devices  14.6 us (7%)
  other arithmetic  8.7 us (4%)
  local copies, waits for them, and re-layouts  4.45 us (2%)
    reduce_scatter x1, waiting for transfers between devices, shards(): reduced = lax.psum_scatter(joined, 'dp', scatter_dimension=0, tiled=True)  60 us
    all_to_all x1, blocking collectives, exchange(): lax.all_to_all(shaped, ('expert', 'dp'), split_axis=0, concat_axis=0, til...  33.5 us
    all_to_all x2, waiting for transfers between devices, exchange(): lax.all_to_all(shaped, ('expert', 'dp'), split_axis=0, concat_axis=0, til...  20.2 us
    ppermute x1, waiting for transfers between devices, partner_2(): return lax.ppermute(block, axis, route)  13.6 us
    all_to_all x2, starting transfers between devices, exchange(): lax.all_to_all(shaped, ('expert', 'dp'), split_axis=0, concat_axis=0, til...  13.1 us
    dot_general x1, matrix products, shards(): jnp.einsum('sf,df->sd', gate_up_grad, weight_in, preferred_element_type=j...  6.26 us
    concatenate x1, other arithmetic, shards(): jnp.concatenate([part_in, part_out, bands], axis=1)  3.96 us
  transfers between devices with their start and end apart: 4, of which 4 were waited for; matrix products, arithmetic and copies ran while one was open for 10% of the time, Pallas kernels for 0%

profile of v11, /device:TPU:24, one launch (start us, length us, event | category | flops | bytes accessed | tf_op | source)
XLA Modules:
  0.0 196.3 jit_solution(10991985689762269450)
XLA Ops:
  7.2 0.9 copy.21
  8.2 0.8 copy.20
  9.1 0.5 fusion.19
  9.7 0.4 fusion.27
  10.1 0.4 select_reduce_fusion
  10.5 1.6 convolution_convert_fusion
  12.2 1.5 fusion.9
  13.9 33.5 %all_to_all.15 = bf16[16,16,4096]{2,1,0:T(8,128)(2,1)S(1)} all-to-all(bf16[16,16,4096]{2,1,0:T(8,128)(2,1)S(1)} %bitcast.53), channel_id=1, replica_groups={{0,16,40,56,64,80,104,120,128,144,168,184,192,208,232,248},{1,17,41,57,..., dimensions={0} | all-to-all | bytes 4194304 | tf_op jit(solution)/shard_map/all_to_all | solution.py:33
  47.4 1.8 fusion.2
  49.2 1.3 multiply_convert_fusion.4
  50.9 0.8 multiply_convert_fusion.1
  52.0 1.8 multiply_convert_fusion
  53.9 4.0 %pad_maximum_fusion = bf16[16,192,1536]{2,1,0:T(8,128)(2,1)} fusion(bf16[16,16,1536]{2,1,0:T(8,128)(2,1)S(1)} %bitcast.56, bf16[16,48,1536]{2,1,0:T(8,128)(2,1)S(1)} %bitcast.62, bf16[16,128,1536]{2,1,0:T(8,128)(2,1)S(1)} %bitcast.55), kind=kLoop, calls=%fused_computation.1 | loop fusion | flops 28311552 | bytes 18874368 | tf_op jit(solution)/shard_map/concatenate | solution.py:121
  57.9 3.0 %fusion.13 = bf16[256,2048]{1,0:T(8,128)(2,1)} fusion(bf16[256,768]{1,0:T(8,128)(2,1)} %copy-done.1, bf16[1,768,2048]{2,1,0:T(8,128)(2,1)S(1)} %copy-done), kind=kOutput, calls=%fused_computation.17 | convolution fusion | flops 805830656 | bytes 4587520 | tf_op jit(solution)/shard_map/dot_general | solution.py:90
  60.8 6.5 %all-to-all-start.1 = ((bf16[16,16,2048]{2,1,0:T(8,128)(2,1)}), bf16[16,16,2048]{2,1,0:T(8,128)(2,1)}, u32[]{:S(2)}, u32[]{:S(2)}) async-start(bf16[16,16,2048]{2,1,0:T(8,128)(2,1)} %bitcast.64), calls=%async_computation.1 | async-start | bytes 2097152 | tf_op jit(solution)/shard_map/all_to_all | solution.py:33
  67.3 6.3 %fusion.10 = bf16[256,2048]{1,0:T(8,128)(2,1)} fusion(bf16[1,2048,1536]{2,1,0:T(8,128)(2,1)} %param.12, bf16[256,768]{1,0:T(8,128)(2,1)} %copy-done.5, bf16[256,768]{1,0:T(8,128)(2,1)} %copy-done.4), kind=kOutput, calls=%fused_computation.16 | convolution fusion | flops 1612709888 | bytes 8126464 | tf_op jit(solution)/shard_map/sf,df->sd/dot_general | solution.py:100
  73.6 9.2 %all-to-all-done.1 = bf16[16,16,2048]{2,1,0:T(8,128)(2,1)} async-done(((bf16[16,16,2048]{2,1,0:T(8,128)(2,1)}), bf16[16,16,2048]{2,1,0:T(8,128)(2,1)}, u32[]{:S(2)}, u32[]{:S(2)}) %all-to-all-start.1) | async-done | bytes 1048608 | tf_op jit(solution)/shard_map/all_to_all | solution.py:33
  82.8 6.6 %all-to-all-start.2 = ((bf16[16,16,2048]{2,1,0:T(8,128)(2,1)}), bf16[16,16,2048]{2,1,0:T(8,128)(2,1)}, u32[]{:S(2)}, u32[]{:S(2)}) async-start(bf16[16,16,2048]{2,1,0:T(8,128)(2,1)} %bitcast.63), calls=%async_computation.2 | async-start | bytes 2097152 | tf_op jit(solution)/shard_map/all_to_all | solution.py:33
  89.4 2.5 %convolution_bitcast_fusion = f32[128,256]{0,1:T(8,128)} fusion(bf16[256,2048]{1,0:T(8,128)(2,1)} %bitcast.5, bf16[128,2048]{1,0:T(8,128)(2,1)} %param.8), kind=kOutput, calls=%fused_computation.24 | convolution fusion | flops 134217728 | bytes 1703936 | tf_op jit(solution)/shard_map/td,sd->ts/dot_general | solution.py:133
  91.9 1.0 copy.22
  92.9 1.0 select_reduce_fusion.2
  93.9 11.0 %all-to-all-done.2 = bf16[16,16,2048]{2,1,0:T(8,128)(2,1)} async-done(((bf16[16,16,2048]{2,1,0:T(8,128)(2,1)}), bf16[16,16,2048]{2,1,0:T(8,128)(2,1)}, u32[]{:S(2)}, u32[]{:S(2)}) %all-to-all-start.2) | async-done | bytes 1048608 | tf_op jit(solution)/shard_map/all_to_all | solution.py:33
  104.9 2.4 %convolution_convert_fusion.1 = bf16[128,2048]{1,0:T(8,128)(2,1)} fusion(bf16[128,256]{1,0:T(8,128)(2,1)S(1)} %fusion.27, bf16[256,2048]{1,0:T(8,128)(2,1)} %bitcast.7), kind=kOutput, calls=%fused_computation.18 | convolution fusion | flops 134479872 | bytes 1638400 | tf_op jit(solution)/shard_map/ts,sd->td/dot_general | solution.py:135
  107.3 2.6 %convolution_convert_fusion.2 = bf16[128,2048]{1,0:T(8,128)(2,1)} fusion(f32[128,256]{1,0:T(8,128)S(1)} %get-tuple-element.19, bf16[256,2048]{1,0:T(8,128)(2,1)} %bitcast.5), kind=kOutput, calls=%fused_computation.19 | convolution fusion | flops 805568512 | bytes 1703936 | tf_op jit(solution)/shard_map/dot_general | solution.py:127
  109.9 60.0 %reduce-scatter.2.cloned.1.call-done = bf16[192,1536]{1,0:T(8,128)(2,1)} async-done(((bf16[3072,1536]{1,0:T(8,128)(2,1)}), bf16[192,1536]{1,0:T(8,128)(2,1)}) %reduce-scatter.2.cloned.1.call-update) | async-done | bytes 589840 | tf_op jit(solution)/shard_map/reduce_scatter | solution.py:124
  169.9 1.4 collective-permute-start
  171.3 0.6 fusion.32
  172.6 0.7 copy.25
  173.3 13.6 %collective-permute-done = bf16[192,1536]{1,0:T(8,128)(2,1)} collective-permute-done((bf16[192,1536]{1,0:T(8,128)(2,1)}, bf16[192,1536]{1,0:T(8,128)(2,1)}, u32[]{:S(2)}, u32[]{:S(2)}) %collective-permute-start) | collective-permute-done | bytes 589856 | tf_op jit(solution)/shard_map/ppermute | solution.py:14
  186.8 1.1 broadcast_select_fusion
  188.0 0.8 slice_bitcast_fusion
  188.8 0.7 maximum_bitcast_fusion
  (30 shorter events, 1.2 us)
Async XLA Ops:
  7.2 42.0 %copy-start = (bf16[1,768,2048]{2,1,0:T(8,128)(2,1)S(1)}, bf16[1,768,2048]{2,1,0:T(8,128)(2,1)}, u32[]{:S(2)}) copy-start(bf16[1,768,2048]{2,1,0:T(8,128)(2,1)} %param.13) | copy-start | bytes 9437188
  7.2 162.7 %reduce-scatter.2.cloned.1.call-start = ((), (), s32[]{:S(2)}) async-start(), calls=%async_computation.4 | async-start | bytes 10027008 | tf_op jit(solution)/shard_map/reduce_scatter | solution.py:124
  10.5 36.9 %slice-start = ((s8[6291456]{0:T(1024)(128)(4,1)}), s8[4194304]{0:T(1024)(128)(4,1)S(1)}, s32[]{:S(2)}) async-start(s8[6291456]{0:T(1024)(128)(4,1)} %bitcast.65), calls=%async_computation.5 | async-start | bytes 8388608
  13.7 33.7 %slice-start.1 = ((s8[6291456]{0:T(1024)(128)(4,1)}), s8[2097152]{0:T(1024)(128)(4,1)S(1)}, s32[]{:S(2)}) async-start(s8[6291456]{0:T(1024)(128)(4,1)} %bitcast.65), calls=%async_computation.6 | async-start | bytes 4194304
  50.5 1.5 copy-start.1
  50.5 1.5 copy-start.4
  50.5 1.5 copy-start.5
  60.8 22.0 %all-to-all-start.1 = ((bf16[16,16,2048]{2,1,0:T(8,128)(2,1)}), bf16[16,16,2048]{2,1,0:T(8,128)(2,1)}, u32[]{:S(2)}, u32[]{:S(2)}) async-start(bf16[16,16,2048]{2,1,0:T(8,128)(2,1)} %bitcast.64), calls=%async_computation.1 | async-start | bytes 2097152 | tf_op jit(solution)/shard_map/all_to_all | solution.py:33
  82.8 22.1 %all-to-all-start.2 = ((bf16[16,16,2048]{2,1,0:T(8,128)(2,1)}), bf16[16,16,2048]{2,1,0:T(8,128)(2,1)}, u32[]{:S(2)}, u32[]{:S(2)}) async-start(bf16[16,16,2048]{2,1,0:T(8,128)(2,1)} %bitcast.63), calls=%async_computation.2 | async-start | bytes 2097152 | tf_op jit(solution)/shard_map/all_to_all | solution.py:33
  89.4 81.9 %copy-start.3 = (s32[16]{0:T(128)S(1)}, s32[16]{0:T(128)}, u32[]{:S(2)}) copy-start(s32[16]{0:T(128)} %param.11) | copy-start | bytes 196
  93.9 78.7 %copy-start.2 = (f32[128,8]{1,0:T(8,128)S(1)}, f32[128,8]{1,0:T(8,128)}, u32[]{:S(2)}) copy-start(f32[128,8]{1,0:T(8,128)} %select_reduce_fusion.2) | copy-start | bytes 12292
  169.9 16.9 %collective-permute-start = (bf16[192,1536]{1,0:T(8,128)(2,1)}, bf16[192,1536]{1,0:T(8,128)(2,1)}, u32[]{:S(2)}, u32[]{:S(2)}) collective-permute-start(bf16[192,1536]{1,0:T(8,128)(2,1)} %reduce-scatter.2.cloned.1.call-done), channel_id=1, source_target_pairs={{0,128},{128,0},{16,144},{144,16},{32,160},{160,32},{48,176},{176,... | collective-permute-start | bytes 1769480 | tf_op jit(solution)/shard_map/ppermute | solution.py:14
Sparse Core Ops, SparseCore 0:
  58.0 111.8 reduce-scatter.1

commit v12 on v11

--- a/solution.py
+++ b/solution.py
@@ -138,14 +138,19 @@
 
     mixed, x_grad, gate_grad, reduced = lax.optimization_barrier((mixed, x_grad, gate_grad, reduced))
     swapped = partner_2(reduced, "expert", half_bit)
-    reduced = jnp.where(is_moved, swapped, reduced)
-    grad_in = reduced[:in_rows]
-    tail = reduced[in_rows + out_rows :]
-    grad_out = jnp.concatenate(
-        [reduced[in_rows : in_rows + out_rows],
-         jnp.concatenate([tail[:, k * rest : (k + 1) * rest] for k in range(in_cols // rest)], axis=0)],
-        axis=1,
-    )
+
+    def unpack(block):
+        tail = block[in_rows + out_rows :]
+        bands_back = [tail[:, k * rest : (k + 1) * rest] for k in range(in_cols // rest)]
+        out_block = jnp.concatenate(
+            [block[in_rows : in_rows + out_rows], jnp.concatenate(bands_back, axis=0)], axis=1
+        )
+        return block[:in_rows], out_block
+
+    in_moved, out_moved = unpack(swapped)
+    in_kept, out_kept = unpack(reduced)
+    grad_in = jnp.where(is_moved, in_moved, in_kept)
+    grad_out = jnp.where(is_moved, out_moved, out_kept)
     return (mixed, x_grad, gate_grad, grad_in[None], grad_out[None])
 
 

time: 197 us -> 199 us (1.010)
  local copies, waits for them, and re-layouts: 4.45 us -> 7.01 us
  transfers between devices with their start and end apart: 4 -> 4, of which waited for: 4 -> 4; matrix products, arithmetic and copies ran while one was open for 10% -> 11% of each run, Pallas kernels for 0% -> 0%
where the time goes in v12:
time: 199 us; the launch traced here: 198 us
  waiting for transfers between devices  92.1 us (46%)
  blocking collectives  33.5 us (17%)
  matrix products  26.4 us (13%)
  between operations  14.9 us (7%)
  starting transfers between devices  14.6 us (7%)
  other arithmetic  9.52 us (5%)
  local copies, waits for them, and re-layouts  7.01 us (4%)
    reduce_scatter x1, waiting for transfers between devices, shards(): reduced = lax.psum_scatter(joined, 'dp', scatter_dimension=0, tiled=True)  60 us
    all_to_all x1, blocking collectives, exchange(): lax.all_to_all(shaped, ('expert', 'dp'), split_axis=0, concat_axis=0, til...  33.5 us
    all_to_all x2, waiting for transfers between devices, exchange(): lax.all_to_all(shaped, ('expert', 'dp'), split_axis=0, concat_axis=0, til...  18.9 us
    ppermute x1, waiting for transfers between devices, partner_2(): return lax.ppermute(block, axis, route)  13.2 us
    all_to_all x2, starting transfers between devices, exchange(): lax.all_to_all(shaped, ('expert', 'dp'), split_axis=0, concat_axis=0, til...  13.1 us
    dot_general x1, matrix products, shards(): jnp.einsum('sf,df->sd', gate_up_grad, weight_in, preferred_element_type=j...  6.27 us
  transfers between devices with their start and end apart: 4, of which 4 were waited for; matrix products, arithmetic and copies ran while one was open for 11% of the time, Pallas kernels for 0%

profile of v12, /device:TPU:24, one launch (start us, length us, event | category | flops | bytes accessed | tf_op | source)
XLA Modules:
  0.0 198.0 jit_solution(455255099613193438)
XLA Ops:
  7.2 0.9 copy.21
  8.2 0.8 copy.20
  10.5 1.6 convolution_convert_fusion
  12.2 1.5 fusion.9
  13.9 33.5 %all_to_all.15 = bf16[16,16,4096]{2,1,0:T(8,128)(2,1)S(1)} all-to-all(bf16[16,16,4096]{2,1,0:T(8,128)(2,1)S(1)} %bitcast.59), channel_id=1, replica_groups={{0,16,40,56,64,80,104,120,128,144,168,184,192,208,232,248},{1,17,41,57,..., dimensions={0} | all-to-all | bytes 4194304 | tf_op jit(solution)/shard_map/all_to_all | solution.py:33
  47.4 1.8 fusion.2
  49.2 1.3 multiply_convert_fusion.4
  50.9 0.8 multiply_convert_fusion.1
  52.0 1.8 multiply_convert_fusion
  53.9 4.0 %pad_maximum_fusion = bf16[16,192,1536]{2,1,0:T(8,128)(2,1)} fusion(bf16[16,16,1536]{2,1,0:T(8,128)(2,1)S(1)} %bitcast.62, bf16[16,48,1536]{2,1,0:T(8,128)(2,1)S(1)} %bitcast.68, bf16[16,128,1536]{2,1,0:T(8,128)(2,1)S(1)} %bitcast.61), kind=kLoop, calls=%fused_computation.1 | loop fusion | flops 28311552 | bytes 18874368 | tf_op jit(solution)/shard_map/concatenate | solution.py:121
  57.9 3.0 %fusion.13 = bf16[256,2048]{1,0:T(8,128)(2,1)} fusion(bf16[256,768]{1,0:T(8,128)(2,1)} %copy-done.1, bf16[1,768,2048]{2,1,0:T(8,128)(2,1)S(1)} %copy-done), kind=kOutput, calls=%fused_computation.17 | convolution fusion | flops 805830656 | bytes 4587520 | tf_op jit(solution)/shard_map/dot_general | solution.py:90
  60.8 6.5 %all-to-all-start.1 = ((bf16[16,16,2048]{2,1,0:T(8,128)(2,1)}), bf16[16,16,2048]{2,1,0:T(8,128)(2,1)}, u32[]{:S(2)}, u32[]{:S(2)}) async-start(bf16[16,16,2048]{2,1,0:T(8,128)(2,1)} %bitcast.70), calls=%async_computation.1 | async-start | bytes 2097152 | tf_op jit(solution)/shard_map/all_to_all | solution.py:33
  67.3 6.3 %fusion.10 = bf16[256,2048]{1,0:T(8,128)(2,1)} fusion(bf16[1,2048,1536]{2,1,0:T(8,128)(2,1)} %param.12, bf16[256,768]{1,0:T(8,128)(2,1)} %copy-done.5, bf16[256,768]{1,0:T(8,128)(2,1)} %copy-done.4), kind=kOutput, calls=%fused_computation.16 | convolution fusion | flops 1612709888 | bytes 8126464 | tf_op jit(solution)/shard_map/sf,df->sd/dot_general | solution.py:100
  73.6 9.2 %all-to-all-done.1 = bf16[16,16,2048]{2,1,0:T(8,128)(2,1)} async-done(((bf16[16,16,2048]{2,1,0:T(8,128)(2,1)}), bf16[16,16,2048]{2,1,0:T(8,128)(2,1)}, u32[]{:S(2)}, u32[]{:S(2)}) %all-to-all-start.1) | async-done | bytes 1048608 | tf_op jit(solution)/shard_map/all_to_all | solution.py:33
  82.8 6.6 %all-to-all-start.2 = ((bf16[16,16,2048]{2,1,0:T(8,128)(2,1)}), bf16[16,16,2048]{2,1,0:T(8,128)(2,1)}, u32[]{:S(2)}, u32[]{:S(2)}) async-start(bf16[16,16,2048]{2,1,0:T(8,128)(2,1)} %bitcast.69), calls=%async_computation.2 | async-start | bytes 2097152 | tf_op jit(solution)/shard_map/all_to_all | solution.py:33
  89.4 0.6 fusion.33
  90.7 2.5 %convolution_bitcast_fusion = f32[128,256]{0,1:T(8,128)} fusion(bf16[256,2048]{1,0:T(8,128)(2,1)} %bitcast.5, bf16[128,2048]{1,0:T(8,128)(2,1)} %param.8), kind=kOutput, calls=%fused_computation.24 | convolution fusion | flops 134217728 | bytes 1703936 | tf_op jit(solution)/shard_map/td,sd->ts/dot_general | solution.py:133
  93.2 1.0 copy.22
  94.2 1.0 select_reduce_fusion.2
  95.2 9.7 %all-to-all-done.2 = bf16[16,16,2048]{2,1,0:T(8,128)(2,1)} async-done(((bf16[16,16,2048]{2,1,0:T(8,128)(2,1)}), bf16[16,16,2048]{2,1,0:T(8,128)(2,1)}, u32[]{:S(2)}, u32[]{:S(2)}) %all-to-all-start.2) | async-done | bytes 1048608 | tf_op jit(solution)/shard_map/all_to_all | solution.py:33
  104.9 2.4 %convolution_convert_fusion.1 = bf16[128,2048]{1,0:T(8,128)(2,1)} fusion(bf16[128,256]{1,0:T(8,128)(2,1)S(1)} %fusion.27, bf16[256,2048]{1,0:T(8,128)(2,1)} %bitcast.7), kind=kOutput, calls=%fused_computation.18 | convolution fusion | flops 134479872 | bytes 1638400 | tf_op jit(solution)/shard_map/ts,sd->td/dot_general | solution.py:135
  107.3 2.6 %convolution_convert_fusion.2 = bf16[128,2048]{1,0:T(8,128)(2,1)} fusion(f32[128,256]{1,0:T(8,128)S(1)} %get-tuple-element.19, bf16[256,2048]{1,0:T(8,128)(2,1)} %bitcast.5), kind=kOutput, calls=%fused_computation.19 | convolution fusion | flops 805568512 | bytes 1703936 | tf_op jit(solution)/shard_map/dot_general | solution.py:127
  109.9 60.0 %reduce-scatter.2.cloned.1.call-done = bf16[192,1536]{1,0:T(8,128)(2,1)} async-done(((bf16[3072,1536]{1,0:T(8,128)(2,1)}), bf16[192,1536]{1,0:T(8,128)(2,1)}) %reduce-scatter.2.cloned.1.call-update) | async-done | bytes 589840 | tf_op jit(solution)/shard_map/reduce_scatter | solution.py:124
  169.9 1.4 collective-permute-start
  171.3 0.8 fusion.36
  172.1 0.7 copy.25
  172.7 0.9 slice_bitcast_fusion.1
  173.7 13.2 %collective-permute-done = bf16[192,1536]{1,0:T(8,128)(2,1)} collective-permute-done((bf16[192,1536]{1,0:T(8,128)(2,1)}, bf16[192,1536]{1,0:T(8,128)(2,1)}, u32[]{:S(2)}, u32[]{:S(2)}) %collective-permute-start) | collective-permute-done | bytes 589856 | tf_op jit(solution)/shard_map/ppermute | solution.py:14
  186.8 0.8 fusion.37
  187.6 0.9 slice_bitcast_fusion
  188.5 0.7 maximum_select_fusion
  189.2 1.9 fusion.28
  (33 shorter events, 2.5 us)
Async XLA Ops:
  7.2 42.0 %copy-start = (bf16[1,768,2048]{2,1,0:T(8,128)(2,1)S(1)}, bf16[1,768,2048]{2,1,0:T(8,128)(2,1)}, u32[]{:S(2)}) copy-start(bf16[1,768,2048]{2,1,0:T(8,128)(2,1)} %param.13) | copy-start | bytes 9437188
  7.2 162.7 %reduce-scatter.2.cloned.1.call-start = ((), (), s32[]{:S(2)}) async-start(), calls=%async_computation.4 | async-start | bytes 10027008 | tf_op jit(solution)/shard_map/reduce_scatter | solution.py:124
  10.5 36.9 %slice-start = ((s8[6291456]{0:T(1024)(128)(4,1)}), s8[4194304]{0:T(1024)(128)(4,1)S(1)}, s32[]{:S(2)}) async-start(s8[6291456]{0:T(1024)(128)(4,1)} %bitcast.71), calls=%async_computation.5 | async-start | bytes 8388608
  13.7 33.7 %slice-start.1 = ((s8[6291456]{0:T(1024)(128)(4,1)}), s8[2097152]{0:T(1024)(128)(4,1)S(1)}, s32[]{:S(2)}) async-start(s8[6291456]{0:T(1024)(128)(4,1)} %bitcast.71), calls=%async_computation.6 | async-start | bytes 4194304
  50.5 1.5 copy-start.1
  50.5 1.5 copy-start.4
  50.5 1.5 copy-start.5
  60.8 22.0 %all-to-all-start.1 = ((bf16[16,16,2048]{2,1,0:T(8,128)(2,1)}), bf16[16,16,2048]{2,1,0:T(8,128)(2,1)}, u32[]{:S(2)}, u32[]{:S(2)}) async-start(bf16[16,16,2048]{2,1,0:T(8,128)(2,1)} %bitcast.70), calls=%async_computation.1 | async-start | bytes 2097152 | tf_op jit(solution)/shard_map/all_to_all | solution.py:33
  67.3 22.1 %copy-start.3 = (s32[16]{0:T(128)S(1)}, s32[16]{0:T(128)}, u32[]{:S(2)}) copy-start(s32[16]{0:T(128)} %param.11) | copy-start | bytes 196
  82.8 22.1 %all-to-all-start.2 = ((bf16[16,16,2048]{2,1,0:T(8,128)(2,1)}), bf16[16,16,2048]{2,1,0:T(8,128)(2,1)}, u32[]{:S(2)}, u32[]{:S(2)}) async-start(bf16[16,16,2048]{2,1,0:T(8,128)(2,1)} %bitcast.69), calls=%async_computation.2 | async-start | bytes 2097152 | tf_op jit(solution)/shard_map/all_to_all | solution.py:33
  95.2 76.9 %copy-start.2 = (f32[128,8]{1,0:T(8,128)S(1)}, f32[128,8]{1,0:T(8,128)}, u32[]{:S(2)}) copy-start(f32[128,8]{1,0:T(8,128)} %select_reduce_fusion.2) | copy-start | bytes 12292
  169.9 16.9 %collective-permute-start = (bf16[192,1536]{1,0:T(8,128)(2,1)}, bf16[192,1536]{1,0:T(8,128)(2,1)}, u32[]{:S(2)}, u32[]{:S(2)}) collective-permute-start(bf16[192,1536]{1,0:T(8,128)(2,1)} %reduce-scatter.2.cloned.1.call-done), channel_id=1, source_target_pairs={{0,128},{128,0},{16,144},{144,16},{32,160},{160,32},{48,176},{176,... | collective-permute-start | bytes 1769480 | tf_op jit(solution)/shard_map/ppermute | solution.py:14
Sparse Core Ops, SparseCore 0:
  58.0 111.8 reduce-scatter.1

commit v13 on v11

--- a/solution.py
+++ b/solution.py
@@ -72,12 +72,13 @@
     weigh = jnp.sum(jnp.where(slot_hot, gate_weights[:, :, None], 0.0), axis=1)
     slot_gate = jnp.sum(weigh, axis=0)
 
-    send_x = jnp.einsum("ts,td->sd", select, tokens, preferred_element_type=jnp.float32).astype(
-        jnp.bfloat16
+    picked = jnp.einsum(
+        "ts,td->sd", select, jnp.concatenate([tokens, cotangent], axis=1),
+        preferred_element_type=jnp.float32,
     )
-    send_dy = jnp.einsum("ts,td->sd", select, cotangent, preferred_element_type=jnp.float32)
-    send_c = (send_dy * slot_gate[:, None]).astype(jnp.bfloat16)
-    arrived = exchange(jnp.concatenate([send_x, send_c], axis=1), expert_count, capacity)
+    column = jnp.arange(2 * model_width, dtype=jnp.int32)
+    factor = jnp.where(column[None, :] < model_width, 1.0, slot_gate[:, None])
+    arrived = exchange((picked * factor).astype(jnp.bfloat16), expert_count, capacity)
     rows_x = arrived[:, :model_width]
     rows_c = arrived[:, model_width:]
 

time: 197 us -> 196 us (level)
  no operation moved by 1% of the time
where the time goes in v13:
time: 196 us; the launch traced here: 195 us
  waiting for transfers between devices  93.8 us (48%)
  blocking collectives  33.5 us (17%)
  matrix products  25.3 us (13%)
  between operations  14.9 us (8%)
  starting transfers between devices  14.6 us (7%)
  other arithmetic  8.49 us (4%)
  local copies, waits for them, and re-layouts  4.44 us (2%)
    reduce_scatter x1, waiting for transfers between devices, shards(): reduced = lax.psum_scatter(joined, 'dp', scatter_dimension=0, tiled=True)  60 us
    all_to_all x1, blocking collectives, exchange(): lax.all_to_all(shaped, ('expert', 'dp'), split_axis=0, concat_axis=0, til...  33.5 us
    all_to_all x2, waiting for transfers between devices, exchange(): lax.all_to_all(shaped, ('expert', 'dp'), split_axis=0, concat_axis=0, til...  20.2 us
    ppermute x1, waiting for transfers between devices, partner_2(): return lax.ppermute(block, axis, route)  13.6 us
    all_to_all x2, starting transfers between devices, exchange(): lax.all_to_all(shaped, ('expert', 'dp'), split_axis=0, concat_axis=0, til...  13.1 us
    dot_general x1, matrix products, shards(): jnp.einsum('sf,df->sd', gate_up_grad, weight_in, preferred_element_type=j...  6.26 us
    concatenate x1, other arithmetic, shards(): jnp.concatenate([part_in, part_out, bands], axis=1)  3.96 us
  transfers between devices with their start and end apart: 4, of which 4 were waited for; matrix products, arithmetic and copies ran while one was open for 10% of the time, Pallas kernels for 0%

profile of v13, /device:TPU:24, one launch (start us, length us, event | category | flops | bytes accessed | tf_op | source)
XLA Modules:
  0.0 195.0 jit_solution(17923766996515738126)
XLA Ops:
  7.2 0.9 copy.21
  8.2 0.8 copy.20
  9.1 0.5 fusion.19
  9.7 0.4 fusion.30
  10.1 0.4 select_reduce_fusion
  10.5 2.1 %fusion.4 = bf16[256,4096]{1,0:T(8,128)(2,1)S(1)} fusion(bf16[128,256]{1,0:T(8,128)(2,1)S(1)} %fusion.30, f32[256]{0:T(256)S(1)} %get-tuple-element.18, pred[4096]{0:T(1024)(128)(4,1)S(1)} %iota_compare_fusion.13, bf16[128,2048]{1,0:T(8,128)(2,1)} %param.8, bf16[128,2048]{1,0:T(8,128)(2,1)} %param.7), kind=kOutput, calls=%fused_computation.7 | convolution fusion | flops 273678336 | bytes 3216384 | tf_op jit(solution)/shard_map/ts,td->sd/dot_general | solution.py:75
  12.6 33.5 %all_to_all.15 = bf16[16,16,4096]{2,1,0:T(8,128)(2,1)S(1)} all-to-all(bf16[16,16,4096]{2,1,0:T(8,128)(2,1)S(1)} %bitcast.59), channel_id=1, replica_groups={{0,16,40,56,64,80,104,120,128,144,168,184,192,208,232,248},{1,17,41,57,..., dimensions={0} | all-to-all | bytes 4194304 | tf_op jit(solution)/shard_map/all_to_all | solution.py:33
  46.1 1.8 fusion.2
  47.9 1.3 multiply_convert_fusion.4
  49.2 0.4 fusion.31
  49.6 0.8 multiply_convert_fusion.1
  50.7 1.8 multiply_convert_fusion
  52.6 4.0 %pad_maximum_fusion = bf16[16,192,1536]{2,1,0:T(8,128)(2,1)} fusion(bf16[16,16,1536]{2,1,0:T(8,128)(2,1)S(1)} %bitcast.52, bf16[16,48,1536]{2,1,0:T(8,128)(2,1)S(1)} %bitcast.58, bf16[16,128,1536]{2,1,0:T(8,128)(2,1)S(1)} %bitcast.51), kind=kLoop, calls=%fused_computation.1 | loop fusion | flops 28311552 | bytes 18874368 | tf_op jit(solution)/shard_map/concatenate | solution.py:122
  56.6 3.0 %fusion.13 = bf16[256,2048]{1,0:T(8,128)(2,1)} fusion(bf16[256,768]{1,0:T(8,128)(2,1)} %copy-done.1, bf16[1,768,2048]{2,1,0:T(8,128)(2,1)S(1)} %copy-done), kind=kOutput, calls=%fused_computation.16 | convolution fusion | flops 805830656 | bytes 4587520 | tf_op jit(solution)/shard_map/dot_general | solution.py:91
  59.5 6.5 %all-to-all-start.1 = ((bf16[16,16,2048]{2,1,0:T(8,128)(2,1)}), bf16[16,16,2048]{2,1,0:T(8,128)(2,1)}, u32[]{:S(2)}, u32[]{:S(2)}) async-start(bf16[16,16,2048]{2,1,0:T(8,128)(2,1)} %bitcast.61), calls=%async_computation.1 | async-start | bytes 2097152 | tf_op jit(solution)/shard_map/all_to_all | solution.py:33
  66.0 6.3 %fusion.10 = bf16[256,2048]{1,0:T(8,128)(2,1)} fusion(bf16[1,2048,1536]{2,1,0:T(8,128)(2,1)} %param.12, bf16[256,768]{1,0:T(8,128)(2,1)} %copy-done.6, bf16[256,768]{1,0:T(8,128)(2,1)} %copy-done.5), kind=kOutput, calls=%fused_computation.15 | convolution fusion | flops 1612709888 | bytes 8126464 | tf_op jit(solution)/shard_map/sf,df->sd/dot_general | solution.py:101
  72.3 9.2 %all-to-all-done.1 = bf16[16,16,2048]{2,1,0:T(8,128)(2,1)} async-done(((bf16[16,16,2048]{2,1,0:T(8,128)(2,1)}), bf16[16,16,2048]{2,1,0:T(8,128)(2,1)}, u32[]{:S(2)}, u32[]{:S(2)}) %all-to-all-start.1) | async-done | bytes 1048608 | tf_op jit(solution)/shard_map/all_to_all | solution.py:33
  81.5 6.6 %all-to-all-start.2 = ((bf16[16,16,2048]{2,1,0:T(8,128)(2,1)}), bf16[16,16,2048]{2,1,0:T(8,128)(2,1)}, u32[]{:S(2)}, u32[]{:S(2)}) async-start(bf16[16,16,2048]{2,1,0:T(8,128)(2,1)} %bitcast.60), calls=%async_computation.2 | async-start | bytes 2097152 | tf_op jit(solution)/shard_map/all_to_all | solution.py:33
  88.1 2.5 %convolution_bitcast_fusion = f32[128,256]{0,1:T(8,128)} fusion(bf16[256,2048]{1,0:T(8,128)(2,1)} %bitcast.5, bf16[128,2048]{1,0:T(8,128)(2,1)} %param.8), kind=kOutput, calls=%fused_computation.22 | convolution fusion | flops 134217728 | bytes 1703936 | tf_op jit(solution)/shard_map/td,sd->ts/dot_general | solution.py:134
  90.6 1.0 copy.22
  91.6 1.0 select_reduce_fusion.2
  92.6 11.0 %all-to-all-done.2 = bf16[16,16,2048]{2,1,0:T(8,128)(2,1)} async-done(((bf16[16,16,2048]{2,1,0:T(8,128)(2,1)}), bf16[16,16,2048]{2,1,0:T(8,128)(2,1)}, u32[]{:S(2)}, u32[]{:S(2)}) %all-to-all-start.2) | async-done | bytes 1048608 | tf_op jit(solution)/shard_map/all_to_all | solution.py:33
  103.6 2.3 %convolution_convert_fusion = bf16[128,2048]{1,0:T(8,128)(2,1)} fusion(bf16[128,256]{1,0:T(8,128)(2,1)S(1)} %fusion.30, bf16[256,2048]{1,0:T(8,128)(2,1)} %bitcast.7), kind=kOutput, calls=%fused_computation.17 | convolution fusion | flops 134479872 | bytes 1638400 | tf_op jit(solution)/shard_map/ts,sd->td/dot_general | solution.py:136
  106.0 2.6 %convolution_convert_fusion.1 = bf16[128,2048]{1,0:T(8,128)(2,1)} fusion(f32[128,256]{1,0:T(8,128)S(1)} %get-tuple-element.19, bf16[256,2048]{1,0:T(8,128)(2,1)} %bitcast.5), kind=kOutput, calls=%fused_computation.18 | convolution fusion | flops 805568512 | bytes 1703936 | tf_op jit(solution)/shard_map/dot_general | solution.py:128
  108.6 60.0 %reduce-scatter.2.cloned.1.call-done = bf16[192,1536]{1,0:T(8,128)(2,1)} async-done(((bf16[3072,1536]{1,0:T(8,128)(2,1)}), bf16[192,1536]{1,0:T(8,128)(2,1)}) %reduce-scatter.2.cloned.1.call-update) | async-done | bytes 589840 | tf_op jit(solution)/shard_map/reduce_scatter | solution.py:125
  168.6 1.4 collective-permute-start
  170.0 0.6 fusion.35
  171.3 0.7 copy.25
  172.0 13.6 %collective-permute-done = bf16[192,1536]{1,0:T(8,128)(2,1)} collective-permute-done((bf16[192,1536]{1,0:T(8,128)(2,1)}, bf16[192,1536]{1,0:T(8,128)(2,1)}, u32[]{:S(2)}, u32[]{:S(2)}) %collective-permute-start) | collective-permute-done | bytes 589856 | tf_op jit(solution)/shard_map/ppermute | solution.py:14
  185.5 1.1 broadcast_select_fusion
  186.7 0.8 slice_bitcast_fusion
  187.4 0.7 maximum_bitcast_fusion
  (26 shorter events, 0.6 us)
Async XLA Ops:
  7.2 40.7 %copy-start = (bf16[1,768,2048]{2,1,0:T(8,128)(2,1)S(1)}, bf16[1,768,2048]{2,1,0:T(8,128)(2,1)}, u32[]{:S(2)}) copy-start(bf16[1,768,2048]{2,1,0:T(8,128)(2,1)} %param.13) | copy-start | bytes 9437188
  7.2 161.4 %reduce-scatter.2.cloned.1.call-start = ((), (), s32[]{:S(2)}) async-start(), calls=%async_computation.4 | async-start | bytes 10027008 | tf_op jit(solution)/shard_map/reduce_scatter | solution.py:125
  10.5 35.6 %copy-start.3 = (bf16[1,2048,1536]{2,1,0:T(8,128)(2,1)S(1)}, bf16[1,2048,1536]{2,1,0:T(8,128)(2,1)}, u32[]{:S(2)}) copy-start(bf16[1,2048,1536]{2,1,0:T(8,128)(2,1)} %param.12) | copy-start | bytes 18874372
  49.2 1.5 copy-start.1
  49.2 1.5 copy-start.5
  49.2 1.5 copy-start.6
  59.5 22.0 %all-to-all-start.1 = ((bf16[16,16,2048]{2,1,0:T(8,128)(2,1)}), bf16[16,16,2048]{2,1,0:T(8,128)(2,1)}, u32[]{:S(2)}, u32[]{:S(2)}) async-start(bf16[16,16,2048]{2,1,0:T(8,128)(2,1)} %bitcast.61), calls=%async_computation.1 | async-start | bytes 2097152 | tf_op jit(solution)/shard_map/all_to_all | solution.py:33
  81.5 22.1 %all-to-all-start.2 = ((bf16[16,16,2048]{2,1,0:T(8,128)(2,1)}), bf16[16,16,2048]{2,1,0:T(8,128)(2,1)}, u32[]{:S(2)}, u32[]{:S(2)}) async-start(bf16[16,16,2048]{2,1,0:T(8,128)(2,1)} %bitcast.60), calls=%async_computation.2 | async-start | bytes 2097152 | tf_op jit(solution)/shard_map/all_to_all | solution.py:33
  88.1 81.9 %copy-start.4 = (s32[16]{0:T(128)S(1)}, s32[16]{0:T(128)}, u32[]{:S(2)}) copy-start(s32[16]{0:T(128)} %param.11) | copy-start | bytes 196
  92.6 78.7 %copy-start.2 = (f32[128,8]{1,0:T(8,128)S(1)}, f32[128,8]{1,0:T(8,128)}, u32[]{:S(2)}) copy-start(f32[128,8]{1,0:T(8,128)} %select_reduce_fusion.2) | copy-start | bytes 12292
  168.6 16.9 %collective-permute-start = (bf16[192,1536]{1,0:T(8,128)(2,1)}, bf16[192,1536]{1,0:T(8,128)(2,1)}, u32[]{:S(2)}, u32[]{:S(2)}) collective-permute-start(bf16[192,1536]{1,0:T(8,128)(2,1)} %reduce-scatter.2.cloned.1.call-done), channel_id=1, source_target_pairs={{0,128},{128,0},{16,144},{144,16},{32,160},{160,32},{48,176},{176,... | collective-permute-start | bytes 1769480 | tf_op jit(solution)/shard_map/ppermute | solution.py:14
Sparse Core Ops, SparseCore 0:
  56.7 111.8 reduce-scatter.1

commit v14 on v13

--- a/solution.py
+++ b/solution.py
@@ -137,7 +137,6 @@
         jnp.bfloat16
     )
 
-    mixed, x_grad, gate_grad, reduced = lax.optimization_barrier((mixed, x_grad, gate_grad, reduced))
     swapped = partner_2(reduced, "expert", half_bit)
     reduced = jnp.where(is_moved, swapped, reduced)
     grad_in = reduced[:in_rows]

time: 196 us -> 196 us (level)
    reduce_scatter x1, waiting for transfers between devices: 60 us -> 75.7 us  [shards(): reduced = lax.psum_scatter(joined, 'dp', scatter_dimension=0, tiled=True)]
    all_to_all x2, waiting for transfers between devices: 20.2 us -> 9.22 us  [exchange(): lax.all_to_all(shaped, ('expert', 'dp'), split_axis=0, concat_axis=0, til...]
    ppermute x1, waiting for transfers between devices: 13.6 us -> 8 us  [partner_2(): return lax.ppermute(block, axis, route)]
  transfers between devices with their start and end apart: 4 -> 4, of which waited for: 4 -> 3; matrix products, arithmetic and copies ran while one was open for 10% -> 11% of each run, Pallas kernels for 0% -> 0%
where the time goes in v14:
time: 196 us; the launch traced here: 195 us
  waiting for transfers between devices  92.9 us (47%)
  blocking collectives  33.5 us (17%)
  matrix products  25.4 us (13%)
  between operations  14.9 us (8%)
  starting transfers between devices  14.6 us (7%)
  other arithmetic  8.49 us (4%)
  local copies, waits for them, and re-layouts  5.28 us (3%)
    reduce_scatter x1, waiting for transfers between devices, shards(): reduced = lax.psum_scatter(joined, 'dp', scatter_dimension=0, tiled=True)  75.7 us
    all_to_all x1, blocking collectives, exchange(): lax.all_to_all(shaped, ('expert', 'dp'), split_axis=0, concat_axis=0, til...  33.5 us
    all_to_all x2, starting transfers between devices, exchange(): lax.all_to_all(shaped, ('expert', 'dp'), split_axis=0, concat_axis=0, til...  13.1 us
    all_to_all x2, waiting for transfers between devices, exchange(): lax.all_to_all(shaped, ('expert', 'dp'), split_axis=0, concat_axis=0, til...  9.22 us
    ppermute x1, waiting for transfers between devices, partner_2(): return lax.ppermute(block, axis, route)  8 us
    dot_general x1, matrix products, shards(): jnp.einsum('sf,df->sd', gate_up_grad, weight_in, preferred_element_type=j...  6.27 us
    concatenate x1, other arithmetic, shards(): jnp.concatenate([part_in, part_out, bands], axis=1)  3.96 us
  transfers between devices with their start and end apart: 4, of which 3 were waited for; matrix products, arithmetic and copies ran while one was open for 11% of the time, Pallas kernels for 0%

profile of v14, /device:TPU:24, one launch (start us, length us, event | category | flops | bytes accessed | tf_op | source)
XLA Modules:
  0.0 195.0 jit_solution(4219645203937899962)
XLA Ops:
  7.2 0.9 copy.21
  8.2 0.8 copy.20
  9.1 0.5 fusion.19
  9.7 0.4 fusion.30
  10.1 0.4 select_reduce_fusion
  10.5 2.1 %fusion.4 = bf16[256,4096]{1,0:T(8,128)(2,1)S(1)} fusion(bf16[128,256]{1,0:T(8,128)(2,1)S(1)} %fusion.30, f32[256]{0:T(256)S(1)} %get-tuple-element.10, pred[4096]{0:T(1024)(128)(4,1)S(1)} %iota_compare_fusion.13, bf16[128,2048]{1,0:T(8,128)(2,1)} %param.8, bf16[128,2048]{1,0:T(8,128)(2,1)} %param.7), kind=kOutput, calls=%fused_computation.7 | convolution fusion | flops 273678336 | bytes 3216384 | tf_op jit(solution)/shard_map/ts,td->sd/dot_general | solution.py:75
  12.6 33.5 %all_to_all.15 = bf16[16,16,4096]{2,1,0:T(8,128)(2,1)S(1)} all-to-all(bf16[16,16,4096]{2,1,0:T(8,128)(2,1)S(1)} %bitcast.59), channel_id=1, replica_groups={{0,16,40,56,64,80,104,120,128,144,168,184,192,208,232,248},{1,17,41,57,..., dimensions={0} | all-to-all | bytes 4194304 | tf_op jit(solution)/shard_map/all_to_all | solution.py:33
  46.1 1.8 fusion.2
  47.9 1.3 multiply_convert_fusion.4
  49.2 0.4 fusion.31
  49.6 0.8 multiply_convert_fusion.1
  50.4 0.2 fusion.27
  50.7 1.8 multiply_convert_fusion
  52.6 4.0 %pad_maximum_fusion = bf16[16,192,1536]{2,1,0:T(8,128)(2,1)} fusion(bf16[16,16,1536]{2,1,0:T(8,128)(2,1)S(1)} %bitcast.52, bf16[16,48,1536]{2,1,0:T(8,128)(2,1)S(1)} %bitcast.58, bf16[16,128,1536]{2,1,0:T(8,128)(2,1)S(1)} %bitcast.51), kind=kLoop, calls=%fused_computation.1 | loop fusion | flops 28311552 | bytes 18874368 | tf_op jit(solution)/shard_map/concatenate | solution.py:122
  56.6 3.0 %fusion.13 = bf16[256,2048]{1,0:T(8,128)(2,1)} fusion(bf16[256,768]{1,0:T(8,128)(2,1)} %copy-done.2, bf16[1,768,2048]{2,1,0:T(8,128)(2,1)S(1)} %copy-done), kind=kOutput, calls=%fused_computation.16 | convolution fusion | flops 805830656 | bytes 4587520 | tf_op jit(solution)/shard_map/dot_general | solution.py:91
  59.5 6.5 %all-to-all-start.1 = ((bf16[16,16,2048]{2,1,0:T(8,128)(2,1)}), bf16[16,16,2048]{2,1,0:T(8,128)(2,1)}, u32[]{:S(2)}, u32[]{:S(2)}) async-start(bf16[16,16,2048]{2,1,0:T(8,128)(2,1)} %bitcast.61), calls=%async_computation.1 | async-start | bytes 2097152 | tf_op jit(solution)/shard_map/all_to_all | solution.py:33
  66.0 6.3 %fusion.10 = bf16[256,2048]{1,0:T(8,128)(2,1)} fusion(bf16[1,2048,1536]{2,1,0:T(8,128)(2,1)} %param.12, bf16[256,768]{1,0:T(8,128)(2,1)} %copy-done.6, bf16[256,768]{1,0:T(8,128)(2,1)} %copy-done.5), kind=kOutput, calls=%fused_computation.15 | convolution fusion | flops 1612709888 | bytes 8126464 | tf_op jit(solution)/shard_map/sf,df->sd/dot_general | solution.py:101
  72.3 9.2 %all-to-all-done.1 = bf16[16,16,2048]{2,1,0:T(8,128)(2,1)} async-done(((bf16[16,16,2048]{2,1,0:T(8,128)(2,1)}), bf16[16,16,2048]{2,1,0:T(8,128)(2,1)}, u32[]{:S(2)}, u32[]{:S(2)}) %all-to-all-start.1) | async-done | bytes 1048608 | tf_op jit(solution)/shard_map/all_to_all | solution.py:33
  81.5 6.6 %all-to-all-start.2 = ((bf16[16,16,2048]{2,1,0:T(8,128)(2,1)}), bf16[16,16,2048]{2,1,0:T(8,128)(2,1)}, u32[]{:S(2)}, u32[]{:S(2)}) async-start(bf16[16,16,2048]{2,1,0:T(8,128)(2,1)} %bitcast.60), calls=%async_computation.2 | async-start | bytes 2097152 | tf_op jit(solution)/shard_map/all_to_all | solution.py:33
  88.1 0.6 fusion.35
  89.4 2.5 %convolution_bitcast_fusion = f32[128,256]{0,1:T(8,128)} fusion(bf16[256,2048]{1,0:T(8,128)(2,1)} %bitcast.5, bf16[128,2048]{1,0:T(8,128)(2,1)} %param.8), kind=kOutput, calls=%fused_computation.22 | convolution fusion | flops 134217728 | bytes 1703936 | tf_op jit(solution)/shard_map/td,sd->ts/dot_general | solution.py:134
  91.9 1.0 copy.22
  92.9 75.7 %reduce-scatter.2.cloned.1.call-done = bf16[192,1536]{1,0:T(8,128)(2,1)} async-done(((bf16[3072,1536]{1,0:T(8,128)(2,1)}), bf16[192,1536]{1,0:T(8,128)(2,1)}) %reduce-scatter.2.cloned.1.call-update) | async-done | bytes 589840 | tf_op jit(solution)/shard_map/reduce_scatter | solution.py:125
  168.6 1.4 collective-permute-start
  170.0 1.0 select_reduce_fusion.2
  171.0 1.5 copy.25
  172.5 2.4 %convolution_convert_fusion = bf16[128,2048]{1,0:T(8,128)(2,1)} fusion(bf16[128,256]{1,0:T(8,128)(2,1)S(1)} %fusion.30, bf16[256,2048]{1,0:T(8,128)(2,1)} %bitcast.7), kind=kOutput, calls=%fused_computation.17 | convolution fusion | flops 134479872 | bytes 1638400 | tf_op jit(solution)/shard_map/ts,sd->td/dot_general | solution.py:136
  174.9 2.6 %convolution_convert_fusion.1 = bf16[128,2048]{1,0:T(8,128)(2,1)} fusion(f32[128,256]{1,0:T(8,128)S(1)} %get-tuple-element.11, bf16[256,2048]{1,0:T(8,128)(2,1)} %bitcast.5), kind=kOutput, calls=%fused_computation.18 | convolution fusion | flops 805568512 | bytes 1703936 | tf_op jit(solution)/shard_map/dot_general | solution.py:128
  177.5 8.0 %collective-permute-done = bf16[192,1536]{1,0:T(8,128)(2,1)} collective-permute-done((bf16[192,1536]{1,0:T(8,128)(2,1)}, bf16[192,1536]{1,0:T(8,128)(2,1)}, u32[]{:S(2)}, u32[]{:S(2)}) %collective-permute-start) | collective-permute-done | bytes 589856 | tf_op jit(solution)/shard_map/ppermute | solution.py:14
  185.5 1.1 broadcast_select_fusion
  186.7 0.8 slice_bitcast_fusion
  187.5 0.7 maximum_bitcast_fusion
  (26 shorter events, 0.4 us)
Async XLA Ops:
  7.2 40.7 %copy-start = (bf16[1,768,2048]{2,1,0:T(8,128)(2,1)S(1)}, bf16[1,768,2048]{2,1,0:T(8,128)(2,1)}, u32[]{:S(2)}) copy-start(bf16[1,768,2048]{2,1,0:T(8,128)(2,1)} %param.13) | copy-start | bytes 9437188
  7.2 161.4 %reduce-scatter.2.cloned.1.call-start = ((), (), s32[]{:S(2)}) async-start(), calls=%async_computation.4 | async-start | bytes 10027008 | tf_op jit(solution)/shard_map/reduce_scatter | solution.py:125
  10.5 35.6 %copy-start.3 = (bf16[1,2048,1536]{2,1,0:T(8,128)(2,1)S(1)}, bf16[1,2048,1536]{2,1,0:T(8,128)(2,1)}, u32[]{:S(2)}) copy-start(bf16[1,2048,1536]{2,1,0:T(8,128)(2,1)} %param.12) | copy-start | bytes 18874372
  49.2 1.5 copy-start.2
  49.2 1.5 copy-start.5
  49.2 1.5 copy-start.6
  59.5 22.0 %all-to-all-start.1 = ((bf16[16,16,2048]{2,1,0:T(8,128)(2,1)}), bf16[16,16,2048]{2,1,0:T(8,128)(2,1)}, u32[]{:S(2)}, u32[]{:S(2)}) async-start(bf16[16,16,2048]{2,1,0:T(8,128)(2,1)} %bitcast.61), calls=%async_computation.1 | async-start | bytes 2097152 | tf_op jit(solution)/shard_map/all_to_all | solution.py:33
  66.0 22.1 %copy-start.4 = (s32[16]{0:T(128)S(1)}, s32[16]{0:T(128)}, u32[]{:S(2)}) copy-start(s32[16]{0:T(128)} %param.11) | copy-start | bytes 196
  81.5 91.0 %all-to-all-start.2 = ((bf16[16,16,2048]{2,1,0:T(8,128)(2,1)}), bf16[16,16,2048]{2,1,0:T(8,128)(2,1)}, u32[]{:S(2)}, u32[]{:S(2)}) async-start(bf16[16,16,2048]{2,1,0:T(8,128)(2,1)} %bitcast.60), calls=%async_computation.2 | async-start | bytes 2097152 | tf_op jit(solution)/shard_map/all_to_all | solution.py:33
  168.6 16.9 %collective-permute-start = (bf16[192,1536]{1,0:T(8,128)(2,1)}, bf16[192,1536]{1,0:T(8,128)(2,1)}, u32[]{:S(2)}, u32[]{:S(2)}) collective-permute-start(bf16[192,1536]{1,0:T(8,128)(2,1)} %reduce-scatter.2.cloned.1.call-done), channel_id=1, source_target_pairs={{0,128},{128,0},{16,144},{144,16},{32,160},{160,32},{48,176},{176,... | collective-permute-start | bytes 1769480 | tf_op jit(solution)/shard_map/ppermute | solution.py:14
  172.5 13.0 %copy-start.1 = (bf16[192,1536]{1,0:T(8,128)(2,1)S(1)}, bf16[192,1536]{1,0:T(8,128)(2,1)}, u32[]{:S(2)}) copy-start(bf16[192,1536]{1,0:T(8,128)(2,1)} %reduce-scatter.2.cloned.1.call-done) | copy-start | bytes 1769476
Sparse Core Ops, SparseCore 0:
  56.7 111.8 reduce-scatter.1
